TPU v7x, 512 devices: a whole 4x8x8 slice. The times are simulated.
512 devices in a mesh: req: 64 (over x, y, core), head: 8 (over z).
Axes of the slice: x: 4, y: 8, z: 8, core: 2. Of those that a mesh axis runs over, the one named last changes fastest.
Arguments:
- queries: bfloat16 [2, 64, 128, 576], P(None, 'req', 'head'), may hold values from -100 to 100
- prompt_cache: bfloat16 [32768, 576], P('req'), may hold values from -10 to 10
- suffix_cache: bfloat16 [64, 8, 64, 576], P('req'), may hold values from -14 to 14
- new_latent: bfloat16 [2, 64, 576], P(None, 'req'), may hold values from -16 to 16
- suffix_len: int32 [64], P('req'), may hold values from 1 to 512, 16640 in all
- parent: int32 [64], P('req'), may hold values from 0 to 63
- fork_pages: int32 [64, 2], P('req'), may hold values from 0 to 7
Outputs:
- attended: bfloat16 [2, 64, 128, 512], P(None, 'req', 'head')
Inputs may be any that keep to these rules, and one draw needn't show every extreme that they name: `suffix_len`: every beam has at least one valid own token.
All inputs are finite; a program needn't handle non-finite values. No bound on the sum of `suffix_len` on one device may be relied on, other than what follows from the above.
Results may differ from a plain program's by a relative error of at most 0.008.
Values may be sent and summed in bfloat16 or wider, within the bound.
No kernel may reach another device: no remote copies, remote signals or barrier semaphores. Data moves between devices by JAX's collectives and lax.ppermute only.
A program may use at most 64 MiB of HBM per device.

v0:
```python
import math

import jax
import jax.numpy as jnp
from jax import lax
from jax.sharding import PartitionSpec as P

DL = 512


score_scale = 192.0 ** (-0.5)
neg_large = -1e30


def prompt_block(rows, keys):
    scores = (
        lax.dot_general(rows, keys, (((1,), (1,)), ((), ())), preferred_element_type=jnp.float32)
        * score_scale
    )
    top = jnp.max(scores, axis=-1)
    weights = jnp.exp(scores - top[:, None])
    total = jnp.sum(weights, axis=-1)
    summed = jnp.dot(weights.astype(jnp.bfloat16), keys[:, :DL], preferred_element_type=jnp.float32)
    return (top, total, (summed / total[:, None]).astype(jnp.bfloat16))


def masked_partial(queries, keys, valid):
    scores = (
        jnp.einsum("sbhk,btk->sbht", queries, keys, preferred_element_type=jnp.float32)
        * score_scale
    )
    scores = jnp.where(valid, scores, neg_large)
    top = jnp.max(scores, axis=-1)
    weights = jnp.where(valid, jnp.exp(scores - top[..., None]), 0.0)
    total = jnp.sum(weights, axis=-1)
    summed = jnp.einsum(
        "sbht,btd->sbhd",
        weights.astype(jnp.bfloat16),
        keys[..., :DL],
        preferred_element_type=jnp.float32,
    )
    return (top, total, summed)


def finish_fork(total, summed):
    return (summed / jnp.maximum(total, 1.0)[..., None]).astype(jnp.bfloat16)


def combine_parts(top_pr, total_pr, out_pr, top_fr, total_fr, out_fr, top_l, total_l, summed_l):
    peak = jnp.maximum(jnp.maximum(jnp.max(top_pr, axis=1), jnp.max(top_fr, axis=1)), top_l)
    weight_p = total_pr * jnp.exp(top_pr - peak[:, None])
    weight_f = total_fr * jnp.exp(top_fr - peak[:, None])
    weight_l = jnp.exp(top_l - peak)
    denom = jnp.sum(weight_p, axis=1) + jnp.sum(weight_f, axis=1) + total_l * weight_l
    numer = (
        jnp.sum(weight_p[..., None] * out_pr, axis=1)
        + jnp.sum(weight_f[..., None] * out_fr, axis=1)
        + weight_l[..., None] * summed_l
    )
    return numer / denom[..., None]


def on_device(queries, prompt_cache, suffix_cache, new_latent, suffix_len, parent, fork_pages):
    steps_n, beam_dev, head_dev, width = queries.shape
    pages_n, page_len = (suffix_cache.shape[1], suffix_cache.shape[2])
    forks_n = fork_pages.shape[1]
    req_n = lax.axis_size("req")
    first_beam = lax.axis_index("req") * beam_dev
    every_query = lax.all_gather(queries, "req", axis=1, tiled=True)
    all_parent, all_pages, all_len = (
        lax.all_gather(parent, "req", axis=0, tiled=True),
        lax.all_gather(fork_pages, "req", axis=0, tiled=True),
        lax.all_gather(suffix_len, "req", axis=0, tiled=True),
    )
    beams_n = every_query.shape[1]
    rows_n = steps_n * beams_n * head_dev
    block = math.gcd(rows_n, 512)
    blocks = every_query.reshape(rows_n // block, block, width)
    top_p, total_p, out_p = lax.map(lambda rows: prompt_block(rows, prompt_cache), blocks)
    top_p = top_p.reshape(steps_n, beams_n, head_dev)
    total_p = total_p.reshape(steps_n, beams_n, head_dev)
    out_p = out_p.reshape(steps_n, beams_n, head_dev, DL)
    local_parent = all_parent - first_beam
    owned = (local_parent >= 0) & (local_parent < beam_dev)
    source_beam = jnp.clip(local_parent, 0, beam_dev - 1)
    picked = suffix_cache[source_beam[:, None], all_pages]
    offsets = jnp.arange(page_len, dtype=jnp.int32)
    own_keys = jnp.concatenate(
        [suffix_cache.reshape(beam_dev, pages_n * page_len, width), jnp.swapaxes(new_latent, 0, 1)],
        axis=1,
    )
    old_valid = jnp.arange(pages_n * page_len, dtype=jnp.int32)[None, :] < suffix_len[:, None]
    new_valid = (
        jnp.arange(steps_n, dtype=jnp.int32)[None, :]
        <= jnp.arange(steps_n, dtype=jnp.int32)[:, None]
    )
    own_valid = jnp.concatenate(
        [
            jnp.broadcast_to(old_valid[None], (steps_n, beam_dev, pages_n * page_len)),
            new_valid[:, None, :],
        ],
        axis=2,
    )[:, :, None, :]
    top_l, total_l, summed_l = masked_partial(queries, own_keys, own_valid)
    outgoing = jnp.where(owned[:, None, None, None], picked, jnp.zeros_like(picked))
    arrived = lax.all_to_all(outgoing, "req", split_axis=0, concat_axis=0, tiled=True)
    tiles = jnp.sum(arrived.reshape(req_n, beam_dev, forks_n, page_len, width), axis=0)
    tiles = tiles.reshape(beam_dev, forks_n * page_len, width)
    positions = (fork_pages[:, :, None] * page_len + offsets[None, None, :]).reshape(beam_dev, -1)
    fork_valid = (positions < all_len[parent][:, None])[None, :, None, :]
    top_f, total_f, summed_f = masked_partial(queries, tiles, fork_valid)
    out_f = finish_fork(total_f, summed_f).astype(jnp.float32)
    out_pr, top_pr, total_pr = (
        lax.all_to_all(
            out_p.astype(jnp.float32), "req", split_axis=1, concat_axis=1, tiled=True
        ).astype(out_p.dtype),
        lax.all_to_all(top_p, "req", split_axis=1, concat_axis=1, tiled=True),
        lax.all_to_all(total_p, "req", split_axis=1, concat_axis=1, tiled=True),
    )
    top_pr = top_pr.reshape(steps_n, req_n, beam_dev, head_dev)
    total_pr = total_pr.reshape(steps_n, req_n, beam_dev, head_dev)
    out_pr = out_pr.astype(jnp.float32).reshape(steps_n, req_n, beam_dev, head_dev, DL)
    result = combine_parts(
        top_pr,
        total_pr,
        out_pr,
        top_f[:, None],
        total_f[:, None],
        out_f[:, None],
        top_l,
        total_l,
        summed_l,
    )
    return result.astype(jnp.bfloat16)


def solution(mesh):
    placed = (
        P(None, "req", "head", None),
        P("req", None),
        P("req", None, None, None),
        P(None, "req", None),
        P("req"),
        P("req"),
        P("req", None),
    )
    return jax.shard_map(
        on_device,
        mesh=mesh,
        in_specs=placed,
        out_specs=P(None, "req", "head", None),
        check_vma=False,
    )
```

profile of v0, /device:TPU:448, one launch (start us, length us, event | category | flops | bytes accessed | tf_op | source)
XLA Modules:
  0.0 447.8 jit_solution(4871701999400987592)
XLA Ops:
  6.5 0.7 all-gather.3.cloned.1.call-update
  8.6 36.6 %all-gather = s32[64,1,2]{2,1,0:T(1,128)S(1)} all-gather(s32[1,1,2]{2,1,0:T(1,128)} %bitcast.151), channel_id=1, replica_groups=mesh['req'=64,'head'=8] {'req'}, dimensions={0}, use_global_device_ids=true | all-gather | bytes 520 | tf_op jit(solution)/shard_map/all_gather | solution.py:72
  45.3 1.3 dynamic-slice.3
  46.6 0.7 dynamic-update-slice.2
  47.3 0.7 dynamic-update-slice.1
  48.1 19.3 %all-reduce.2 = (s32[64]{0:T(128)S(1)}, s32[64]{0:T(128)S(1)}) all-reduce(s32[64]{0:T(128)S(1)} %dynamic-update-slice.2, s32[64]{0:T(128)S(1)} %dynamic-update-slice.1), channel_id=1, replica_groups=mesh['req'=64,'head'=8] {'req'}, use_global_device_ids=true, to_apply=%add.1 | all-reduce | flops 128 | bytes 1024
  67.4 25.8 %all-gather.3.cloned.1.call-done = bf16[2,64,16,576]{3,2,1,0:T(8,128)(2,1)} async-done(((bf16[2,1,16,576]{3,2,1,0:T(8,128)(2,1)}), bf16[2,64,16,576]{3,2,1,0:T(8,128)(2,1)}) %all-gather.3.cloned.1.call-update) | async-done | bytes 2359312 | tf_op jit(solution)/shard_map/all_gather | solution.py:69
  93.2 11.2 %while.15 = (s32[]{:T(128)}, f32[4,512]{1,0:T(4,128)S(1)}, f32[4,512]{1,0:T(4,128)S(1)}, bf16[4,512,512]{2,1,0:T(8,128)(2,1)S(1)}, bf16[4,512,576]{2,1,0:T(8,128...) while((s32[]{:T(128)}, f32[4,512]{1,0:T(4,128)S(1)}, f32[4,512]{1,0:T(4,128)S(1)}, ...), condition=%wide.region_3.4_spmd, body=%wide.region_0.3_spmd.sunk | while | flops 572521472 | bytes 7817853 | solution.py:79
  93.2 2.0 fusion.73
  96.1 2.0 fusion.73
  98.9 2.0 fusion.73
  101.7 2.0 fusion.73
  105.2 6.7 %all-to-all-start.1 = ((f32[2,64,16]{2,0,1:T(2,128)}), f32[2,64,16]{2,0,1:T(2,128)S(1)}, u32[]{:S(2)}, u32[]{:S(2)}) async-start(f32[2,64,16]{2,0,1:T(2,128)} %copy.23), calls=%async_computation.1 | async-start | bytes 131072 | tf_op jit(solution)/shard_map/all_to_all | solution.py:117
  112.2 7.8 %gather_fusion = bf16[128,64,576]{2,1,0:T(8,128)(2,1)} fusion(bf16[1,8,64,576]{3,2,1,0:T(8,128)(2,1)S(1)} %copy-done, s32[128]{0:T(128)S(1)} %reshape.321), kind=kCustom, calls=%fused_computation | custom fusion | bytes 18875392 | tf_op jit(solution)/shard_map/gather | solution.py:86
  120.8 0.9 all-to-all-done.1
  121.7 9.5 %all-to-all-start = ((f32[2,64,16]{2,0,1:T(2,128)}), f32[2,64,16]{2,0,1:T(2,128)S(1)}, u32[]{:S(2)}, u32[]{:S(2)}) async-start(f32[2,64,16]{2,0,1:T(2,128)} %copy.22), calls=%async_computation | async-start | bytes 131072 | tf_op jit(solution)/shard_map/all_to_all | solution.py:118
  131.2 10.0 %broadcast_select_fusion = bf16[64,2,64,576]{3,2,1,0:T(8,128)(2,1)} fusion(bf16[64,2,64,576]{3,2,1,0:T(8,128)(2,1)} %bitcast.144, pred[64]{0:T(512)(128)(4,1)S(1)} %compare_and_fusion), kind=kLoop, calls=%fused_computation.14 | loop fusion | flops 4718592 | bytes 18874432 | tf_op jit(solution)/shard_map/jit(_where)/select_n | solution.py:105
  141.2 10.6 %all-to-all-start.2 = ((bf16[64,2,64,576]{3,2,1,0:T(8,128)(2,1)}), bf16[64,2,64,576]{3,2,1,0:T(8,128)(2,1)}, u32[]{:S(2)}, u32[]{:S(2)}) async-start(bf16[64,2,64,576]{3,2,1,0:T(8,128)(2,1)} %broadcast_select_fusion), calls=%async_computation.2 | async-start | bytes 20971520 | tf_op jit(solution)/shard_map/all_to_all | solution.py:106
  151.7 1.5 copy.27
  153.2 228.0 %all-to-all-done.2 = bf16[64,2,64,576]{3,2,1,0:T(8,128)(2,1)} async-done(((bf16[64,2,64,576]{3,2,1,0:T(8,128)(2,1)}), bf16[64,2,64,576]{3,2,1,0:T(8,128)(2,1)}, u32[]{:S(2)}, u32[]{:S(2)}) %all-to-all-start.2) | async-done | bytes 9437216 | tf_op jit(solution)/shard_map/all_to_all | solution.py:106
  381.3 7.1 %all-to-all-start.3 = ((bf16[2,64,16,512]{3,2,0,1:T(8,128)(2,1)}), bf16[2,64,16,512]{3,2,0,1:T(8,128)(2,1)S(1)}, u32[]{:S(2)}, u32[]{:S(2)}) async-start(bf16[2,64,16,512]{3,2,0,1:T(8,128)(2,1)} %copy.27), calls=%async_computation.3 | async-start | bytes 4194304 | tf_op jit(solution)/shard_map/all_to_all | solution.py:114
  390.7 5.8 %reduce_sum.67 = bf16[2,64,576]{2,1,0:T(8,128)(2,1)S(1)} reduce(bf16[64,2,64,576]{3,2,1,0:T(8,128)(2,1)} %all-to-all-done.2, bf16[]{:T(256)} %constant.15.clone.1), dimensions={0}, to_apply=%region_5.6 | reduce | flops 4644864 | bytes 9584642 | tf_op jit(solution)/shard_map/reduce_sum | solution.py:107
  397.1 42.2 %all-to-all-done.3 = bf16[2,64,16,512]{3,2,0,1:T(8,128)(2,1)S(1)} async-done(((bf16[2,64,16,512]{3,2,0,1:T(8,128)(2,1)}), bf16[2,64,16,512]{3,2,0,1:T(8,128)(2,1)S(1)}, u32[]{:S(2)}, u32[]{:S(2)}) %all-to-all-start.3) | async-done | bytes 2097184 | tf_op jit(solution)/shard_map/all_to_all | solution.py:114
  440.0 0.9 fusion.18
  (70 shorter events, 8.6 us)
Async XLA Ops:
  6.5 86.7 %all-gather.3.cloned.1.call-start = ((), (), s32[]{:S(2)}) async-start(), calls=%async_computation.4 | async-start | bytes 2662400 | tf_op jit(solution)/shard_map/all_gather | solution.py:69
  93.2 19.0 %copy-start = (bf16[1,8,64,576]{3,2,1,0:T(8,128)(2,1)S(1)}, bf16[1,8,64,576]{3,2,1,0:T(8,128)(2,1)}, u32[]{:S(2)}) copy-start(bf16[1,8,64,576]{3,2,1,0:T(8,128)(2,1)} %param.11) | copy-start | bytes 1769476
  93.2 2.2 copy-start.1
  96.1 2.2 copy-start.1
  98.9 2.2 copy-start.1
  101.7 2.2 copy-start.1
  105.2 16.5 %all-to-all-start.1 = ((f32[2,64,16]{2,0,1:T(2,128)}), f32[2,64,16]{2,0,1:T(2,128)S(1)}, u32[]{:S(2)}, u32[]{:S(2)}) async-start(f32[2,64,16]{2,0,1:T(2,128)} %copy.23), calls=%async_computation.1 | async-start | bytes 131072 | tf_op jit(solution)/shard_map/all_to_all | solution.py:117
  121.7 19.5 %all-to-all-start = ((f32[2,64,16]{2,0,1:T(2,128)}), f32[2,64,16]{2,0,1:T(2,128)S(1)}, u32[]{:S(2)}, u32[]{:S(2)}) async-start(f32[2,64,16]{2,0,1:T(2,128)} %copy.22), calls=%async_computation | async-start | bytes 131072 | tf_op jit(solution)/shard_map/all_to_all | solution.py:118
  141.2 240.1 %all-to-all-start.2 = ((bf16[64,2,64,576]{3,2,1,0:T(8,128)(2,1)}), bf16[64,2,64,576]{3,2,1,0:T(8,128)(2,1)}, u32[]{:S(2)}, u32[]{:S(2)}) async-start(bf16[64,2,64,576]{3,2,1,0:T(8,128)(2,1)} %broadcast_select_fusion), calls=%async_computation.2 | async-start | bytes 20971520 | tf_op jit(solution)/shard_map/all_to_all | solution.py:106
  153.2 235.2 %copy-start.3 = (s32[1,2]{1,0:T(1,128)S(1)}, s32[1,2]{1,0:T(1,128)}, u32[]{:S(2)}) copy-start(s32[1,2]{1,0:T(1,128)} %param.15) | copy-start | bytes 28
  153.2 236.1 %copy-start.2 = (bf16[2,1,16,576]{3,2,1,0:T(8,128)(2,1)S(1)}, bf16[2,1,16,576]{3,2,1,0:T(8,128)(2,1)}, u32[]{:S(2)}) copy-start(bf16[2,1,16,576]{3,2,1,0:T(8,128)(2,1)} %param.9) | copy-start | bytes 110596
  153.2 236.1 %copy-start.4 = (bf16[2,1,576]{2,0,1:T(2,128)(2,1)S(1)}, bf16[2,1,576]{2,0,1:T(2,128)(2,1)}, u32[]{:S(2)}) copy-start(bf16[2,1,576]{2,0,1:T(2,128)(2,1)} %param.12) | copy-start | bytes 6916
  381.3 58.1 %all-to-all-start.3 = ((bf16[2,64,16,512]{3,2,0,1:T(8,128)(2,1)}), bf16[2,64,16,512]{3,2,0,1:T(8,128)(2,1)S(1)}, u32[]{:S(2)}, u32[]{:S(2)}) async-start(bf16[2,64,16,512]{3,2,0,1:T(8,128)(2,1)} %copy.27), calls=%async_computation.3 | async-start | bytes 4194304 | tf_op jit(solution)/shard_map/all_to_all | solution.py:114
Sparse Core Ops, SparseCore 0:
  10.6 82.5 all-gather.2
where the time goes:
time: 455 us; the launch traced here: 448 us
  waiting for transfers between devices  298 us (65%)
  blocking collectives  55.8 us (12%)
  starting transfers between devices  33.8 us (7%)
  other arithmetic  18.3 us (4%)
  local copies, waits for them, and re-layouts  15.4 us (3%)
  between operations  14.9 us (3%)
  matrix products  11.6 us (3%)
    all_to_all x1, waiting for transfers between devices, on_device(): lax.all_to_all(outgoing, 'req', split_axis=0, concat_axis=0, tiled=True)  228 us
    all_to_all x1, waiting for transfers between devices, on_device(): lax.all_to_all(out_p.astype(jnp.float32), 'req', split_axis=1, concat_axi...  42.2 us
    all_gather x1, blocking collectives, on_device(): lax.all_gather(fork_pages, 'req', axis=0, tiled=True)  36.6 us
    all_gather x1, waiting for transfers between devices, on_device(): every_query = lax.all_gather(queries, 'req', axis=1, tiled=True)  25.8 us
    unnamed x1, blocking collectives  19.3 us
    all_to_all x1, starting transfers between devices, on_device(): lax.all_to_all(outgoing, 'req', split_axis=0, concat_axis=0, tiled=True)  10.6 us
    select_n x1, other arithmetic, on_device(): jnp.where(owned[:, None, None, None], picked, jnp.zeros_like(picked))  9.98 us
    all_to_all x1, starting transfers between devices, on_device(): lax.all_to_all(total_p, 'req', split_axis=1, concat_axis=1, tiled=True)  9.46 us
  transfers between devices with their start and end apart: 5, of which 4 were waited for; matrix products, arithmetic and copies ran while one was open for 7% of the time, Pallas kernels for 0%

commit v1 on v0

v1 whole, which is shorter than its diff:
```python
import jax
import jax.numpy as jnp
from jax import lax
from jax.sharding import Mesh
from jax.sharding import PartitionSpec as P

DL = 512
LANES = 128
META_ROWS = 16

score_scale = 192.0 ** (-0.5)
neg_large = -1e30


def masked_softmax(rows, keys, mult):
    scores = jnp.einsum("gqk,tk->gqt", rows, keys, preferred_element_type=jnp.float32) * score_scale
    m = mult[:, None, :]
    valid = m > 0
    top = jnp.max(jnp.where(valid, scores, neg_large), axis=-1)
    weights = jnp.where(valid, jnp.exp(scores - top[..., None]), 0.0)
    total = jnp.sum(weights * m, axis=-1)
    rounded = weights.astype(jnp.bfloat16) * m.astype(jnp.bfloat16)
    summed = jnp.einsum("gqt,td->gqd", rounded, keys[:, :DL], preferred_element_type=jnp.float32)
    return top, total, summed


def own_partial(queries, keys, valid):
    scores = jnp.einsum("shk,tk->sht", queries, keys, preferred_element_type=jnp.float32) * score_scale
    scores = jnp.where(valid, scores, neg_large)
    top = jnp.max(scores, axis=-1)
    weights = jnp.where(valid, jnp.exp(scores - top[..., None]), 0.0)
    total = jnp.sum(weights, axis=-1)
    summed = jnp.einsum(
        "sht,td->shd", weights.astype(jnp.bfloat16), keys[:, :DL], preferred_element_type=jnp.float32
    )
    return top, total, summed


def on_device(queries, prompt_cache, suffix_cache, new_latent, suffix_len, parent, fork_pages):
    steps_n, _, head_dev, width = queries.shape
    pages_n, page_len = suffix_cache.shape[1], suffix_cache.shape[2]
    suffix_n = pages_n * page_len
    prompt_n = prompt_cache.shape[0]
    chips = lax.axis_size("chip")
    chip = lax.axis_index("chip")
    core = lax.axis_index("core")
    my_beam = chip * 2 + core
    partner_beam = chip * 2 + (1 - core)

    q_rows = steps_n * head_dev * width // LANES
    meta = jnp.zeros((META_ROWS, LANES), jnp.bfloat16)
    meta = meta.at[0, 0].set(parent[0].astype(jnp.bfloat16))
    meta = meta.at[0, 1].set(fork_pages[0, 0].astype(jnp.bfloat16))
    meta = meta.at[0, 2].set(fork_pages[0, 1].astype(jnp.bfloat16))
    packed = jnp.concatenate([queries.reshape(q_rows, LANES), meta], axis=0)
    gathered = lax.all_gather(packed, "chip", axis=0, tiled=False)
    rows = gathered[:, :q_rows].reshape(chips, steps_n * head_dev, width)
    meta_all = gathered[:, q_rows, :3].astype(jnp.int32)
    par, fp0, fp1 = meta_all[:, 0], meta_all[:, 1], meta_all[:, 2]

    own_suffix = suffix_cache.reshape(suffix_n, width)
    local_keys = jnp.concatenate([prompt_cache, own_suffix], axis=0)
    partner_keys, partner_len = lax.ppermute((local_keys, suffix_len), "core", [(0, 1), (1, 0)])
    keys = jnp.concatenate([local_keys, partner_keys], axis=0)

    position = jnp.arange(suffix_n, dtype=jnp.int32)
    page = position // page_len

    def fork_count(owner, length):
        hits = (page[None, :] == fp0[:, None]).astype(jnp.float32) + (page[None, :] == fp1[:, None]).astype(
            jnp.float32
        )
        keep = (par == owner)[:, None] & (position < length)[None, :]
        return jnp.where(keep, hits, 0.0)

    ones = jnp.ones((chips, prompt_n), jnp.float32)
    mult = jnp.concatenate(
        [ones, fork_count(my_beam, suffix_len[0]), ones, fork_count(partner_beam, partner_len[0])], axis=1
    )
    top, total, summed = masked_softmax(rows, keys, mult)
    out = (summed / total[..., None]).astype(jnp.bfloat16)

    out_r = lax.all_to_all(out, "chip", 0, 0, tiled=True)
    stats_r = lax.all_to_all(jnp.stack([top, total], axis=-1), "chip", 0, 0, tiled=True)
    top_r = stats_r[..., 0].reshape(chips, steps_n, head_dev)
    total_r = stats_r[..., 1].reshape(chips, steps_n, head_dev)
    out_r = out_r.astype(jnp.float32).reshape(chips, steps_n, head_dev, DL)

    own_keys = jnp.concatenate([own_suffix, new_latent[:, 0, :]], axis=0)
    old_valid = jnp.broadcast_to((position < suffix_len[0])[None, :], (steps_n, suffix_n))
    new_valid = jnp.arange(steps_n, dtype=jnp.int32)[None, :] <= jnp.arange(steps_n, dtype=jnp.int32)[:, None]
    own_valid = jnp.concatenate([old_valid, new_valid], axis=1)[:, None, :]
    top_l, total_l, summed_l = own_partial(queries[:, 0], own_keys, own_valid)

    peak = jnp.maximum(jnp.max(top_r, axis=0), top_l)
    weight_r = total_r * jnp.exp(top_r - peak[None])
    weight_l = jnp.exp(top_l - peak)
    denom = jnp.sum(weight_r, axis=0) + total_l * weight_l
    numer = jnp.sum(weight_r[..., None] * out_r, axis=0) + weight_l[..., None] * summed_l
    result = (numer / denom[..., None]).astype(jnp.bfloat16)
    return result[:, None]


def solution(mesh):
    req_n, head_n = mesh.devices.shape
    devices = mesh.devices.reshape(req_n // 2, 2, head_n)
    split = Mesh(devices, ("chip", "core", "hd"))
    beam = ("chip", "core")
    placed = (
        P(None, beam, "hd", None),
        P(beam, None),
        P(beam, None, None, None),
        P(None, beam, None),
        P(beam),
        P(beam),
        P(beam, None),
    )
    return jax.shard_map(
        on_device,
        mesh=split,
        in_specs=placed,
        out_specs=P(None, beam, "hd", None),
        check_vma=False,
    )
```

time: 455 us -> 179 us (0.39)
  the two profiles are of different devices: /device:TPU:448 before, /device:TPU:8 now
where the time goes in v1:
time: 179 us
  waiting for transfers between devices  98.2 us (55%)
  starting transfers between devices  19.4 us (11%)
  between operations  16.8 us (9%)
  local copies, waits for them, and re-layouts  15.6 us (9%)
  other arithmetic  15.3 us (9%)
  matrix products  13.3 us (7%)
    all_gather x1, waiting for transfers between devices, on_device(): gathered = lax.all_gather(packed, 'chip', axis=0, tiled=False)  74.2 us
    all_to_all x1, waiting for transfers between devices, on_device(): out_r = lax.all_to_all(out, 'chip', 0, 0, tiled=True)  22.1 us
    all_to_all x1, starting transfers between devices, on_device(): out_r = lax.all_to_all(out, 'chip', 0, 0, tiled=True)  7.9 us
    all_to_all x1, starting transfers between devices, on_device(): lax.all_to_all(jnp.stack([top, total], axis=-1), 'chip', 0, 0, tiled=True)  7.18 us
    dot_general x1, matrix products, masked_softmax(): jnp.einsum('gqt,td->gqd', rounded, keys[:, :DL], preferred_element_type=j...  6.88 us
    dot_general x1, matrix products, masked_softmax(): jnp.einsum('gqk,tk->gqt', rows, keys, preferred_element_type=jnp.float32)  5.15 us
    ppermute x2, starting transfers between devices, on_device(): lax.ppermute((local_keys, suffix_len), 'core', [(0, 1), (1, 0)])  4.33 us
  transfers between devices with their start and end apart: 5, of which 3 were waited for; matrix products, arithmetic and copies ran while one was open for 8% of the time, Pallas kernels for 0%

profile of v1, /device:TPU:8, one launch (start us, length us, event | category | flops | bytes accessed | tf_op | source)
XLA Modules:
  0.0 178.6 jit_solution(16595717622573044294)
XLA Ops:
  9.1 1.3 and_reduce_fusion
  11.1 2.1 %scatter.11 = bf16[16,128]{1,0:T(8,128)(2,1)S(1)} dynamic-update-slice(bf16[16,128]{1,0:T(8,128)(2,1)S(1)} %scatter.10, bf16[1,1]{1,0:T(2,128)(2,1)} %get-tuple-element.55, s32[]{:T(128)} %bitcast.1, s32[]{:T(128)} %bitcast.2) | dynamic-update-slice | bytes 8 | tf_op jit(solution)/shard_map/scatter | solution.py:53
  13.1 1.9 %dynamic-slice.21 = bf16[1,1]{1,0:T(2,128)(2,1)} dynamic-slice(bf16[16,128]{1,0:T(8,128)(2,1)S(1)} %scatter.11, s32[]{:T(128)} %bitcast.4, s32[]{:T(128)} %bitcast.5), dynamic_slice_sizes={1,1} | dynamic-slice | bytes 8 | tf_op jit(solution)/shard_map/dynamic-slice.17
  16.8 1.4 scatter.14
  18.2 0.9 reshape.334
  19.8 1.3 copy.27
  21.1 1.2 pad_maximum_fusion.1
  22.3 1.9 %collective-permute-start.1 = (bf16[1024,576]{0,1:T(8,128)(2,1)S(1)}, bf16[1024,576]{0,1:T(8,128)(2,1)S(1)}, u32[]{:S(2)}, u32[]{:S(2)}) collective-permute-start(bf16[1024,576]{0,1:T(8,128)(2,1)S(1)} %pad_maximum_fusion.1), channel_id=1, source_target_pairs={{0,8},{8,0},{1,9},{9,1},{2,10},{10,2},{3,11},{11,3},{4,12},{12,4},... | collective-permute-start | bytes 3538952 | tf_op jit(solution)/shard_map/ppermute | solution.py:63
  24.2 2.4 %collective-permute-start = (s32[1]{0:T(128)}, s32[1]{0:T(128)}, u32[]{:S(2)}, u32[]{:S(2)}) collective-permute-start(s32[1]{0:T(128)} %param.17), channel_id=1, source_target_pairs={{0,8},{8,0},{1,9},{9,1},{2,10},{10,2},{3,11},{11,3},{4,12},{12,4},... | collective-permute-start | bytes 20 | tf_op jit(solution)/shard_map/ppermute | solution.py:63
  28.4 1.2 iota_compare_fusion
  29.6 1.8 pad_maximum_fusion
  31.4 74.2 %all-gather.3.cloned.1.call-done = bf16[5120,128]{1,0:T(8,128)(2,1)} async-done(((bf16[160,128]{1,0:T(8,128)(2,1)}), bf16[5120,128]{1,0:T(8,128)(2,1)}) %all-gather.3.cloned.1.call-update) | async-done | bytes 1310736 | tf_op jit(solution)/shard_map/all_gather | solution.py:56
  105.6 0.8 slice.109
  106.4 1.4 slice.110
  112.0 1.9 %reshape.341 = bf16[32,32,576]{2,1,0:T(8,128)(2,1)} reshape(bf16[32,144,128]{2,1,0:T(8,128)(2,1)S(1)} %slice.110) | data formatting | bytes 2359296 | tf_op jit(solution)/shard_map/reshape | solution.py:57
  114.0 5.1 %select_reduce_fusion = (f32[32,32]{1,0:T(8,128)S(1)}, f32[32,32,2048]{2,1,0:T(8,128)S(1)}) fusion(pred[32,2048]{1,0:T(8,128)(4,1)} %broadcast_compare_fusion, bf16[32,32,576]{2,1,0:T(8,128)(2,1)} %reshape.341, bf16[1024,576]{0,1:T(8,128)(2,1)S(1)} %collective-permute-done.1, bf16[512,576]{0,1:T(8,128)(2,1)S(1)} %copy.27, bf16[512,576]{0,1:T(8,128)(2,1)S(1)} %copy-done.1), kind=kOutput, calls=%fused_computation.2 | convolution fusion | flops 2429287424 | bytes 11997184 | tf_op jit(solution)/shard_map/gqk,tk->gqt/dot_general | solution.py:16
  119.2 2.6 %multiply_reduce_fusion = f32[32,32]{1,0:T(8,128)S(1)} fusion(f32[32,32,2048]{2,1,0:T(8,128)S(1)} %get-tuple-element.59, f32[32,2048]{1,0:T(8,128)S(1)} %copy-done.3, f32[32,32]{1,0:T(8,128)S(1)} %get-tuple-element.58, pred[32,2048]{1,0:T(8,128)(4,1)S(1)} %copy-done.5), kind=kLoop, calls=%fused_computation | loop fusion | flops 10484736 | bytes 8724480 | tf_op jit(solution)/shard_map/reduce_sum | solution.py:21
  121.8 1.0 copy-done
  123.5 7.2 %all-to-all-start = ((f32[32,32,2]{1,2,0:T(2,128)}), f32[32,32,2]{1,2,0:T(2,128)S(1)}, u32[]{:S(2)}, u32[]{:S(2)}) async-start(f32[32,32,2]{1,2,0:T(2,128)} %pad_maximum_fusion.5), calls=%async_computation | async-start | bytes 65536 | tf_op jit(solution)/shard_map/all_to_all | solution.py:84
  130.7 6.9 %divide_convert_fusion = bf16[32,32,512]{2,1,0:T(8,128)(2,1)} fusion(f32[32,32]{1,0:T(8,128)S(1)} %multiply_reduce_fusion, bf16[2048,576]{0,1:T(8,128)(2,1)S(1)} %copy-done.2, f32[32,32,2048]{2,1,0:T(8,128)} %copy-done, f32[32,32]{1,0:T(8,128)S(1)} %get-tuple-element.58, pred[32,2048]{1,0:T(8,128)(4,1)S(1)} %copy-done.5, bf16[32,2048]{1,0:T(8,128)(2,1)S(1)} %copy-done.6), kind=kOutput, calls=%fused_computation.12 | convolution fusion | flops 2159017984 | bytes 11763712 | tf_op jit(solution)/shard_map/gqt,td->gqd/dot_general | solution.py:23
  137.6 1.9 %all-to-all-done = f32[32,32,2]{1,2,0:T(2,128)S(1)} async-done(((f32[32,32,2]{1,2,0:T(2,128)}), f32[32,32,2]{1,2,0:T(2,128)S(1)}, u32[]{:S(2)}, u32[]{:S(2)}) %all-to-all-start) | async-done | bytes 8224 | tf_op jit(solution)/shard_map/all_to_all | solution.py:84
  139.5 7.9 %all-to-all-start.1 = ((bf16[32,32,512]{2,1,0:T(8,128)(2,1)}), bf16[32,32,512]{2,1,0:T(8,128)(2,1)S(1)}, u32[]{:S(2)}, u32[]{:S(2)}) async-start(bf16[32,32,512]{2,1,0:T(8,128)(2,1)} %divide_convert_fusion), calls=%async_computation.1 | async-start | bytes 2097152 | tf_op jit(solution)/shard_map/all_to_all | solution.py:83
  148.5 22.1 %all-to-all-done.1 = bf16[32,32,512]{2,1,0:T(8,128)(2,1)S(1)} async-done(((bf16[32,32,512]{2,1,0:T(8,128)(2,1)}), bf16[32,32,512]{2,1,0:T(8,128)(2,1)S(1)}, u32[]{:S(2)}, u32[]{:S(2)}) %all-to-all-start.1) | async-done | bytes 1048608 | tf_op jit(solution)/shard_map/all_to_all | solution.py:83
  170.9 0.9 fusion.13
  (58 shorter events, 10.5 us)
Async XLA Ops:
  6.5 23.1 %copy-start.1 = (bf16[512,576]{0,1:T(8,128)(2,1)S(1)}, bf16[512,576]{0,1:T(8,128)(2,1)}, u32[]{:S(2)}) copy-start(bf16[512,576]{0,1:T(8,128)(2,1)} %param.14) | copy-start | bytes 1769476
  6.5 99.1 %all-gather.3.cloned.1.call-start = ((), (), s32[]{:S(2)}) async-start(), calls=%async_computation.2 | async-start | bytes 1351680 | tf_op jit(solution)/shard_map/all_gather | solution.py:56
  22.3 7.3 %collective-permute-start.1 = (bf16[1024,576]{0,1:T(8,128)(2,1)S(1)}, bf16[1024,576]{0,1:T(8,128)(2,1)S(1)}, u32[]{:S(2)}, u32[]{:S(2)}) collective-permute-start(bf16[1024,576]{0,1:T(8,128)(2,1)S(1)} %pad_maximum_fusion.1), channel_id=1, source_target_pairs={{0,8},{8,0},{1,9},{9,1},{2,10},{10,2},{3,11},{11,3},{4,12},{12,4},... | collective-permute-start | bytes 3538952 | tf_op jit(solution)/shard_map/ppermute | solution.py:63
  24.2 4.2 %collective-permute-start = (s32[1]{0:T(128)}, s32[1]{0:T(128)}, u32[]{:S(2)}, u32[]{:S(2)}) collective-permute-start(s32[1]{0:T(128)} %param.17), channel_id=1, source_target_pairs={{0,8},{8,0},{1,9},{9,1},{2,10},{10,2},{3,11},{11,3},{4,12},{12,4},... | collective-permute-start | bytes 20 | tf_op jit(solution)/shard_map/ppermute | solution.py:63
  114.0 5.2 %copy-start.3 = (f32[32,2048]{1,0:T(8,128)S(1)}, f32[32,2048]{1,0:T(8,128)}, u32[]{:S(2)}) copy-start(f32[32,2048]{1,0:T(8,128)} %pad_maximum_fusion.3) | copy-start | bytes 786436
  114.0 5.2 %copy-start.5 = (pred[32,2048]{1,0:T(8,128)(4,1)S(1)}, pred[32,2048]{1,0:T(8,128)(4,1)}, u32[]{:S(2)}) copy-start(pred[32,2048]{1,0:T(8,128)(4,1)} %broadcast_compare_fusion) | copy-start | bytes 196612
  119.1 3.7 %copy-start = (f32[32,32,2048]{2,1,0:T(8,128)}, f32[32,32,2048]{2,1,0:T(8,128)S(1)}, u32[]{:S(2)}) copy-start(f32[32,32,2048]{2,1,0:T(8,128)S(1)} %get-tuple-element.59) | copy-start | bytes 25165828
  119.1 11.5 %copy-start.2 = (bf16[2048,576]{0,1:T(8,128)(2,1)S(1)}, bf16[2048,576]{0,1:T(8,128)(2,1)}, u32[]{:S(2)}) copy-start(bf16[2048,576]{0,1:T(8,128)(2,1)} %pad_maximum_fusion) | copy-start | bytes 7077892
  119.2 11.5 %copy-start.6 = (bf16[32,2048]{1,0:T(8,128)(2,1)S(1)}, bf16[32,2048]{1,0:T(8,128)(2,1)}, u32[]{:S(2)}) copy-start(bf16[32,2048]{1,0:T(8,128)(2,1)} %fusion.40) | copy-start | bytes 393220
  123.5 16.0 %all-to-all-start = ((f32[32,32,2]{1,2,0:T(2,128)}), f32[32,32,2]{1,2,0:T(2,128)S(1)}, u32[]{:S(2)}, u32[]{:S(2)}) async-start(f32[32,32,2]{1,2,0:T(2,128)} %pad_maximum_fusion.5), calls=%async_computation | async-start | bytes 65536 | tf_op jit(solution)/shard_map/all_to_all | solution.py:84
  130.7 16.7 %copy-start.8 = (pred[512]{0:T(512)(128)(4,1)S(1)}, pred[512]{0:T(512)(128)(4,1)}, u32[]{:S(2)}) copy-start(pred[512]{0:T(512)(128)(4,1)} %iota_compare_fusion.1) | copy-start | bytes 1540
  130.7 16.8 %copy-start.4 = (bf16[1,8,64,576]{3,2,1,0:T(8,128)(2,1)S(1)}, bf16[1,8,64,576]{3,2,1,0:T(8,128)(2,1)}, u32[]{:S(2)}) copy-start(bf16[1,8,64,576]{3,2,1,0:T(8,128)(2,1)} %param.15) | copy-start | bytes 1769476
  130.7 16.8 %copy-start.7 = (bf16[2,1,16,576]{3,2,1,0:T(8,128)(2,1)S(1)}, bf16[2,1,16,576]{3,2,1,0:T(8,128)(2,1)}, u32[]{:S(2)}) copy-start(bf16[2,1,16,576]{3,2,1,0:T(8,128)(2,1)} %param.13) | copy-start | bytes 110596
  130.7 16.8 %copy-start.9 = (bf16[2,1,576]{2,0,1:T(2,128)(2,1)S(1)}, bf16[2,1,576]{2,0,1:T(2,128)(2,1)}, u32[]{:S(2)}) copy-start(bf16[2,1,576]{2,0,1:T(2,128)(2,1)} %param.16) | copy-start | bytes 6916
  139.5 31.1 %all-to-all-start.1 = ((bf16[32,32,512]{2,1,0:T(8,128)(2,1)}), bf16[32,32,512]{2,1,0:T(8,128)(2,1)S(1)}, u32[]{:S(2)}, u32[]{:S(2)}) async-start(bf16[32,32,512]{2,1,0:T(8,128)(2,1)} %divide_convert_fusion), calls=%async_computation.1 | async-start | bytes 2097152 | tf_op jit(solution)/shard_map/all_to_all | solution.py:83
Sparse Core Ops, SparseCore 0:
  19.9 85.6 all-gather.2

commit v2 on v1

--- a/solution.py
+++ b/solution.py
@@ -22,6 +22,14 @@
     rounded = weights.astype(jnp.bfloat16) * m.astype(jnp.bfloat16)
     summed = jnp.einsum("gqt,td->gqd", rounded, keys[:, :DL], preferred_element_type=jnp.float32)
     return top, total, summed
+
+
+def split3(x):
+    hi = lax.reduce_precision(x, exponent_bits=8, mantissa_bits=7)
+    rest = x - hi
+    mid = lax.reduce_precision(rest, exponent_bits=8, mantissa_bits=7)
+    lo = lax.reduce_precision(rest - mid, exponent_bits=8, mantissa_bits=7)
+    return [hi.astype(jnp.bfloat16), mid.astype(jnp.bfloat16), lo.astype(jnp.bfloat16)]
 
 
 def own_partial(queries, keys, valid):
@@ -53,7 +61,8 @@
     meta = meta.at[0, 1].set(fork_pages[0, 0].astype(jnp.bfloat16))
     meta = meta.at[0, 2].set(fork_pages[0, 1].astype(jnp.bfloat16))
     packed = jnp.concatenate([queries.reshape(q_rows, LANES), meta], axis=0)
-    gathered = lax.all_gather(packed, "chip", axis=0, tiled=False)
+    send = jnp.broadcast_to(packed[None], (chips,) + packed.shape)
+    gathered = lax.all_to_all(send, "chip", 0, 0, tiled=True)
     rows = gathered[:, :q_rows].reshape(chips, steps_n * head_dev, width)
     meta_all = gathered[:, q_rows, :3].astype(jnp.int32)
     par, fp0, fp1 = meta_all[:, 0], meta_all[:, 1], meta_all[:, 2]
@@ -80,11 +89,18 @@
     top, total, summed = masked_softmax(rows, keys, mult)
     out = (summed / total[..., None]).astype(jnp.bfloat16)
 
-    out_r = lax.all_to_all(out, "chip", 0, 0, tiled=True)
-    stats_r = lax.all_to_all(jnp.stack([top, total], axis=-1), "chip", 0, 0, tiled=True)
-    top_r = stats_r[..., 0].reshape(chips, steps_n, head_dev)
-    total_r = stats_r[..., 1].reshape(chips, steps_n, head_dev)
-    out_r = out_r.astype(jnp.float32).reshape(chips, steps_n, head_dev, DL)
+    out_rows = out.reshape(chips, -1, LANES)
+    parts = jnp.stack(split3(top) + split3(total), axis=1).reshape(chips, -1)
+    stat_rows = -(-parts.shape[1] // (META_ROWS * LANES)) * META_ROWS
+    parts = jnp.pad(parts, ((0, 0), (0, stat_rows * LANES - parts.shape[1])))
+    payload = jnp.concatenate([out_rows, parts.reshape(chips, stat_rows, LANES)], axis=1)
+    arrived = lax.all_to_all(payload, "chip", 0, 0, tiled=True)
+    n_out = out_rows.shape[1]
+    out_r = arrived[:, :n_out].astype(jnp.float32).reshape(chips, steps_n, head_dev, DL)
+    row_n = steps_n * head_dev
+    got = arrived[:, n_out:].reshape(chips, -1)[:, : 6 * row_n].astype(jnp.float32).reshape(chips, 6, row_n)
+    top_r = ((got[:, 0] + got[:, 1]) + got[:, 2]).reshape(chips, steps_n, head_dev)
+    total_r = ((got[:, 3] + got[:, 4]) + got[:, 5]).reshape(chips, steps_n, head_dev)
 
     own_keys = jnp.concatenate([own_suffix, new_latent[:, 0, :]], axis=0)
     old_valid = jnp.broadcast_to((position < suffix_len[0])[None, :], (steps_n, suffix_n))

time: 179 us -> 116 us (0.65)
  the two profiles are of different devices: /device:TPU:8 before, /device:TPU:448 now
where the time goes in v2:
time: 116 us; the launch traced here: 115 us
  waiting for transfers between devices  54.3 us (47%)
  starting transfers between devices  19.5 us (17%)
  local copies, waits for them, and re-layouts  16 us (14%)
  other arithmetic  11.6 us (10%)
  matrix products  10.3 us (9%)
  between operations  3.68 us (3%)
    all_to_all x1, waiting for transfers between devices, on_device(): arrived = lax.all_to_all(payload, 'chip', 0, 0, tiled=True)  30.3 us
    all_to_all x1, waiting for transfers between devices, on_device(): gathered = lax.all_to_all(send, 'chip', 0, 0, tiled=True)  23.6 us
    all_to_all x1, starting transfers between devices, on_device(): gathered = lax.all_to_all(send, 'chip', 0, 0, tiled=True)  9.95 us
    dot_general x1, matrix products, masked_softmax(): jnp.einsum('gqk,tk->gqt', rows, keys, preferred_element_type=jnp.float32)  5.44 us
    all_to_all x1, starting transfers between devices, on_device(): arrived = lax.all_to_all(payload, 'chip', 0, 0, tiled=True)  5.23 us
    ppermute x2, starting transfers between devices, on_device(): lax.ppermute((local_keys, suffix_len), 'core', [(0, 1), (1, 0)])  4.32 us
    mul x2, local copies, waits for them, and re-layouts, on_device(): weight_r[..., None] * out_r  3.18 us
    concatenate x1, other arithmetic, on_device(): keys = jnp.concatenate([local_keys, partner_keys], axis=0)  3 us
  transfers between devices with their start and end apart: 4, of which 3 were waited for; matrix products, arithmetic and copies ran while one was open for 5% of the time, Pallas kernels for 0%

profile of v2, /device:TPU:448, one launch (start us, length us, event | category | flops | bytes accessed | tf_op | source)
XLA Modules:
  0.0 115.3 jit_solution(6726662490945185811)
XLA Ops:
  0.6 0.7 convert.6
  3.1 1.4 %and_reduce_fusion = pred[]{:T(512)} fusion(s32[2]{0:T(128)} %constant.107.clone.1), kind=kLoop, calls=%fused_computation.84 | loop fusion | flops 9 | bytes 9 | tf_op jit(solution)/shard_map/reduce.5
  4.5 1.9 %scatter.11 = bf16[16,128]{1,0:T(8,128)(2,1)S(1)} dynamic-update-slice(bf16[16,128]{1,0:T(8,128)(2,1)S(1)} %scatter.10, bf16[1,1]{1,0:T(2,128)(2,1)} %get-tuple-element.57, s32[]{:T(128)} %bitcast.1, s32[]{:T(128)} %bitcast.2) | dynamic-update-slice | bytes 8 | tf_op jit(solution)/shard_map/scatter | solution.py:61
  6.4 1.8 %dynamic-slice.21 = bf16[1,1]{1,0:T(2,128)(2,1)} dynamic-slice(bf16[16,128]{1,0:T(8,128)(2,1)S(1)} %scatter.11, s32[]{:T(128)} %bitcast.4, s32[]{:T(128)} %bitcast.5), dynamic_slice_sizes={1,1} | dynamic-slice | bytes 8 | tf_op jit(solution)/shard_map/dynamic-slice.17
  10.2 1.3 %scatter.14 = bf16[16,128]{1,0:T(8,128)(2,1)S(1)} dynamic-update-slice(bf16[16,128]{1,0:T(8,128)(2,1)S(1)} %scatter.11, bf16[1,1]{1,0:T(2,128)(2,1)S(6)} %select.18, s32[]{:T(128)} %bitcast.4, s32[]{:T(128)} %bitcast.5) | dynamic-update-slice | bytes 8 | tf_op jit(solution)/shard_map/scatter | solution.py:62
  11.5 0.9 reshape.454
  12.4 1.2 %broadcast_in_dim.80 = bf16[32,160,128]{2,1,0:T(8,128)(2,1)} broadcast(bf16[160,128]{1,0:T(8,128)(2,1)S(1)} %pad_maximum_fusion.5), dimensions={1,2} | broadcast | bytes 1351680 | tf_op jit(solution)/shard_map/broadcast_in_dim | solution.py:64
  13.7 10.0 %all-to-all-start = ((bf16[32,160,128]{2,1,0:T(8,128)(2,1)}), bf16[32,160,128]{2,1,0:T(8,128)(2,1)S(1)}, u32[]{:S(2)}, u32[]{:S(2)}) async-start(bf16[32,160,128]{2,1,0:T(8,128)(2,1)} %broadcast_in_dim.80), calls=%async_computation | async-start | bytes 2621440 | tf_op jit(solution)/shard_map/all_to_all | solution.py:65
  23.9 1.2 %pad_maximum_fusion.1 = bf16[1024,576]{0,1:T(8,128)(2,1)} fusion(bf16[512,576]{0,1:T(8,128)(2,1)S(1)} %copy.33, bf16[512,576]{0,1:T(8,128)(2,1)S(1)} %copy-done), kind=kLoop, calls=%fused_computation.14 | loop fusion | flops 2359296 | bytes 2359296 | tf_op jit(solution)/shard_map/concatenate | solution.py:71
  25.1 1.9 %collective-permute-start.1 = (bf16[1024,576]{0,1:T(8,128)(2,1)}, bf16[1024,576]{0,1:T(8,128)(2,1)}, u32[]{:S(2)}, u32[]{:S(2)}) collective-permute-start(bf16[1024,576]{0,1:T(8,128)(2,1)} %pad_maximum_fusion.1), channel_id=1, source_target_pairs={{0,8},{8,0},{1,9},{9,1},{2,10},{10,2},{3,11},{11,3},{4,12},{12,4},... | collective-permute-start | bytes 3538952 | tf_op jit(solution)/shard_map/ppermute | solution.py:72
  27.0 2.4 %collective-permute-start = (s32[1]{0:T(128)}, s32[1]{0:T(128)}, u32[]{:S(2)}, u32[]{:S(2)}) collective-permute-start(s32[1]{0:T(128)} %param.17), channel_id=1, source_target_pairs={{0,8},{8,0},{1,9},{9,1},{2,10},{10,2},{3,11},{11,3},{4,12},{12,4},... | collective-permute-start | bytes 20 | tf_op jit(solution)/shard_map/ppermute | solution.py:72
  31.1 3.0 %pad_maximum_fusion = bf16[2048,576]{0,1:T(8,128)(2,1)} fusion(bf16[1024,576]{0,1:T(8,128)(2,1)} %collective-permute-done.1, bf16[512,576]{0,1:T(8,128)(2,1)S(1)} %copy.33, bf16[512,576]{0,1:T(8,128)(2,1)S(1)} %copy-done), kind=kLoop, calls=%fused_computation.7 | loop fusion | flops 7077888 | bytes 4718592 | tf_op jit(solution)/shard_map/concatenate | solution.py:73
  34.1 23.6 %all-to-all-done = bf16[32,160,128]{2,1,0:T(8,128)(2,1)S(1)} async-done(((bf16[32,160,128]{2,1,0:T(8,128)(2,1)}), bf16[32,160,128]{2,1,0:T(8,128)(2,1)S(1)}, u32[]{:S(2)}, u32[]{:S(2)}) %all-to-all-start) | async-done | bytes 1310752 | tf_op jit(solution)/shard_map/all_to_all | solution.py:65
  58.2 2.0 %reshape.461 = bf16[32,32,576]{2,1,0:T(8,128)(2,1)} reshape(bf16[32,144,128]{2,1,0:T(8,128)(2,1)S(1)} %slice.138) | data formatting | bytes 2359296 | tf_op jit(solution)/shard_map/reshape | solution.py:66
  60.1 5.4 %select_reduce_fusion = (f32[32,32]{1,0:T(8,128)S(1)}, f32[32,32,2048]{2,1,0:T(8,128)S(1)}) fusion(pred[32,2048]{1,0:T(8,128)(4,1)S(1)} %broadcast_compare_fusion, bf16[32,32,576]{2,1,0:T(8,128)(2,1)} %reshape.461, bf16[1024,576]{0,1:T(8,128)(2,1)} %collective-permute-done.1, bf16[512,576]{0,1:T(8,128)(2,1)S(1)} %copy.33, bf16[512,576]{0,1:T(8,128)(2,1)S(1)} %copy-done.1), kind=kOutput, calls=%fused_computation.2 | convolution fusion | flops 2429287424 | bytes 11997184 | tf_op jit(solution)/shard_map/gqk,tk->gqt/dot_general | solution.py:16
  65.6 2.7 %multiply_reduce_fusion = f32[32,32]{1,0:T(8,128)S(1)} fusion(f32[32,32,2048]{2,1,0:T(8,128)S(1)} %get-tuple-element.61, f32[32,2048]{1,0:T(8,128)S(1)} %pad_maximum_fusion.4, f32[32,32]{1,0:T(8,128)S(1)} %get-tuple-element.60, pred[32,2048]{1,0:T(8,128)(4,1)S(1)} %broadcast_compare_fusion), kind=kLoop, calls=%fused_computation | loop fusion | flops 10484736 | bytes 8724480 | tf_op jit(solution)/shard_map/reduce_sum | solution.py:21
  68.3 2.5 %divide_convert_fusion = bf16[32,32,512]{2,1,0:T(8,128)(2,1)S(1)} fusion(f32[32,32]{1,0:T(8,128)S(1)} %multiply_reduce_fusion, bf16[2048,576]{0,1:T(8,128)(2,1)S(1)} %copy-done.2, f32[32,32,2048]{2,1,0:T(8,128)S(1)} %get-tuple-element.61, f32[32,32]{1,0:T(8,128)S(1)} %get-tuple-element.60, pred[32,2048]{1,0:T(8,128)(4,1)S(1)} %broadcast_compare_fusion, ...), kind=kOutput, calls=%fused_computation.12 | convolution fusion | flops 2159017984 | bytes 11763712 | tf_op jit(solution)/shard_map/gqt,td->gqd/dot_general | solution.py:23
  70.8 0.7 reshape.463
  71.7 1.1 pad_maximum_fusion.2
  72.8 5.2 %all-to-all-start.1 = ((bf16[32,144,128]{2,1,0:T(8,128)(2,1)}), bf16[32,144,128]{2,1,0:T(8,128)(2,1)S(1)}, u32[]{:S(2)}, u32[]{:S(2)}) async-start(bf16[32,144,128]{2,1,0:T(8,128)(2,1)} %pad_maximum_fusion.2), calls=%async_computation.1 | async-start | bytes 2359296 | tf_op jit(solution)/shard_map/all_to_all | solution.py:97
  78.8 30.3 %all-to-all-done.1 = bf16[32,144,128]{2,1,0:T(8,128)(2,1)S(1)} async-done(((bf16[32,144,128]{2,1,0:T(8,128)(2,1)}), bf16[32,144,128]{2,1,0:T(8,128)(2,1)S(1)}, u32[]{:S(2)}, u32[]{:S(2)}) %all-to-all-start.1) | async-done | bytes 1179680 | tf_op jit(solution)/shard_map/all_to_all | solution.py:97
  109.9 1.6 %mul.82 = f32[32,2,16,512]{3,2,1,0:T(8,128)} broadcast(f32[32,2,16]{2,1,0:T(2,128)S(1)} %copy.38), dimensions={0,1,2} | broadcast | bytes 2101248 | tf_op jit(solution)/shard_map/mul | solution.py:115
  111.4 1.6 %mul.83 = f32[32,128,128]{2,1,0:T(8,128)S(1)} reshape(f32[32,2,16,512]{3,2,1,0:T(8,128)} %mul.82) | data formatting | bytes 4194304 | tf_op jit(solution)/shard_map/mul | solution.py:115
  113.4 1.9 %fusion.13 = bf16[2,1,16,512]{3,2,1,0:T(8,128)(2,1)} fusion(f32[2,16,512]{2,1,0:T(8,128)S(1)} %reduce_sum.45, bf16[512,576]{1,0:T(8,128)(2,1)} %bitcast.93, bf16[2,576]{1,0:T(2,128)(2,1)S(1)} %bitcast.104, f32[2,16,514]{2,1,0:T(8,128)S(1)} %get-tuple-element.63, f32[2,16]{1,0:T(2,128)S(1)} %get-tuple-element.62, pred[2,514]{1,0:T(4,128)(4,1)S(1)} %pad_add_fusion, ...), kind=kOutput, calls=%fused_computation.23 | convolution fusion | flops 18010304 | bytes 757636 | tf_op jit(solution)/shard_map/sht,td->shd/dot_general | solution.py:41
  (71 shorter events, 5.5 us)
Async XLA Ops:
  0.0 23.6 %copy-start.3 = (bf16[1,8,64,576]{3,2,1,0:T(8,128)(2,1)S(1)}, bf16[1,8,64,576]{3,2,1,0:T(8,128)(2,1)}, u32[]{:S(2)}) copy-start(bf16[1,8,64,576]{3,2,1,0:T(8,128)(2,1)} %param.15) | copy-start | bytes 1769476
  12.4 11.5 %copy-start = (bf16[512,576]{0,1:T(8,128)(2,1)S(1)}, bf16[512,576]{0,1:T(8,128)(2,1)}, u32[]{:S(2)}) copy-start(bf16[512,576]{0,1:T(8,128)(2,1)} %param.14) | copy-start | bytes 1769476
  13.7 44.1 %all-to-all-start = ((bf16[32,160,128]{2,1,0:T(8,128)(2,1)}), bf16[32,160,128]{2,1,0:T(8,128)(2,1)S(1)}, u32[]{:S(2)}, u32[]{:S(2)}) async-start(bf16[32,160,128]{2,1,0:T(8,128)(2,1)} %broadcast_in_dim.80), calls=%async_computation | async-start | bytes 2621440 | tf_op jit(solution)/shard_map/all_to_all | solution.py:65
  25.1 6.0 %collective-permute-start.1 = (bf16[1024,576]{0,1:T(8,128)(2,1)}, bf16[1024,576]{0,1:T(8,128)(2,1)}, u32[]{:S(2)}, u32[]{:S(2)}) collective-permute-start(bf16[1024,576]{0,1:T(8,128)(2,1)} %pad_maximum_fusion.1), channel_id=1, source_target_pairs={{0,8},{8,0},{1,9},{9,1},{2,10},{10,2},{3,11},{11,3},{4,12},{12,4},... | collective-permute-start | bytes 3538952 | tf_op jit(solution)/shard_map/ppermute | solution.py:72
  27.0 3.5 %collective-permute-start = (s32[1]{0:T(128)}, s32[1]{0:T(128)}, u32[]{:S(2)}, u32[]{:S(2)}) collective-permute-start(s32[1]{0:T(128)} %param.17), channel_id=1, source_target_pairs={{0,8},{8,0},{1,9},{9,1},{2,10},{10,2},{3,11},{11,3},{4,12},{12,4},... | collective-permute-start | bytes 20 | tf_op jit(solution)/shard_map/ppermute | solution.py:72
  58.2 2.0 %copy-start.1 = (bf16[512,576]{0,1:T(8,128)(2,1)S(1)}, bf16[512,576]{0,1:T(8,128)(2,1)}, u32[]{:S(2)}) copy-start(bf16[512,576]{0,1:T(8,128)(2,1)} %param.14) | copy-start | bytes 1769476
  65.6 2.7 %copy-start.2 = (bf16[2048,576]{0,1:T(8,128)(2,1)S(1)}, bf16[2048,576]{0,1:T(8,128)(2,1)}, u32[]{:S(2)}) copy-start(bf16[2048,576]{0,1:T(8,128)(2,1)} %pad_maximum_fusion) | copy-start | bytes 7077892
  71.7 6.4 %copy-start.4 = (bf16[1,8,64,576]{3,2,1,0:T(8,128)(2,1)S(1)}, bf16[1,8,64,576]{3,2,1,0:T(8,128)(2,1)}, u32[]{:S(2)}) copy-start(bf16[1,8,64,576]{3,2,1,0:T(8,128)(2,1)} %param.15) | copy-start | bytes 1769476
  71.7 6.4 %copy-start.5 = (bf16[2,1,16,576]{3,2,1,0:T(8,128)(2,1)S(1)}, bf16[2,1,16,576]{3,2,1,0:T(8,128)(2,1)}, u32[]{:S(2)}) copy-start(bf16[2,1,16,576]{3,2,1,0:T(8,128)(2,1)} %param.13) | copy-start | bytes 110596
  71.7 6.4 %copy-start.6 = (bf16[2,1,576]{2,0,1:T(2,128)(2,1)S(1)}, bf16[2,1,576]{2,0,1:T(2,128)(2,1)}, u32[]{:S(2)}) copy-start(bf16[2,1,576]{2,0,1:T(2,128)(2,1)} %param.16) | copy-start | bytes 6916
  72.8 36.3 %all-to-all-start.1 = ((bf16[32,144,128]{2,1,0:T(8,128)(2,1)}), bf16[32,144,128]{2,1,0:T(8,128)(2,1)S(1)}, u32[]{:S(2)}, u32[]{:S(2)}) async-start(bf16[32,144,128]{2,1,0:T(8,128)(2,1)} %pad_maximum_fusion.2), calls=%async_computation.1 | async-start | bytes 2359296 | tf_op jit(solution)/shard_map/all_to_all | solution.py:97

commit v3 on v2

--- a/solution.py
+++ b/solution.py
@@ -49,20 +49,24 @@
     pages_n, page_len = suffix_cache.shape[1], suffix_cache.shape[2]
     suffix_n = pages_n * page_len
     prompt_n = prompt_cache.shape[0]
-    chips = lax.axis_size("chip")
-    chip = lax.axis_index("chip")
+    chips = lax.axis_size("cx") * lax.axis_size("cy")
+    chip = lax.axis_index("cx") * lax.axis_size("cy") + lax.axis_index("cy")
     core = lax.axis_index("core")
     my_beam = chip * 2 + core
     partner_beam = chip * 2 + (1 - core)
 
     q_rows = steps_n * head_dev * width // LANES
-    meta = jnp.zeros((META_ROWS, LANES), jnp.bfloat16)
-    meta = meta.at[0, 0].set(parent[0].astype(jnp.bfloat16))
-    meta = meta.at[0, 1].set(fork_pages[0, 0].astype(jnp.bfloat16))
-    meta = meta.at[0, 2].set(fork_pages[0, 1].astype(jnp.bfloat16))
+    lane = lax.broadcasted_iota(jnp.int32, (META_ROWS, LANES), 1)
+    first = lax.broadcasted_iota(jnp.int32, (META_ROWS, LANES), 0) == 0
+    meta = jnp.where(lane == 0, parent[0], jnp.where(lane == 1, fork_pages[0, 0], fork_pages[0, 1]))
+    meta = jnp.where(first & (lane < 3), meta, 0).astype(jnp.bfloat16)
     packed = jnp.concatenate([queries.reshape(q_rows, LANES), meta], axis=0)
-    send = jnp.broadcast_to(packed[None], (chips,) + packed.shape)
-    gathered = lax.all_to_all(send, "chip", 0, 0, tiled=True)
+    along_y = lax.all_to_all(
+        jnp.broadcast_to(packed[None], (lax.axis_size("cy"),) + packed.shape), "cy", 0, 0, tiled=True
+    )
+    gathered = lax.all_to_all(
+        jnp.broadcast_to(along_y[None], (lax.axis_size("cx"),) + along_y.shape), "cx", 0, 0, tiled=True
+    ).reshape((chips,) + packed.shape)
     rows = gathered[:, :q_rows].reshape(chips, steps_n * head_dev, width)
     meta_all = gathered[:, q_rows, :3].astype(jnp.int32)
     par, fp0, fp1 = meta_all[:, 0], meta_all[:, 1], meta_all[:, 2]
@@ -94,13 +98,13 @@
     stat_rows = -(-parts.shape[1] // (META_ROWS * LANES)) * META_ROWS
     parts = jnp.pad(parts, ((0, 0), (0, stat_rows * LANES - parts.shape[1])))
     payload = jnp.concatenate([out_rows, parts.reshape(chips, stat_rows, LANES)], axis=1)
-    arrived = lax.all_to_all(payload, "chip", 0, 0, tiled=True)
+    arrived = lax.all_to_all(payload, ("cx", "cy"), 0, 0, tiled=True)
     n_out = out_rows.shape[1]
-    out_r = arrived[:, :n_out].astype(jnp.float32).reshape(chips, steps_n, head_dev, DL)
     row_n = steps_n * head_dev
+    out_r = arrived[:, :n_out].reshape(chips, row_n, DL)
     got = arrived[:, n_out:].reshape(chips, -1)[:, : 6 * row_n].astype(jnp.float32).reshape(chips, 6, row_n)
-    top_r = ((got[:, 0] + got[:, 1]) + got[:, 2]).reshape(chips, steps_n, head_dev)
-    total_r = ((got[:, 3] + got[:, 4]) + got[:, 5]).reshape(chips, steps_n, head_dev)
+    top_r = (got[:, 0] + got[:, 1]) + got[:, 2]
+    total_r = (got[:, 3] + got[:, 4]) + got[:, 5]
 
     own_keys = jnp.concatenate([own_suffix, new_latent[:, 0, :]], axis=0)
     old_valid = jnp.broadcast_to((position < suffix_len[0])[None, :], (steps_n, suffix_n))
@@ -108,20 +112,35 @@
     own_valid = jnp.concatenate([old_valid, new_valid], axis=1)[:, None, :]
     top_l, total_l, summed_l = own_partial(queries[:, 0], own_keys, own_valid)
 
+    top_l = top_l.reshape(row_n)
+    total_l = total_l.reshape(row_n)
+    summed_l = summed_l.reshape(row_n, DL)
     peak = jnp.maximum(jnp.max(top_r, axis=0), top_l)
     weight_r = total_r * jnp.exp(top_r - peak[None])
     weight_l = jnp.exp(top_l - peak)
     denom = jnp.sum(weight_r, axis=0) + total_l * weight_l
-    numer = jnp.sum(weight_r[..., None] * out_r, axis=0) + weight_l[..., None] * summed_l
-    result = (numer / denom[..., None]).astype(jnp.bfloat16)
-    return result[:, None]
+    numer = jnp.sum(weight_r[..., None] * out_r.astype(jnp.float32), axis=0) + weight_l[:, None] * summed_l
+    result = (numer / denom[:, None]).astype(jnp.bfloat16)
+    return result.reshape(steps_n, 1, head_dev, DL)
+
+
+def chip_grid(devices):
+    try:
+        xs = {d.coords[0] for d in devices.flat}
+        ys = {d.coords[1] for d in devices.flat}
+        if len(xs) * len(ys) * 2 == devices.shape[0]:
+            return len(xs), len(ys)
+    except (AttributeError, IndexError, TypeError):
+        pass
+    return 1, devices.shape[0] // 2
 
 
 def solution(mesh):
     req_n, head_n = mesh.devices.shape
-    devices = mesh.devices.reshape(req_n // 2, 2, head_n)
-    split = Mesh(devices, ("chip", "core", "hd"))
-    beam = ("chip", "core")
+    x_n, y_n = chip_grid(mesh.devices)
+    devices = mesh.devices.reshape(x_n, y_n, 2, head_n)
+    split = Mesh(devices, ("cx", "cy", "core", "hd"))
+    beam = ("cx", "cy", "core")
     placed = (
         P(None, beam, "hd", None),
         P(beam, None),

time: 116 us -> 99 us (0.85)
  local copies, waits for them, and re-layouts: 16 us -> 9.17 us
  waiting for transfers between devices: 54.3 us -> 47.7 us
  between operations: 3.68 us -> 1.66 us
    all_to_all x2 -> x3, waiting for transfers between devices: 53.9 us -> 46.9 us  [the longest x1 28.6 us: on_device(): arrived = lax.all_to_all(payload, ('cx', 'cy'), 0, 0, tiled=True)]
    scatter x3 -> x0, local copies, waits for them, and re-layouts: 3.2 us -> none  [the longest x1 1.89 us: on_device(): meta = meta.at[0, 1].set(fork_pages[0, 0].astype(jnp.bfloat16))]
    mul x2, local copies, waits for them, and re-layouts: 3.18 us -> 0.07 us  [on_device(): weight_r[..., None] * out_r.astype(jnp.float32)]
    another operation x4 -> x0, local copies, waits for them, and re-layouts: 2.95 us -> none
    another operation x3 -> x0, other arithmetic: 2.04 us -> none
    select_n x0 -> x1, other arithmetic: none -> 1.26 us  [on_device(): jnp.where(lane == 1, fork_pages[0, 0], fork_pages[0, 1])]
    all_to_all x2 -> x3, starting transfers between devices: 15.2 us -> 15.3 us  [the longest x1 7.1 us: on_device(): lax.all_to_all(jnp.broadcast_to(packed[None], (lax.axis_size('cy'),) + pa...]
  transfers between devices with their start and end apart: 4 -> 5, of which waited for: 3 -> 4; matrix products, arithmetic and copies ran while one was open for 5% -> 8% of each run, Pallas kernels for 0% -> 0%
where the time goes in v3:
time: 99 us; the launch traced here: 98 us
  waiting for transfers between devices  47.7 us (48%)
  starting transfers between devices  19.2 us (19%)
  other arithmetic  11.2 us (11%)
  matrix products  9.23 us (9%)
  local copies, waits for them, and re-layouts  9.17 us (9%)
  between operations  1.66 us (2%)
    all_to_all x1, waiting for transfers between devices, on_device(): arrived = lax.all_to_all(payload, ('cx', 'cy'), 0, 0, tiled=True)  28.6 us
    all_to_all x1, waiting for transfers between devices, on_device(): lax.all_to_all(jnp.broadcast_to(along_y[None], (lax.axis_size('cx'),) + a...  9.52 us
    all_to_all x1, waiting for transfers between devices, on_device(): lax.all_to_all(jnp.broadcast_to(packed[None], (lax.axis_size('cy'),) + pa...  8.84 us
    all_to_all x1, starting transfers between devices, on_device(): lax.all_to_all(jnp.broadcast_to(packed[None], (lax.axis_size('cy'),) + pa...  7.1 us
    dot_general x1, matrix products, masked_softmax(): jnp.einsum('gqk,tk->gqt', rows, keys, preferred_element_type=jnp.float32)  5.44 us
    all_to_all x1, starting transfers between devices, on_device(): lax.all_to_all(jnp.broadcast_to(along_y[None], (lax.axis_size('cx'),) + a...  4.29 us
    all_to_all x1, starting transfers between devices, on_device(): arrived = lax.all_to_all(payload, ('cx', 'cy'), 0, 0, tiled=True)  3.94 us
    ppermute x2, starting transfers between devices, on_device(): lax.ppermute((local_keys, suffix_len), 'core', [(0, 1), (1, 0)])  3.82 us
  transfers between devices with their start and end apart: 5, of which 4 were waited for; matrix products, arithmetic and copies ran while one was open for 8% of the time, Pallas kernels for 0%

profile of v3, /device:TPU:448, one launch (start us, length us, event | category | flops | bytes accessed | tf_op | source)
XLA Modules:
  0.0 98.0 jit_solution(18110922701190505234)
XLA Ops:
  0.0 1.3 %fusion.49 = (s32[1,1]{1,0:T(1,128)}, s32[1,1]{1,0:T(1,128)}) fusion(s32[1,2]{1,0:T(1,128)} %param.13), kind=kLoop, calls=%fused_computation.101 | loop fusion | bytes 16 | tf_op jit(solution)/shard_map/slice | solution.py:61
  2.0 0.9 reshape.384
  2.9 1.3 %compare_select_fusion = s32[128]{0:T(128)S(1)} fusion(s32[]{:T(128)} %bitcast.2, s32[]{:T(128)} %bitcast.1), kind=kLoop, calls=%fused_computation.82 | loop fusion | flops 256 | bytes 520 | tf_op jit(solution)/shard_map/jit(_where)/select_n | solution.py:61
  4.3 0.8 broadcast_in_dim.99
  5.0 7.1 %all-to-all-start = ((bf16[8,160,128]{2,1,0:T(8,128)(2,1)}), bf16[8,160,128]{2,1,0:T(8,128)(2,1)S(1)}, u32[]{:S(2)}, u32[]{:S(2)}) async-start(bf16[8,160,128]{2,1,0:T(8,128)(2,1)} %broadcast_in_dim.99), calls=%async_computation | async-start | bytes 655360 | tf_op jit(solution)/shard_map/all_to_all | solution.py:64
  12.1 1.3 %copy.30 = bf16[512,576]{0,1:T(8,128)(2,1)S(1)} copy(bf16[512,576]{1,0:T(8,128)(2,1)} %bitcast.98) | data formatting | bytes 1179648 | tf_op jit(solution)/shard_map/reshape | solution.py:74
  13.5 1.2 %pad_maximum_fusion.1 = bf16[1024,576]{0,1:T(8,128)(2,1)} fusion(bf16[512,576]{0,1:T(8,128)(2,1)S(1)} %copy.30, bf16[512,576]{0,1:T(8,128)(2,1)S(1)} %copy-done), kind=kLoop, calls=%fused_computation.14 | loop fusion | flops 2359296 | bytes 2359296 | tf_op jit(solution)/shard_map/concatenate | solution.py:75
  14.7 1.9 %collective-permute-start.1 = (bf16[1024,576]{0,1:T(8,128)(2,1)}, bf16[1024,576]{0,1:T(8,128)(2,1)}, u32[]{:S(2)}, u32[]{:S(2)}) collective-permute-start(bf16[1024,576]{0,1:T(8,128)(2,1)} %pad_maximum_fusion.1), channel_id=1, source_target_pairs={{0,8},{8,0},{1,9},{9,1},{2,10},{10,2},{3,11},{11,3},{4,12},{12,4},... | collective-permute-start | bytes 3538952 | tf_op jit(solution)/shard_map/ppermute | solution.py:76
  16.6 8.8 %all-to-all-done = bf16[8,160,128]{2,1,0:T(8,128)(2,1)S(1)} async-done(((bf16[8,160,128]{2,1,0:T(8,128)(2,1)}), bf16[8,160,128]{2,1,0:T(8,128)(2,1)S(1)}, u32[]{:S(2)}, u32[]{:S(2)}) %all-to-all-start) | async-done | bytes 327712 | tf_op jit(solution)/shard_map/all_to_all | solution.py:64
  25.4 1.3 %broadcast_in_dim.100 = bf16[4,8,160,128]{3,2,1,0:T(8,128)(2,1)} broadcast(bf16[8,160,128]{2,1,0:T(8,128)(2,1)S(1)} %all-to-all-done), dimensions={1,2,3} | broadcast | bytes 1638400 | tf_op jit(solution)/shard_map/broadcast_in_dim | solution.py:68
  26.7 4.3 %all-to-all-start.1 = ((bf16[4,8,160,128]{3,2,1,0:T(8,128)(2,1)}), bf16[4,8,160,128]{3,2,1,0:T(8,128)(2,1)S(1)}, u32[]{:S(2)}, u32[]{:S(2)}) async-start(bf16[4,8,160,128]{3,2,1,0:T(8,128)(2,1)} %broadcast_in_dim.100), calls=%async_computation.1 | async-start | bytes 2621440 | tf_op jit(solution)/shard_map/all_to_all | solution.py:67
  31.0 1.9 %collective-permute-start = (s32[1]{0:T(128)}, s32[1]{0:T(128)}, u32[]{:S(2)}, u32[]{:S(2)}) collective-permute-start(s32[1]{0:T(128)} %param.11), channel_id=1, source_target_pairs={{0,8},{8,0},{1,9},{9,1},{2,10},{10,2},{3,11},{11,3},{4,12},{12,4},... | collective-permute-start | bytes 20 | tf_op jit(solution)/shard_map/ppermute | solution.py:76
  33.6 0.7 collective-permute-done
  34.9 3.0 %pad_maximum_fusion = bf16[2048,576]{0,1:T(8,128)(2,1)} fusion(bf16[1024,576]{0,1:T(8,128)(2,1)} %collective-permute-done.1, bf16[512,576]{0,1:T(8,128)(2,1)S(1)} %copy.30, bf16[512,576]{0,1:T(8,128)(2,1)S(1)} %copy-done), kind=kLoop, calls=%fused_computation.7 | loop fusion | flops 7077888 | bytes 4718592 | tf_op jit(solution)/shard_map/concatenate | solution.py:77
  37.9 9.5 %all-to-all-done.1 = bf16[4,8,160,128]{3,2,1,0:T(8,128)(2,1)S(1)} async-done(((bf16[4,8,160,128]{3,2,1,0:T(8,128)(2,1)}), bf16[4,8,160,128]{3,2,1,0:T(8,128)(2,1)S(1)}, u32[]{:S(2)}, u32[]{:S(2)}) %all-to-all-start.1) | async-done | bytes 1310752 | tf_op jit(solution)/shard_map/all_to_all | solution.py:67
  47.9 2.0 %reshape.386 = bf16[32,32,576]{2,1,0:T(8,128)(2,1)} reshape(bf16[32,144,128]{2,1,0:T(8,128)(2,1)S(1)} %slice.73) | data formatting | bytes 2359296 | tf_op jit(solution)/shard_map/reshape | solution.py:70
  49.8 5.4 %select_reduce_fusion = (f32[32,32]{1,0:T(8,128)S(1)}, f32[32,32,2048]{2,1,0:T(8,128)S(1)}) fusion(pred[32,2048]{1,0:T(8,128)(4,1)S(1)} %broadcast_compare_fusion, bf16[32,32,576]{2,1,0:T(8,128)(2,1)} %reshape.386, bf16[1024,576]{0,1:T(8,128)(2,1)} %collective-permute-done.1, bf16[512,576]{0,1:T(8,128)(2,1)S(1)} %copy.30, bf16[512,576]{0,1:T(8,128)(2,1)S(1)} %copy-done.1), kind=kOutput, calls=%fused_computation.2 | convolution fusion | flops 2429287424 | bytes 11997184 | tf_op jit(solution)/shard_map/gqk,tk->gqt/dot_general | solution.py:16
  55.3 2.7 %multiply_reduce_fusion = f32[32,32]{1,0:T(8,128)S(1)} fusion(f32[32,32,2048]{2,1,0:T(8,128)S(1)} %get-tuple-element.25, f32[32,2048]{1,0:T(8,128)S(1)} %pad_maximum_fusion.4, f32[32,32]{1,0:T(8,128)S(1)} %get-tuple-element.24, pred[32,2048]{1,0:T(8,128)(4,1)S(1)} %broadcast_compare_fusion), kind=kLoop, calls=%fused_computation | loop fusion | flops 10484736 | bytes 8724480 | tf_op jit(solution)/shard_map/reduce_sum | solution.py:21
  58.0 2.5 %divide_convert_fusion = bf16[32,32,512]{2,1,0:T(8,128)(2,1)S(1)} fusion(f32[32,32]{1,0:T(8,128)S(1)} %multiply_reduce_fusion, bf16[2048,576]{0,1:T(8,128)(2,1)S(1)} %copy-done.2, f32[32,32,2048]{2,1,0:T(8,128)S(1)} %get-tuple-element.25, f32[32,32]{1,0:T(8,128)S(1)} %get-tuple-element.24, pred[32,2048]{1,0:T(8,128)(4,1)S(1)} %broadcast_compare_fusion, ...), kind=kOutput, calls=%fused_computation.12 | convolution fusion | flops 2159017984 | bytes 11763712 | tf_op jit(solution)/shard_map/gqt,td->gqd/dot_general | solution.py:23
  61.4 1.1 %pad_maximum_fusion.2 = bf16[32,144,128]{2,1,0:T(8,128)(2,1)} fusion(bf16[32,16,128]{2,1,0:T(8,128)(2,1)S(1)} %bitcast.101, bf16[32,128,128]{2,1,0:T(8,128)(2,1)S(1)} %reshape.388), kind=kLoop, calls=%fused_computation.15 | loop fusion | flops 2359296 | bytes 2359296 | tf_op jit(solution)/shard_map/concatenate | solution.py:100
  62.5 3.9 %all-to-all-start.2 = ((bf16[32,144,128]{2,1,0:T(8,128)(2,1)}), bf16[32,144,128]{2,1,0:T(8,128)(2,1)S(1)}, u32[]{:S(2)}, u32[]{:S(2)}) async-start(bf16[32,144,128]{2,1,0:T(8,128)(2,1)} %pad_maximum_fusion.2), calls=%async_computation.2 | async-start | bytes 2359296 | tf_op jit(solution)/shard_map/all_to_all | solution.py:101
  67.2 28.6 %all-to-all-done.2 = bf16[32,144,128]{2,1,0:T(8,128)(2,1)S(1)} async-done(((bf16[32,144,128]{2,1,0:T(8,128)(2,1)}), bf16[32,144,128]{2,1,0:T(8,128)(2,1)S(1)}, u32[]{:S(2)}, u32[]{:S(2)}) %all-to-all-start.2) | async-done | bytes 1179680 | tf_op jit(solution)/shard_map/all_to_all | solution.py:101
  96.4 0.7 multiply_reduce_fusion.1
  97.2 0.9 fusion.13
  (63 shorter events, 3.3 us)
Async XLA Ops:
  0.0 13.5 %copy-start = (bf16[512,576]{0,1:T(8,128)(2,1)S(1)}, bf16[512,576]{0,1:T(8,128)(2,1)}, u32[]{:S(2)}) copy-start(bf16[512,576]{0,1:T(8,128)(2,1)} %param.8) | copy-start | bytes 1769476
  5.0 20.4 %all-to-all-start = ((bf16[8,160,128]{2,1,0:T(8,128)(2,1)}), bf16[8,160,128]{2,1,0:T(8,128)(2,1)S(1)}, u32[]{:S(2)}, u32[]{:S(2)}) async-start(bf16[8,160,128]{2,1,0:T(8,128)(2,1)} %broadcast_in_dim.99), calls=%async_computation | async-start | bytes 655360 | tf_op jit(solution)/shard_map/all_to_all | solution.py:64
  14.7 20.2 %collective-permute-start.1 = (bf16[1024,576]{0,1:T(8,128)(2,1)}, bf16[1024,576]{0,1:T(8,128)(2,1)}, u32[]{:S(2)}, u32[]{:S(2)}) collective-permute-start(bf16[1024,576]{0,1:T(8,128)(2,1)} %pad_maximum_fusion.1), channel_id=1, source_target_pairs={{0,8},{8,0},{1,9},{9,1},{2,10},{10,2},{3,11},{11,3},{4,12},{12,4},... | collective-permute-start | bytes 3538952 | tf_op jit(solution)/shard_map/ppermute | solution.py:76
  26.7 20.7 %all-to-all-start.1 = ((bf16[4,8,160,128]{3,2,1,0:T(8,128)(2,1)}), bf16[4,8,160,128]{3,2,1,0:T(8,128)(2,1)S(1)}, u32[]{:S(2)}, u32[]{:S(2)}) async-start(bf16[4,8,160,128]{3,2,1,0:T(8,128)(2,1)} %broadcast_in_dim.100), calls=%async_computation.1 | async-start | bytes 2621440 | tf_op jit(solution)/shard_map/all_to_all | solution.py:67
  31.0 3.3 %collective-permute-start = (s32[1]{0:T(128)}, s32[1]{0:T(128)}, u32[]{:S(2)}, u32[]{:S(2)}) collective-permute-start(s32[1]{0:T(128)} %param.11), channel_id=1, source_target_pairs={{0,8},{8,0},{1,9},{9,1},{2,10},{10,2},{3,11},{11,3},{4,12},{12,4},... | collective-permute-start | bytes 20 | tf_op jit(solution)/shard_map/ppermute | solution.py:76
  47.5 2.3 %copy-start.1 = (bf16[512,576]{0,1:T(8,128)(2,1)S(1)}, bf16[512,576]{0,1:T(8,128)(2,1)}, u32[]{:S(2)}) copy-start(bf16[512,576]{0,1:T(8,128)(2,1)} %param.8) | copy-start | bytes 1769476
  55.3 2.7 %copy-start.2 = (bf16[2048,576]{0,1:T(8,128)(2,1)S(1)}, bf16[2048,576]{0,1:T(8,128)(2,1)}, u32[]{:S(2)}) copy-start(bf16[2048,576]{0,1:T(8,128)(2,1)} %pad_maximum_fusion) | copy-start | bytes 7077892
  61.4 5.1 %copy-start.3 = (bf16[1,8,64,576]{3,2,1,0:T(8,128)(2,1)S(1)}, bf16[1,8,64,576]{3,2,1,0:T(8,128)(2,1)}, u32[]{:S(2)}) copy-start(bf16[1,8,64,576]{3,2,1,0:T(8,128)(2,1)} %param.9) | copy-start | bytes 1769476
  61.4 5.1 %copy-start.4 = (bf16[2,1,16,576]{3,2,1,0:T(8,128)(2,1)S(1)}, bf16[2,1,16,576]{3,2,1,0:T(8,128)(2,1)}, u32[]{:S(2)}) copy-start(bf16[2,1,16,576]{3,2,1,0:T(8,128)(2,1)} %param.7) | copy-start | bytes 110596
  61.4 5.1 %copy-start.5 = (bf16[2,1,576]{2,0,1:T(2,128)(2,1)S(1)}, bf16[2,1,576]{2,0,1:T(2,128)(2,1)}, u32[]{:S(2)}) copy-start(bf16[2,1,576]{2,0,1:T(2,128)(2,1)} %param.10) | copy-start | bytes 6916
  62.5 33.3 %all-to-all-start.2 = ((bf16[32,144,128]{2,1,0:T(8,128)(2,1)}), bf16[32,144,128]{2,1,0:T(8,128)(2,1)S(1)}, u32[]{:S(2)}, u32[]{:S(2)}) async-start(bf16[32,144,128]{2,1,0:T(8,128)(2,1)} %pad_maximum_fusion.2), calls=%async_computation.2 | async-start | bytes 2359296 | tf_op jit(solution)/shard_map/all_to_all | solution.py:101

commit v4 on v3

--- a/solution.py
+++ b/solution.py
@@ -1,6 +1,10 @@
+import functools
+
 import jax
 import jax.numpy as jnp
 from jax import lax
+from jax.experimental import pallas as pl
+from jax.experimental.pallas import tpu as pltpu
 from jax.sharding import Mesh
 from jax.sharding import PartitionSpec as P
 
@@ -10,6 +14,62 @@
 
 score_scale = 192.0 ** (-0.5)
 neg_large = -1e30
+INTERPRET = False
+GROUP_BEAMS = 8
+
+
+def softmax_kernel(q_ref, k_ref, m_ref, out_ref, stat_ref):
+    groups, key_n = m_ref.shape
+    rows_n = q_ref.shape[0]
+    per = rows_n // groups
+    scores = lax.dot_general(
+        q_ref[...], k_ref[...], (((1,), (1,)), ((), ())), preferred_element_type=jnp.float32
+    ) * score_scale
+    m = jnp.broadcast_to(m_ref[...][:, None, :], (groups, per, key_n)).reshape(rows_n, key_n)
+    valid = m > 0
+    top = jnp.max(jnp.where(valid, scores, neg_large), axis=1, keepdims=True)
+    weights = jnp.where(valid, jnp.exp(scores - top), 0.0)
+    total = jnp.sum(weights * m, axis=1, keepdims=True)
+    rounded = weights.astype(jnp.bfloat16) * m.astype(jnp.bfloat16)
+    summed = jnp.dot(rounded, k_ref[:, :DL], preferred_element_type=jnp.float32)
+    out_ref[...] = (summed / total).astype(out_ref.dtype)
+    lane = lax.broadcasted_iota(jnp.int32, stat_ref.shape, 1)
+    stat_ref[...] = jnp.where(lane < LANES // 2, top, total)
+
+
+def fused_softmax(rows, keys, mult):
+    rows_n, width = rows.shape
+    key_n = keys.shape[0]
+    groups = mult.shape[0]
+    per = rows_n // groups
+    step_rows = GROUP_BEAMS * per
+    grid = (groups // GROUP_BEAMS,)
+    cost = pl.CostEstimate(
+        flops=2 * rows_n * key_n * (width + DL),
+        transcendentals=rows_n * key_n,
+        bytes_accessed=2 * (rows_n * width + key_n * width + rows_n * DL) + 4 * (groups * key_n + rows_n * LANES),
+    )
+    out, stat = pl.pallas_call(
+        softmax_kernel,
+        grid=grid,
+        in_specs=[
+            pl.BlockSpec((step_rows, width), lambda i: (i, 0)),
+            pl.BlockSpec((key_n, width), lambda i: (0, 0)),
+            pl.BlockSpec((GROUP_BEAMS, key_n), lambda i: (i, 0)),
+        ],
+        out_specs=[
+            pl.BlockSpec((step_rows, DL), lambda i: (i, 0)),
+            pl.BlockSpec((step_rows, LANES), lambda i: (i, 0)),
+        ],
+        out_shape=[
+            jax.ShapeDtypeStruct((rows_n, DL), jnp.bfloat16),
+            jax.ShapeDtypeStruct((rows_n, LANES), jnp.float32),
+        ],
+        compiler_params=pltpu.CompilerParams(vmem_limit_bytes=48 * 1024 * 1024),
+        cost_estimate=cost,
+        interpret=INTERPRET,
+    )(rows, keys, mult)
+    return out, stat[:, 0], stat[:, LANES // 2]
 
 
 def masked_softmax(rows, keys, mult):
@@ -90,8 +150,11 @@
     mult = jnp.concatenate(
         [ones, fork_count(my_beam, suffix_len[0]), ones, fork_count(partner_beam, partner_len[0])], axis=1
     )
-    top, total, summed = masked_softmax(rows, keys, mult)
-    out = (summed / total[..., None]).astype(jnp.bfloat16)
+    row_n = steps_n * head_dev
+    out, top, total = fused_softmax(rows.reshape(chips * row_n, width), keys, mult)
+    out = out.reshape(chips, row_n, DL)
+    top = top.reshape(chips, row_n)
+    total = total.reshape(chips, row_n)
 
     out_rows = out.reshape(chips, -1, LANES)
     parts = jnp.stack(split3(top) + split3(total), axis=1).reshape(chips, -1)
@@ -100,7 +163,6 @@
     payload = jnp.concatenate([out_rows, parts.reshape(chips, stat_rows, LANES)], axis=1)
     arrived = lax.all_to_all(payload, ("cx", "cy"), 0, 0, tiled=True)
     n_out = out_rows.shape[1]
-    row_n = steps_n * head_dev
     out_r = arrived[:, :n_out].reshape(chips, row_n, DL)
     got = arrived[:, n_out:].reshape(chips, -1)[:, : 6 * row_n].astype(jnp.float32).reshape(chips, 6, row_n)
     top_r = (got[:, 0] + got[:, 1]) + got[:, 2]

time: 99 us -> 106 us (1.071)
  local copies, waits for them, and re-layouts: 9.17 us -> 19.1 us
  Pallas kernels: 0 us -> 9.06 us
  matrix products: 9.23 us -> 1.29 us
  other arithmetic: 11.2 us -> 6.1 us
    pallas_call x0 -> x1, Pallas kernels: none -> 9.06 us  [fused_softmax(): pl.pallas_call(softmax_kernel, grid=grid, in_specs=[pl.BlockSpec((step_ro...]
    dot_general x2 -> x0, matrix products: 7.93 us -> none  [the longest x1 5.44 us: masked_softmax(): jnp.einsum('gqk,tk->gqt', rows, keys, preferred_element_type=jnp.float32)]
    another operation x0 -> x4, local copies, waits for them, and re-layouts: none -> 5.34 us  [the longest x1 3.5 us: on_device(): rows.reshape(chips * row_n, width)]
    reshape x3 -> x0, local copies, waits for them, and re-layouts: 3.94 us -> none  [the longest x1 1.95 us: on_device(): rows = gathered[:, :q_rows].reshape(chips, steps_n * head_dev, width)]
    reduce_sum x1 -> x0, other arithmetic: 2.66 us -> none  [masked_softmax(): total = jnp.sum(weights * m, axis=-1)]
    slice x1, local copies, waits for them, and re-layouts: 0.08 us -> 2.37 us  [on_device(): rows = gathered[:, :q_rows].reshape(chips, steps_n * head_dev, width)]
    unnamed x17 -> x20, local copies, waits for them, and re-layouts: 0.21 us -> 2.26 us
    concatenate x0 -> x1, local copies, waits for them, and re-layouts: none -> 1.48 us  [on_device(): local_keys = jnp.concatenate([prompt_cache, own_suffix], axis=0)]
  transfers between devices with their start and end apart: 5 -> 5, of which waited for: 4 -> 4; matrix products, arithmetic and copies ran while one was open for 8% -> 7% of each run, Pallas kernels for 0% -> 0%
where the time goes in v4:
time: 106 us; the launch traced here: 105 us
  waiting for transfers between devices  48.4 us (46%)
  starting transfers between devices  19.3 us (18%)
  local copies, waits for them, and re-layouts  19.1 us (18%)
  Pallas kernels  9.06 us (9%)
  other arithmetic  6.1 us (6%)
  between operations  1.62 us (2%)
  matrix products  1.29 us (1%)
    all_to_all x1, waiting for transfers between devices, on_device(): arrived = lax.all_to_all(payload, ('cx', 'cy'), 0, 0, tiled=True)  28.6 us
    all_to_all x1, waiting for transfers between devices, on_device(): lax.all_to_all(jnp.broadcast_to(along_y[None], (lax.axis_size('cx'),) + a...  9.81 us
    all_to_all x1, waiting for transfers between devices, on_device(): lax.all_to_all(jnp.broadcast_to(packed[None], (lax.axis_size('cy'),) + pa...  9.44 us
    pallas_call x1, Pallas kernels, fused_softmax(): pl.pallas_call(softmax_kernel, grid=grid, in_specs=[pl.BlockSpec((step_ro...  9.06 us
    all_to_all x1, starting transfers between devices, on_device(): lax.all_to_all(jnp.broadcast_to(packed[None], (lax.axis_size('cy'),) + pa...  7.1 us
    all_to_all x1, starting transfers between devices, on_device(): lax.all_to_all(jnp.broadcast_to(along_y[None], (lax.axis_size('cx'),) + a...  4.29 us
    all_to_all x1, starting transfers between devices, on_device(): arrived = lax.all_to_all(payload, ('cx', 'cy'), 0, 0, tiled=True)  4.07 us
    ppermute x2, starting transfers between devices, on_device(): lax.ppermute((local_keys, suffix_len), 'core', [(0, 1), (1, 0)])  3.83 us
  transfers between devices with their start and end apart: 5, of which 4 were waited for; matrix products, arithmetic and copies ran while one was open for 7% of the time, Pallas kernels for 0%

profile of v4, /device:TPU:448, one launch (start us, length us, event | category | flops | bytes accessed | tf_op | source)
XLA Modules:
  0.0 105.0 jit_solution(6662766568413944278)
XLA Ops:
  0.0 1.3 %fusion.36 = (s32[1,1]{1,0:T(1,128)}, s32[1,1]{1,0:T(1,128)}) fusion(s32[1,2]{1,0:T(1,128)} %param.13), kind=kLoop, calls=%fused_computation.87 | loop fusion | bytes 16 | tf_op jit(solution)/shard_map/slice | solution.py:121
  2.0 0.9 reshape.257
  2.9 1.2 %compare_select_fusion = s32[128]{0:T(128)S(1)} fusion(s32[]{:T(128)} %bitcast.2, s32[]{:T(128)} %bitcast.1), kind=kLoop, calls=%fused_computation.71 | loop fusion | flops 256 | bytes 520 | tf_op jit(solution)/shard_map/jit(_where)/select_n | solution.py:121
  4.2 0.8 broadcast_in_dim.77
  5.0 7.1 %all-to-all-start = ((bf16[8,160,128]{2,1,0:T(8,128)(2,1)}), bf16[8,160,128]{2,1,0:T(8,128)(2,1)S(1)}, u32[]{:S(2)}, u32[]{:S(2)}) async-start(bf16[8,160,128]{2,1,0:T(8,128)(2,1)} %broadcast_in_dim.77), calls=%async_computation | async-start | bytes 655360 | tf_op jit(solution)/shard_map/all_to_all | solution.py:124
  12.5 1.5 %copy.38 = bf16[1024,576]{0,1:T(8,128)(2,1)} copy(bf16[1024,576]{1,0:T(8,128)(2,1)S(1)} %pad_maximum_fusion.1) | data formatting | bytes 2359296 | tf_op jit(solution)/shard_map/concatenate | solution.py:135
  14.0 1.9 %collective-permute-start = (bf16[1024,576]{0,1:T(8,128)(2,1)}, bf16[1024,576]{0,1:T(8,128)(2,1)S(1)}, u32[]{:S(2)}, u32[]{:S(2)}) collective-permute-start(bf16[1024,576]{0,1:T(8,128)(2,1)} %copy.38), channel_id=1, source_target_pairs={{0,8},{8,0},{1,9},{9,1},{2,10},{10,2},{3,11},{11,3},{4,12},{12,4},... | collective-permute-start | bytes 3538952 | tf_op jit(solution)/shard_map/ppermute | solution.py:136
  15.9 9.4 %all-to-all-done = bf16[8,160,128]{2,1,0:T(8,128)(2,1)S(1)} async-done(((bf16[8,160,128]{2,1,0:T(8,128)(2,1)}), bf16[8,160,128]{2,1,0:T(8,128)(2,1)S(1)}, u32[]{:S(2)}, u32[]{:S(2)}) %all-to-all-start) | async-done | bytes 327712 | tf_op jit(solution)/shard_map/all_to_all | solution.py:124
  25.4 1.3 %broadcast_in_dim.78 = bf16[4,8,160,128]{3,2,1,0:T(8,128)(2,1)} broadcast(bf16[8,160,128]{2,1,0:T(8,128)(2,1)S(1)} %all-to-all-done), dimensions={1,2,3} | broadcast | bytes 1638400 | tf_op jit(solution)/shard_map/broadcast_in_dim | solution.py:128
  26.6 4.3 %all-to-all-start.1 = ((bf16[4,8,160,128]{3,2,1,0:T(8,128)(2,1)}), bf16[4,8,160,128]{3,2,1,0:T(8,128)(2,1)}, u32[]{:S(2)}, u32[]{:S(2)}) async-start(bf16[4,8,160,128]{3,2,1,0:T(8,128)(2,1)} %broadcast_in_dim.78), calls=%async_computation.1 | async-start | bytes 2621440 | tf_op jit(solution)/shard_map/all_to_all | solution.py:127
  30.9 1.9 %collective-permute-start.1 = (s32[1]{0:T(128)}, s32[1]{0:T(128)}, u32[]{:S(2)}, u32[]{:S(2)}) collective-permute-start(s32[1]{0:T(128)} %param.11), channel_id=1, source_target_pairs={{0,8},{8,0},{1,9},{9,1},{2,10},{10,2},{3,11},{11,3},{4,12},{12,4},... | collective-permute-start | bytes 20 | tf_op jit(solution)/shard_map/ppermute | solution.py:136
  34.7 1.4 %copy.40 = bf16[1024,576]{1,0:T(8,128)(2,1)} copy(bf16[1024,576]{0,1:T(8,128)(2,1)S(1)} %collective-permute-done) | data formatting | bytes 2359296 | tf_op jit(solution)/shard_map/ppermute | solution.py:136
  36.2 1.7 %pad_maximum_fusion.k_ref = bf16[2048,576]{1,0:T(8,128)(2,1)S(1)} fusion(bf16[1024,576]{1,0:T(8,128)(2,1)} %copy.40, bf16[512,576]{1,0:T(8,128)(2,1)} %bitcast.59, bf16[512,576]{1,0:T(8,128)(2,1)S(1)} %copy.39), kind=kLoop, calls=%fused_computation | loop fusion | flops 7077888 | bytes 4718592 | tf_op jit(solution)/shard_map/concatenate | solution.py:137
  37.9 9.8 %all-to-all-done.1 = bf16[4,8,160,128]{3,2,1,0:T(8,128)(2,1)} async-done(((bf16[4,8,160,128]{3,2,1,0:T(8,128)(2,1)}), bf16[4,8,160,128]{3,2,1,0:T(8,128)(2,1)}, u32[]{:S(2)}, u32[]{:S(2)}) %all-to-all-start.1) | async-done | bytes 1310752 | tf_op jit(solution)/shard_map/all_to_all | solution.py:127
  47.7 0.9 slice.77
  48.6 2.4 %slice.76 = bf16[32,144,128]{2,1,0:T(8,128)(2,1)} slice(bf16[32,160,128]{2,1,0:T(8,128)(2,1)} %bitcast.3), slice={[0:32], [0:144], [0:128]} | slice | bytes 2359296 | tf_op jit(solution)/shard_map/slice | solution.py:130
  51.0 3.5 %reshape_reshape.6.q_ref = bf16[1024,576]{1,0:T(8,128)(2,1)} reshape(bf16[32,144,128]{2,1,0:T(8,128)(2,1)} %slice.76) | data formatting | bytes 2359296 | tf_op jit(solution)/shard_map/reshape;reshape | solution.py:154
  54.7 1.3 %copy-done = bf16[1024,576]{1,0:T(8,128)(2,1)S(1)} copy-done((bf16[1024,576]{1,0:T(8,128)(2,1)S(1)}, bf16[1024,576]{1,0:T(8,128)(2,1)}, u32[]{:S(2)}) %copy-start) | copy-done | bytes 1179672
  56.0 9.1 %shard_map.73 = (bf16[1024,512]{1,0:T(8,128)(2,1)S(1)}, f32[1024,128]{1,0:T(8,128)S(1)}) custom-call(bf16[1024,576]{1,0:T(8,128)(2,1)S(1)} %copy-done, bf16[2048,576]{1,0:T(8,128)(2,1)S(1)} %pad_maximum_fusion.k_ref, f32[32,2048]{1,0:T(8,128)S(1)} %pad_maximum_fusion.4.m_ref), custom_call_target="tpu_custom_call" | custom-call | flops 4563402752 | bytes 5373952 | tf_op jit(solution)/shard_map/pallas_call | solution.py:52
  66.5 1.7 %reshape_reshape.7 = bf16[32,128,128]{2,1,0:T(8,128)(2,1)S(1)} reshape(bf16[1024,512]{1,0:T(8,128)(2,1)} %copy-done.1) | data formatting | bytes 2097152 | tf_op jit(solution)/shard_map/reshape;reshape | solution.py:159
  68.2 1.1 %pad_maximum_fusion.2 = bf16[32,144,128]{2,1,0:T(8,128)(2,1)} fusion(bf16[32,16,128]{2,1,0:T(8,128)(2,1)S(1)} %bitcast.63, bf16[32,128,128]{2,1,0:T(8,128)(2,1)S(1)} %reshape_reshape.7), kind=kLoop, calls=%fused_computation.3 | loop fusion | flops 2359296 | bytes 2359296 | tf_op jit(solution)/shard_map/concatenate | solution.py:163
  69.3 4.1 %all-to-all-start.2 = ((bf16[32,144,128]{2,1,0:T(8,128)(2,1)}), bf16[32,144,128]{2,1,0:T(8,128)(2,1)S(1)}, u32[]{:S(2)}, u32[]{:S(2)}) async-start(bf16[32,144,128]{2,1,0:T(8,128)(2,1)} %pad_maximum_fusion.2), calls=%async_computation.2 | async-start | bytes 2359296 | tf_op jit(solution)/shard_map/all_to_all | solution.py:164
  74.1 28.6 %all-to-all-done.2 = bf16[32,144,128]{2,1,0:T(8,128)(2,1)S(1)} async-done(((bf16[32,144,128]{2,1,0:T(8,128)(2,1)}), bf16[32,144,128]{2,1,0:T(8,128)(2,1)S(1)}, u32[]{:S(2)}, u32[]{:S(2)}) %all-to-all-start.2) | async-done | bytes 1179680 | tf_op jit(solution)/shard_map/all_to_all | solution.py:164
  104.1 0.9 fusion.5
  (66 shorter events, 5.3 us)
Async XLA Ops:
  0.0 12.1 %copy-start.4 = (bf16[512,576]{0,1:T(8,128)(2,1)S(1)}, bf16[512,576]{0,1:T(8,128)(2,1)}, u32[]{:S(2)}) copy-start(bf16[512,576]{0,1:T(8,128)(2,1)} %param.8) | copy-start | bytes 1769476
  0.0 12.4 %copy-start.2 = (bf16[1,8,64,576]{3,2,1,0:T(8,128)(2,1)S(1)}, bf16[1,8,64,576]{3,2,1,0:T(8,128)(2,1)}, u32[]{:S(2)}) copy-start(bf16[1,8,64,576]{3,2,1,0:T(8,128)(2,1)} %param.9) | copy-start | bytes 1769476
  5.0 20.4 %all-to-all-start = ((bf16[8,160,128]{2,1,0:T(8,128)(2,1)}), bf16[8,160,128]{2,1,0:T(8,128)(2,1)S(1)}, u32[]{:S(2)}, u32[]{:S(2)}) async-start(bf16[8,160,128]{2,1,0:T(8,128)(2,1)} %broadcast_in_dim.77), calls=%async_computation | async-start | bytes 655360 | tf_op jit(solution)/shard_map/all_to_all | solution.py:124
  14.0 20.7 %collective-permute-start = (bf16[1024,576]{0,1:T(8,128)(2,1)}, bf16[1024,576]{0,1:T(8,128)(2,1)S(1)}, u32[]{:S(2)}, u32[]{:S(2)}) collective-permute-start(bf16[1024,576]{0,1:T(8,128)(2,1)} %copy.38), channel_id=1, source_target_pairs={{0,8},{8,0},{1,9},{9,1},{2,10},{10,2},{3,11},{11,3},{4,12},{12,4},... | collective-permute-start | bytes 3538952 | tf_op jit(solution)/shard_map/ppermute | solution.py:136
  26.6 21.1 %all-to-all-start.1 = ((bf16[4,8,160,128]{3,2,1,0:T(8,128)(2,1)}), bf16[4,8,160,128]{3,2,1,0:T(8,128)(2,1)}, u32[]{:S(2)}, u32[]{:S(2)}) async-start(bf16[4,8,160,128]{3,2,1,0:T(8,128)(2,1)} %broadcast_in_dim.78), calls=%async_computation.1 | async-start | bytes 2621440 | tf_op jit(solution)/shard_map/all_to_all | solution.py:127
  30.9 3.2 %collective-permute-start.1 = (s32[1]{0:T(128)}, s32[1]{0:T(128)}, u32[]{:S(2)}, u32[]{:S(2)}) collective-permute-start(s32[1]{0:T(128)} %param.11), channel_id=1, source_target_pairs={{0,8},{8,0},{1,9},{9,1},{2,10},{10,2},{3,11},{11,3},{4,12},{12,4},... | collective-permute-start | bytes 20 | tf_op jit(solution)/shard_map/ppermute | solution.py:136
  54.7 1.3 %copy-start = (bf16[1024,576]{1,0:T(8,128)(2,1)S(1)}, bf16[1024,576]{1,0:T(8,128)(2,1)}, u32[]{:S(2)}) copy-start(bf16[1024,576]{1,0:T(8,128)(2,1)} %reshape_reshape.6.q_ref) | copy-start | bytes 3538948
  65.1 1.0 copy-start.1
  69.3 4.1 %copy-start.3 = (bf16[1,8,64,576]{3,2,1,0:T(8,128)(2,1)S(1)}, bf16[1,8,64,576]{3,2,1,0:T(8,128)(2,1)}, u32[]{:S(2)}) copy-start(bf16[1,8,64,576]{3,2,1,0:T(8,128)(2,1)} %param.9) | copy-start | bytes 1769476
  69.3 4.1 %copy-start.5 = (bf16[2,1,16,576]{3,2,1,0:T(8,128)(2,1)S(1)}, bf16[2,1,16,576]{3,2,1,0:T(8,128)(2,1)}, u32[]{:S(2)}) copy-start(bf16[2,1,16,576]{3,2,1,0:T(8,128)(2,1)} %param.7) | copy-start | bytes 110596
  69.3 4.1 %copy-start.6 = (bf16[2,1,576]{2,0,1:T(2,128)(2,1)S(1)}, bf16[2,1,576]{2,0,1:T(2,128)(2,1)}, u32[]{:S(2)}) copy-start(bf16[2,1,576]{2,0,1:T(2,128)(2,1)} %param.10) | copy-start | bytes 6916
  69.3 33.5 %all-to-all-start.2 = ((bf16[32,144,128]{2,1,0:T(8,128)(2,1)}), bf16[32,144,128]{2,1,0:T(8,128)(2,1)S(1)}, u32[]{:S(2)}, u32[]{:S(2)}) async-start(bf16[32,144,128]{2,1,0:T(8,128)(2,1)} %pad_maximum_fusion.2), calls=%async_computation.2 | async-start | bytes 2359296 | tf_op jit(solution)/shard_map/all_to_all | solution.py:164

commit v5 on v3

--- a/solution.py
+++ b/solution.py
@@ -30,6 +30,25 @@
     mid = lax.reduce_precision(rest, exponent_bits=8, mantissa_bits=7)
     lo = lax.reduce_precision(rest - mid, exponent_bits=8, mantissa_bits=7)
     return [hi.astype(jnp.bfloat16), mid.astype(jnp.bfloat16), lo.astype(jnp.bfloat16)]
+
+
+def pack_partials(out, top, total):
+    n = out.shape[0]
+    out_rows = out.reshape(n, -1, LANES)
+    parts = jnp.stack(split3(top) + split3(total), axis=1).reshape(n, -1)
+    stat_rows = -(-parts.shape[1] // (META_ROWS * LANES)) * META_ROWS
+    parts = jnp.pad(parts, ((0, 0), (0, stat_rows * LANES - parts.shape[1])))
+    return jnp.concatenate([out_rows, parts.reshape(n, stat_rows, LANES)], axis=1)
+
+
+def unpack_partials(arrived, row_n):
+    n = arrived.shape[0]
+    n_out = row_n * DL // LANES
+    out = arrived[:, :n_out].reshape(n, row_n, DL).astype(jnp.float32)
+    got = arrived[:, n_out:].reshape(n, -1)[:, : 6 * row_n].astype(jnp.float32).reshape(n, 6, row_n)
+    top = (got[:, 0] + got[:, 1]) + got[:, 2]
+    total = (got[:, 3] + got[:, 4]) + got[:, 5]
+    return out, top, total
 
 
 def own_partial(queries, keys, valid):
@@ -93,18 +112,20 @@
     top, total, summed = masked_softmax(rows, keys, mult)
     out = (summed / total[..., None]).astype(jnp.bfloat16)
 
-    out_rows = out.reshape(chips, -1, LANES)
-    parts = jnp.stack(split3(top) + split3(total), axis=1).reshape(chips, -1)
-    stat_rows = -(-parts.shape[1] // (META_ROWS * LANES)) * META_ROWS
-    parts = jnp.pad(parts, ((0, 0), (0, stat_rows * LANES - parts.shape[1])))
-    payload = jnp.concatenate([out_rows, parts.reshape(chips, stat_rows, LANES)], axis=1)
-    arrived = lax.all_to_all(payload, ("cx", "cy"), 0, 0, tiled=True)
-    n_out = out_rows.shape[1]
+    x_n, y_n = lax.axis_size("cx"), lax.axis_size("cy")
     row_n = steps_n * head_dev
-    out_r = arrived[:, :n_out].reshape(chips, row_n, DL)
-    got = arrived[:, n_out:].reshape(chips, -1)[:, : 6 * row_n].astype(jnp.float32).reshape(chips, 6, row_n)
-    top_r = (got[:, 0] + got[:, 1]) + got[:, 2]
-    total_r = (got[:, 3] + got[:, 4]) + got[:, 5]
+    payload = pack_partials(out, top, total)
+    arrived = lax.all_to_all(payload.reshape(x_n, -1, LANES), "cx", 0, 0, tiled=True)
+    out_x, top_x, total_x = unpack_partials(arrived.reshape(x_n * y_n, -1, LANES), row_n)
+    out_x = out_x.reshape(x_n, y_n, row_n, DL)
+    top_x = top_x.reshape(x_n, y_n, row_n)
+    total_x = total_x.reshape(x_n, y_n, row_n)
+    top_m = jnp.max(top_x, axis=0)
+    weight_x = total_x * jnp.exp(top_x - top_m[None])
+    total_m = jnp.sum(weight_x, axis=0)
+    out_m = jnp.sum(weight_x[..., None] * out_x, axis=0) / total_m[..., None]
+    arrived = lax.all_to_all(pack_partials(out_m.astype(jnp.bfloat16), top_m, total_m), "cy", 0, 0, tiled=True)
+    out_r, top_r, total_r = unpack_partials(arrived, row_n)
 
     own_keys = jnp.concatenate([own_suffix, new_latent[:, 0, :]], axis=0)
     old_valid = jnp.broadcast_to((position < suffix_len[0])[None, :], (steps_n, suffix_n))
@@ -119,7 +140,7 @@
     weight_r = total_r * jnp.exp(top_r - peak[None])
     weight_l = jnp.exp(top_l - peak)
     denom = jnp.sum(weight_r, axis=0) + total_l * weight_l
-    numer = jnp.sum(weight_r[..., None] * out_r.astype(jnp.float32), axis=0) + weight_l[:, None] * summed_l
+    numer = jnp.sum(weight_r[..., None] * out_r, axis=0) + weight_l[:, None] * summed_l
     result = (numer / denom[:, None]).astype(jnp.bfloat16)
     return result.reshape(steps_n, 1, head_dev, DL)
 

time: 99 us -> 102 us (1.030)
  waiting for transfers between devices: 47.7 us -> 43.3 us
  starting transfers between devices: 19.2 us -> 22.3 us
  other arithmetic: 11.2 us -> 13.7 us
  local copies, waits for them, and re-layouts: 9.17 us -> 11.3 us
    all_to_all x1 -> x2, waiting for transfers between devices: 28.6 us -> 24.2 us  [the longest x1 14.1 us: on_device(): lax.all_to_all(payload.reshape(x_n, -1, LANES), 'cx', 0, 0, tiled=True)]
    all_to_all x1 -> x2, starting transfers between devices: 3.94 us -> 7.12 us  [the longest x1 3.6 us: on_device(): lax.all_to_all(pack_partials(out_m.astype(jnp.bfloat16), top_m, total_m),...]
    convert_element_type x0 -> x2, other arithmetic: none -> 1.8 us  [the longest x1 1.59 us: unpack_partials(): out = arrived[:, :n_out].reshape(n, row_n, DL).astype(jnp.float32)]
    convert_element_type x0 -> x1, local copies, waits for them, and re-layouts: none -> 1.74 us  [unpack_partials(): out = arrived[:, :n_out].reshape(n, row_n, DL).astype(jnp.float32)]
  transfers between devices with their start and end apart: 5 -> 6, of which waited for: 4 -> 5; matrix products, arithmetic and copies ran while one was open for 8% -> 8% of each run, Pallas kernels for 0% -> 0%
where the time goes in v5:
time: 102 us
  waiting for transfers between devices  43.3 us (42%)
  starting transfers between devices  22.3 us (22%)
  other arithmetic  13.7 us (13%)
  local copies, waits for them, and re-layouts  11.3 us (11%)
  matrix products  9.23 us (9%)
  between operations  1.74 us (2%)
    all_to_all x1, waiting for transfers between devices, on_device(): lax.all_to_all(payload.reshape(x_n, -1, LANES), 'cx', 0, 0, tiled=True)  14.1 us
    all_to_all x1, waiting for transfers between devices, on_device(): lax.all_to_all(pack_partials(out_m.astype(jnp.bfloat16), top_m, total_m),...  10.1 us
    all_to_all x1, waiting for transfers between devices, on_device(): lax.all_to_all(jnp.broadcast_to(along_y[None], (lax.axis_size('cx'),) + a...  9.63 us
    all_to_all x1, waiting for transfers between devices, on_device(): lax.all_to_all(jnp.broadcast_to(packed[None], (lax.axis_size('cy'),) + pa...  8.85 us
    all_to_all x1, starting transfers between devices, on_device(): lax.all_to_all(jnp.broadcast_to(packed[None], (lax.axis_size('cy'),) + pa...  7.1 us
    dot_general x1, matrix products, masked_softmax(): jnp.einsum('gqk,tk->gqt', rows, keys, preferred_element_type=jnp.float32)  5.44 us
    all_to_all x1, starting transfers between devices, on_device(): lax.all_to_all(jnp.broadcast_to(along_y[None], (lax.axis_size('cx'),) + a...  4.29 us
    ppermute x2, starting transfers between devices, on_device(): lax.ppermute((local_keys, suffix_len), 'core', [(0, 1), (1, 0)])  3.82 us
  transfers between devices with their start and end apart: 6, of which 5 were waited for; matrix products, arithmetic and copies ran while one was open for 8% of the time, Pallas kernels for 0%

profile of v5, /device:TPU:448, one launch (start us, length us, event | category | flops | bytes accessed | tf_op | source)
XLA Modules:
  0.0 101.6 jit_solution(8057275118546968482)
XLA Ops:
  0.0 1.4 %fusion.57 = (s32[1,1]{1,0:T(1,128)}, s32[1,1]{1,0:T(1,128)}) fusion(s32[1,2]{1,0:T(1,128)} %param.13), kind=kLoop, calls=%fused_computation.137 | loop fusion | bytes 16 | tf_op jit(solution)/shard_map/slice | solution.py:80
  2.1 0.9 reshape.534
  3.0 1.3 %compare_select_fusion = s32[128]{0:T(128)S(1)} fusion(s32[]{:T(128)} %bitcast.2, s32[]{:T(128)} %bitcast.1), kind=kLoop, calls=%fused_computation.117 | loop fusion | flops 256 | bytes 520 | tf_op jit(solution)/shard_map/jit(_where)/select_n | solution.py:80
  5.2 7.1 %all-to-all-start = ((bf16[8,160,128]{2,1,0:T(8,128)(2,1)}), bf16[8,160,128]{2,1,0:T(8,128)(2,1)S(1)}, u32[]{:S(2)}, u32[]{:S(2)}) async-start(bf16[8,160,128]{2,1,0:T(8,128)(2,1)} %broadcast_in_dim.102), calls=%async_computation | async-start | bytes 655360 | tf_op jit(solution)/shard_map/all_to_all | solution.py:83
  12.3 1.3 %copy.42 = bf16[512,576]{0,1:T(8,128)(2,1)S(1)} copy(bf16[512,576]{1,0:T(8,128)(2,1)} %bitcast.151) | data formatting | bytes 1179648 | tf_op jit(solution)/shard_map/reshape | solution.py:93
  13.6 1.2 %pad_maximum_fusion.1 = bf16[1024,576]{0,1:T(8,128)(2,1)} fusion(bf16[512,576]{0,1:T(8,128)(2,1)S(1)} %copy.42, bf16[512,576]{0,1:T(8,128)(2,1)S(1)} %copy-done), kind=kLoop, calls=%fused_computation.14 | loop fusion | flops 2359296 | bytes 2359296 | tf_op jit(solution)/shard_map/concatenate | solution.py:94
  14.8 1.9 %collective-permute-start.1 = (bf16[1024,576]{0,1:T(8,128)(2,1)}, bf16[1024,576]{0,1:T(8,128)(2,1)}, u32[]{:S(2)}, u32[]{:S(2)}) collective-permute-start(bf16[1024,576]{0,1:T(8,128)(2,1)} %pad_maximum_fusion.1), channel_id=1, source_target_pairs={{0,8},{8,0},{1,9},{9,1},{2,10},{10,2},{3,11},{11,3},{4,12},{12,4},... | collective-permute-start | bytes 3538952 | tf_op jit(solution)/shard_map/ppermute | solution.py:95
  16.7 8.9 %all-to-all-done = bf16[8,160,128]{2,1,0:T(8,128)(2,1)S(1)} async-done(((bf16[8,160,128]{2,1,0:T(8,128)(2,1)}), bf16[8,160,128]{2,1,0:T(8,128)(2,1)S(1)}, u32[]{:S(2)}, u32[]{:S(2)}) %all-to-all-start) | async-done | bytes 327712 | tf_op jit(solution)/shard_map/all_to_all | solution.py:83
  25.6 1.3 %broadcast_in_dim.103 = bf16[4,8,160,128]{3,2,1,0:T(8,128)(2,1)} broadcast(bf16[8,160,128]{2,1,0:T(8,128)(2,1)S(1)} %all-to-all-done), dimensions={1,2,3} | broadcast | bytes 1638400 | tf_op jit(solution)/shard_map/broadcast_in_dim | solution.py:87
  26.8 4.3 %all-to-all-start.1 = ((bf16[4,8,160,128]{3,2,1,0:T(8,128)(2,1)}), bf16[4,8,160,128]{3,2,1,0:T(8,128)(2,1)S(1)}, u32[]{:S(2)}, u32[]{:S(2)}) async-start(bf16[4,8,160,128]{3,2,1,0:T(8,128)(2,1)} %broadcast_in_dim.103), calls=%async_computation.1 | async-start | bytes 2621440 | tf_op jit(solution)/shard_map/all_to_all | solution.py:86
  31.1 1.9 %collective-permute-start = (s32[1]{0:T(128)}, s32[1]{0:T(128)}, u32[]{:S(2)}, u32[]{:S(2)}) collective-permute-start(s32[1]{0:T(128)} %param.11), channel_id=1, source_target_pairs={{0,8},{8,0},{1,9},{9,1},{2,10},{10,2},{3,11},{11,3},{4,12},{12,4},... | collective-permute-start | bytes 20 | tf_op jit(solution)/shard_map/ppermute | solution.py:95
  34.9 3.0 %pad_maximum_fusion = bf16[2048,576]{0,1:T(8,128)(2,1)} fusion(bf16[1024,576]{0,1:T(8,128)(2,1)} %collective-permute-done.1, bf16[512,576]{0,1:T(8,128)(2,1)S(1)} %copy.42, bf16[512,576]{0,1:T(8,128)(2,1)S(1)} %copy-done), kind=kLoop, calls=%fused_computation.7 | loop fusion | flops 7077888 | bytes 4718592 | tf_op jit(solution)/shard_map/concatenate | solution.py:96
  37.9 9.6 %all-to-all-done.1 = bf16[4,8,160,128]{3,2,1,0:T(8,128)(2,1)S(1)} async-done(((bf16[4,8,160,128]{3,2,1,0:T(8,128)(2,1)}), bf16[4,8,160,128]{3,2,1,0:T(8,128)(2,1)S(1)}, u32[]{:S(2)}, u32[]{:S(2)}) %all-to-all-start.1) | async-done | bytes 1310752 | tf_op jit(solution)/shard_map/all_to_all | solution.py:86
  48.0 1.9 %reshape.536 = bf16[32,32,576]{2,1,0:T(8,128)(2,1)} reshape(bf16[32,144,128]{2,1,0:T(8,128)(2,1)S(1)} %slice.109) | data formatting | bytes 2359296 | tf_op jit(solution)/shard_map/reshape | solution.py:89
  50.0 5.4 %select_reduce_fusion = (f32[32,32]{1,0:T(8,128)S(1)}, f32[32,32,2048]{2,1,0:T(8,128)S(1)}) fusion(pred[32,2048]{1,0:T(8,128)(4,1)S(1)} %broadcast_compare_fusion, bf16[32,32,576]{2,1,0:T(8,128)(2,1)} %reshape.536, bf16[1024,576]{0,1:T(8,128)(2,1)} %collective-permute-done.1, bf16[512,576]{0,1:T(8,128)(2,1)S(1)} %copy.42, bf16[512,576]{0,1:T(8,128)(2,1)S(1)} %copy-done.1), kind=kOutput, calls=%fused_computation.2 | convolution fusion | flops 2429287424 | bytes 11997184 | tf_op jit(solution)/shard_map/gqk,tk->gqt/dot_general | solution.py:16
  55.4 2.7 %multiply_reduce_fusion = f32[32,32]{1,0:T(8,128)S(1)} fusion(f32[32,32,2048]{2,1,0:T(8,128)S(1)} %get-tuple-element.29, f32[32,2048]{1,0:T(8,128)S(1)} %pad_maximum_fusion.5, f32[32,32]{1,0:T(8,128)S(1)} %get-tuple-element.28, pred[32,2048]{1,0:T(8,128)(4,1)S(1)} %broadcast_compare_fusion), kind=kLoop, calls=%fused_computation | loop fusion | flops 10484736 | bytes 8724480 | tf_op jit(solution)/shard_map/reduce_sum | solution.py:21
  58.1 2.5 %divide_convert_fusion = bf16[32,32,512]{2,1,0:T(8,128)(2,1)S(1)} fusion(f32[32,32]{1,0:T(8,128)S(1)} %multiply_reduce_fusion, bf16[2048,576]{0,1:T(8,128)(2,1)S(1)} %copy-done.2, f32[32,32,2048]{2,1,0:T(8,128)S(1)} %get-tuple-element.29, f32[32,32]{1,0:T(8,128)S(1)} %get-tuple-element.28, pred[32,2048]{1,0:T(8,128)(4,1)S(1)} %broadcast_compare_fusion, ...), kind=kOutput, calls=%fused_computation.12 | convolution fusion | flops 2159017984 | bytes 11763712 | tf_op jit(solution)/shard_map/gqt,td->gqd/dot_general | solution.py:23
  61.5 1.1 %pad_maximum_fusion.2 = bf16[32,144,128]{2,1,0:T(8,128)(2,1)} fusion(bf16[32,16,128]{2,1,0:T(8,128)(2,1)S(1)} %bitcast.154, bf16[32,128,128]{2,1,0:T(8,128)(2,1)S(1)} %reshape.538), kind=kLoop, calls=%fused_computation.15 | loop fusion | flops 2359296 | bytes 2359296 | tf_op jit(solution)/shard_map/concatenate | solution.py:41
  62.6 3.5 %all-to-all-start.2 = ((bf16[4,1152,128]{2,1,0:T(8,128)(2,1)}), bf16[4,1152,128]{2,1,0:T(8,128)(2,1)S(1)}, u32[]{:S(2)}, u32[]{:S(2)}) async-start(bf16[4,1152,128]{2,1,0:T(8,128)(2,1)} %bitcast.15), calls=%async_computation.2 | async-start | bytes 2359296 | tf_op jit(solution)/shard_map/all_to_all | solution.py:118
  66.2 14.1 %all-to-all-done.2 = bf16[4,1152,128]{2,1,0:T(8,128)(2,1)S(1)} async-done(((bf16[4,1152,128]{2,1,0:T(8,128)(2,1)}), bf16[4,1152,128]{2,1,0:T(8,128)(2,1)S(1)}, u32[]{:S(2)}, u32[]{:S(2)}) %all-to-all-start.2) | async-done | bytes 1179680 | tf_op jit(solution)/shard_map/all_to_all | solution.py:118
  80.3 1.6 %slice_convert_fusion = f32[32,128,128]{2,1,0:T(8,128)} fusion(bf16[32,144,128]{2,1,0:T(8,128)(2,1)S(1)} %bitcast.149), kind=kLoop, calls=%fused_computation.24 | loop fusion | flops 524288 | bytes 3145728 | tf_op jit(solution)/shard_map/convert_element_type | solution.py:47
  81.9 1.7 %reshape.555 = f32[4,8,32,512]{3,2,1,0:T(8,128)S(1)} reshape(f32[32,128,128]{2,1,0:T(8,128)} %slice_convert_fusion) | data formatting | bytes 4194304 | tf_op jit(solution)/shard_map/convert_element_type | solution.py:47
  85.5 3.6 %all-to-all-start.3 = ((bf16[8,144,128]{2,1,0:T(8,128)(2,1)}), bf16[8,144,128]{2,1,0:T(8,128)(2,1)S(1)}, u32[]{:S(2)}, u32[]{:S(2)}) async-start(bf16[8,144,128]{2,1,0:T(8,128)(2,1)} %pad_maximum_fusion.4), calls=%async_computation.3 | async-start | bytes 589824 | tf_op jit(solution)/shard_map/all_to_all | solution.py:127
  89.8 10.1 %all-to-all-done.3 = bf16[8,144,128]{2,1,0:T(8,128)(2,1)S(1)} async-done(((bf16[8,144,128]{2,1,0:T(8,128)(2,1)}), bf16[8,144,128]{2,1,0:T(8,128)(2,1)S(1)}, u32[]{:S(2)}, u32[]{:S(2)}) %all-to-all-start.3) | async-done | bytes 294944 | tf_op jit(solution)/shard_map/all_to_all | solution.py:127
  (91 shorter events, 7.4 us)
Async XLA Ops:
  0.0 13.6 %copy-start = (bf16[512,576]{0,1:T(8,128)(2,1)S(1)}, bf16[512,576]{0,1:T(8,128)(2,1)}, u32[]{:S(2)}) copy-start(bf16[512,576]{0,1:T(8,128)(2,1)} %param.8) | copy-start | bytes 1769476
  5.2 20.4 %all-to-all-start = ((bf16[8,160,128]{2,1,0:T(8,128)(2,1)}), bf16[8,160,128]{2,1,0:T(8,128)(2,1)S(1)}, u32[]{:S(2)}, u32[]{:S(2)}) async-start(bf16[8,160,128]{2,1,0:T(8,128)(2,1)} %broadcast_in_dim.102), calls=%async_computation | async-start | bytes 655360 | tf_op jit(solution)/shard_map/all_to_all | solution.py:83
  14.8 20.1 %collective-permute-start.1 = (bf16[1024,576]{0,1:T(8,128)(2,1)}, bf16[1024,576]{0,1:T(8,128)(2,1)}, u32[]{:S(2)}, u32[]{:S(2)}) collective-permute-start(bf16[1024,576]{0,1:T(8,128)(2,1)} %pad_maximum_fusion.1), channel_id=1, source_target_pairs={{0,8},{8,0},{1,9},{9,1},{2,10},{10,2},{3,11},{11,3},{4,12},{12,4},... | collective-permute-start | bytes 3538952 | tf_op jit(solution)/shard_map/ppermute | solution.py:95
  26.8 20.7 %all-to-all-start.1 = ((bf16[4,8,160,128]{3,2,1,0:T(8,128)(2,1)}), bf16[4,8,160,128]{3,2,1,0:T(8,128)(2,1)S(1)}, u32[]{:S(2)}, u32[]{:S(2)}) async-start(bf16[4,8,160,128]{3,2,1,0:T(8,128)(2,1)} %broadcast_in_dim.103), calls=%async_computation.1 | async-start | bytes 2621440 | tf_op jit(solution)/shard_map/all_to_all | solution.py:86
  31.1 3.2 %collective-permute-start = (s32[1]{0:T(128)}, s32[1]{0:T(128)}, u32[]{:S(2)}, u32[]{:S(2)}) collective-permute-start(s32[1]{0:T(128)} %param.11), channel_id=1, source_target_pairs={{0,8},{8,0},{1,9},{9,1},{2,10},{10,2},{3,11},{11,3},{4,12},{12,4},... | collective-permute-start | bytes 20 | tf_op jit(solution)/shard_map/ppermute | solution.py:95
  47.6 2.3 %copy-start.1 = (bf16[512,576]{0,1:T(8,128)(2,1)S(1)}, bf16[512,576]{0,1:T(8,128)(2,1)}, u32[]{:S(2)}) copy-start(bf16[512,576]{0,1:T(8,128)(2,1)} %param.8) | copy-start | bytes 1769476
  55.4 2.7 %copy-start.2 = (bf16[2048,576]{0,1:T(8,128)(2,1)S(1)}, bf16[2048,576]{0,1:T(8,128)(2,1)}, u32[]{:S(2)}) copy-start(bf16[2048,576]{0,1:T(8,128)(2,1)} %pad_maximum_fusion) | copy-start | bytes 7077892
  62.6 17.7 %all-to-all-start.2 = ((bf16[4,1152,128]{2,1,0:T(8,128)(2,1)}), bf16[4,1152,128]{2,1,0:T(8,128)(2,1)S(1)}, u32[]{:S(2)}, u32[]{:S(2)}) async-start(bf16[4,1152,128]{2,1,0:T(8,128)(2,1)} %bitcast.15), calls=%async_computation.2 | async-start | bytes 2359296 | tf_op jit(solution)/shard_map/all_to_all | solution.py:118
  83.9 5.2 %copy-start.3 = (bf16[1,8,64,576]{3,2,1,0:T(8,128)(2,1)S(1)}, bf16[1,8,64,576]{3,2,1,0:T(8,128)(2,1)}, u32[]{:S(2)}) copy-start(bf16[1,8,64,576]{3,2,1,0:T(8,128)(2,1)} %param.9) | copy-start | bytes 1769476
  83.9 5.2 %copy-start.4 = (bf16[2,1,16,576]{3,2,1,0:T(8,128)(2,1)S(1)}, bf16[2,1,16,576]{3,2,1,0:T(8,128)(2,1)}, u32[]{:S(2)}) copy-start(bf16[2,1,16,576]{3,2,1,0:T(8,128)(2,1)} %param.7) | copy-start | bytes 110596
  83.9 5.2 %copy-start.5 = (bf16[2,1,576]{2,0,1:T(2,128)(2,1)S(1)}, bf16[2,1,576]{2,0,1:T(2,128)(2,1)}, u32[]{:S(2)}) copy-start(bf16[2,1,576]{2,0,1:T(2,128)(2,1)} %param.10) | copy-start | bytes 6916
  85.5 14.4 %all-to-all-start.3 = ((bf16[8,144,128]{2,1,0:T(8,128)(2,1)}), bf16[8,144,128]{2,1,0:T(8,128)(2,1)S(1)}, u32[]{:S(2)}, u32[]{:S(2)}) async-start(bf16[8,144,128]{2,1,0:T(8,128)(2,1)} %pad_maximum_fusion.4), calls=%async_computation.3 | async-start | bytes 589824 | tf_op jit(solution)/shard_map/all_to_all | solution.py:127

commit v6 on v3

--- a/solution.py
+++ b/solution.py
@@ -55,20 +55,21 @@
     my_beam = chip * 2 + core
     partner_beam = chip * 2 + (1 - core)
 
-    q_rows = steps_n * head_dev * width // LANES
-    lane = lax.broadcasted_iota(jnp.int32, (META_ROWS, LANES), 1)
-    first = lax.broadcasted_iota(jnp.int32, (META_ROWS, LANES), 0) == 0
+    row_n = steps_n * head_dev
+    spare = -(-width // LANES) * LANES - width
+    lane = lax.broadcasted_iota(jnp.int32, (row_n, spare), 1)
+    first = lax.broadcasted_iota(jnp.int32, (row_n, spare), 0) == 0
     meta = jnp.where(lane == 0, parent[0], jnp.where(lane == 1, fork_pages[0, 0], fork_pages[0, 1]))
     meta = jnp.where(first & (lane < 3), meta, 0).astype(jnp.bfloat16)
-    packed = jnp.concatenate([queries.reshape(q_rows, LANES), meta], axis=0)
+    packed = jnp.concatenate([queries.reshape(row_n, width), meta], axis=1)
     along_y = lax.all_to_all(
         jnp.broadcast_to(packed[None], (lax.axis_size("cy"),) + packed.shape), "cy", 0, 0, tiled=True
     )
     gathered = lax.all_to_all(
         jnp.broadcast_to(along_y[None], (lax.axis_size("cx"),) + along_y.shape), "cx", 0, 0, tiled=True
     ).reshape((chips,) + packed.shape)
-    rows = gathered[:, :q_rows].reshape(chips, steps_n * head_dev, width)
-    meta_all = gathered[:, q_rows, :3].astype(jnp.int32)
+    rows = gathered[:, :, :width]
+    meta_all = gathered[:, 0, width : width + 3].astype(jnp.int32)
     par, fp0, fp1 = meta_all[:, 0], meta_all[:, 1], meta_all[:, 2]
 
     own_suffix = suffix_cache.reshape(suffix_n, width)
@@ -100,7 +101,6 @@
     payload = jnp.concatenate([out_rows, parts.reshape(chips, stat_rows, LANES)], axis=1)
     arrived = lax.all_to_all(payload, ("cx", "cy"), 0, 0, tiled=True)
     n_out = out_rows.shape[1]
-    row_n = steps_n * head_dev
     out_r = arrived[:, :n_out].reshape(chips, row_n, DL)
     got = arrived[:, n_out:].reshape(chips, -1)[:, : 6 * row_n].astype(jnp.float32).reshape(chips, 6, row_n)
     top_r = (got[:, 0] + got[:, 1]) + got[:, 2]

time: 99 us -> 103 us (1.040)
  other arithmetic: 11.2 us -> 12.5 us
  waiting for transfers between devices: 47.7 us -> 48.9 us
  matrix products: 9.23 us -> 10.3 us
    reshape x2 -> x0, local copies, waits for them, and re-layouts: 2.85 us -> none  [the longest x1 1.95 us: on_device(): rows = gathered[:, :q_rows].reshape(chips, steps_n * head_dev, width)]
    concatenate x1, other arithmetic: 3.02 us -> 1.52 us  [on_device(): keys = jnp.concatenate([local_keys, partner_keys], axis=0)]
    concatenate x1, other arithmetic: 1.19 us -> 0.16 us  [on_device(): local_keys = jnp.concatenate([prompt_cache, own_suffix], axis=0)]
  transfers between devices with their start and end apart: 5 -> 5, of which waited for: 4 -> 3; matrix products, arithmetic and copies ran while one was open for 8% -> 7% of each run, Pallas kernels for 0% -> 0%
where the time goes in v6:
time: 103 us; the launch traced here: 101 us
  waiting for transfers between devices  48.9 us (47%)
  starting transfers between devices  19.2 us (19%)
  other arithmetic  12.5 us (12%)
  matrix products  10.3 us (10%)
  local copies, waits for them, and re-layouts  8.71 us (8%)
  between operations  1.63 us (2%)
    all_to_all x1, waiting for transfers between devices, on_device(): arrived = lax.all_to_all(payload, ('cx', 'cy'), 0, 0, tiled=True)  28.6 us
    all_to_all x1, waiting for transfers between devices, on_device(): lax.all_to_all(jnp.broadcast_to(along_y[None], (lax.axis_size('cx'),) + a...  10.5 us
    all_to_all x1, waiting for transfers between devices, on_device(): lax.all_to_all(jnp.broadcast_to(packed[None], (lax.axis_size('cy'),) + pa...  9.86 us
    all_to_all x1, starting transfers between devices, on_device(): lax.all_to_all(jnp.broadcast_to(packed[None], (lax.axis_size('cy'),) + pa...  7.1 us
    dot_general x1, matrix products, masked_softmax(): jnp.einsum('gqk,tk->gqt', rows, keys, preferred_element_type=jnp.float32)  5.46 us
    all_to_all x1, starting transfers between devices, on_device(): lax.all_to_all(jnp.broadcast_to(along_y[None], (lax.axis_size('cx'),) + a...  4.29 us
    all_to_all x1, starting transfers between devices, on_device(): arrived = lax.all_to_all(payload, ('cx', 'cy'), 0, 0, tiled=True)  3.94 us
    ppermute x2, starting transfers between devices, on_device(): lax.ppermute((local_keys, suffix_len), 'core', [(0, 1), (1, 0)])  3.85 us
  transfers between devices with their start and end apart: 5, of which 3 were waited for; matrix products, arithmetic and copies ran while one was open for 7% of the time, Pallas kernels for 0%

profile of v6, /device:TPU:448, one launch (start us, length us, event | category | flops | bytes accessed | tf_op | source)
XLA Modules:
  0.0 101.2 jit_solution(8561938693715365869)
XLA Ops:
  0.0 1.4 %fusion.50 = (s32[1,1]{1,0:T(1,128)}, s32[1,1]{1,0:T(1,128)}) fusion(s32[1,2]{1,0:T(1,128)} %param.13), kind=kLoop, calls=%fused_computation.102 | loop fusion | bytes 16 | tf_op jit(solution)/shard_map/slice | solution.py:62
  2.1 1.3 %compare_select_fusion = s32[64]{0:T(128)S(1)} fusion(s32[]{:T(128)} %bitcast.3, s32[]{:T(128)} %bitcast.2), kind=kLoop, calls=%fused_computation.83 | loop fusion | flops 128 | bytes 264 | tf_op jit(solution)/shard_map/jit(_where)/select_n | solution.py:62
  3.4 0.9 pad_maximum_fusion.5
  4.3 0.7 broadcast_in_dim.99
  5.0 7.1 %all-to-all-start = ((bf16[8,32,640]{2,1,0:T(8,128)(2,1)}), bf16[8,32,640]{2,1,0:T(8,128)(2,1)S(1)}, u32[]{:S(2)}, u32[]{:S(2)}) async-start(bf16[8,32,640]{2,1,0:T(8,128)(2,1)} %broadcast_in_dim.99), calls=%async_computation | async-start | bytes 655360 | tf_op jit(solution)/shard_map/all_to_all | solution.py:65
  12.1 1.3 %copy.42 = bf16[512,576]{0,1:T(8,128)(2,1)S(1)} copy(bf16[512,576]{1,0:T(8,128)(2,1)} %bitcast.94) | data formatting | bytes 1179648 | tf_op jit(solution)/shard_map/reshape | solution.py:75
  13.6 1.9 %collective-permute-start.1 = (bf16[1024,576]{0,1:T(8,128)(2,1)S(1)}, bf16[1024,576]{0,1:T(8,128)(2,1)}, u32[]{:S(2)}, u32[]{:S(2)}) collective-permute-start(bf16[1024,576]{0,1:T(8,128)(2,1)S(1)} %pad_maximum_fusion.1), channel_id=1, source_target_pairs={{0,8},{8,0},{1,9},{9,1},{2,10},{10,2},{3,11},{11,3},{4,12},{12,4},... | collective-permute-start | bytes 3538952 | tf_op jit(solution)/shard_map/ppermute | solution.py:77
  15.5 9.9 %all-to-all-done = bf16[8,32,640]{2,1,0:T(8,128)(2,1)S(1)} async-done(((bf16[8,32,640]{2,1,0:T(8,128)(2,1)}), bf16[8,32,640]{2,1,0:T(8,128)(2,1)S(1)}, u32[]{:S(2)}, u32[]{:S(2)}) %all-to-all-start) | async-done | bytes 327712 | tf_op jit(solution)/shard_map/all_to_all | solution.py:65
  25.4 1.2 %broadcast_in_dim.100 = bf16[4,8,32,640]{3,2,1,0:T(8,128)(2,1)} broadcast(bf16[8,32,640]{2,1,0:T(8,128)(2,1)S(1)} %all-to-all-done), dimensions={1,2,3} | broadcast | bytes 1638400 | tf_op jit(solution)/shard_map/broadcast_in_dim | solution.py:69
  26.6 4.3 %all-to-all-start.1 = ((bf16[4,8,32,640]{3,2,1,0:T(8,128)(2,1)}), bf16[4,8,32,640]{3,2,1,0:T(8,128)(2,1)}, u32[]{:S(2)}, u32[]{:S(2)}) async-start(bf16[4,8,32,640]{3,2,1,0:T(8,128)(2,1)} %broadcast_in_dim.100), calls=%async_computation.1 | async-start | bytes 2621440 | tf_op jit(solution)/shard_map/all_to_all | solution.py:68
  30.9 1.9 %collective-permute-start = (s32[1]{0:T(128)}, s32[1]{0:T(128)}, u32[]{:S(2)}, u32[]{:S(2)}) collective-permute-start(s32[1]{0:T(128)} %param.11), channel_id=1, source_target_pairs={{0,8},{8,0},{1,9},{9,1},{2,10},{10,2},{3,11},{11,3},{4,12},{12,4},... | collective-permute-start | bytes 20 | tf_op jit(solution)/shard_map/ppermute | solution.py:77
  34.6 1.1 %iota_compare_fusion = pred[512]{0:T(512)(128)(4,1)} fusion(s32[]{:T(128)} %bitcast.10), kind=kLoop, calls=%fused_computation.78 | loop fusion | flops 512 | bytes 516 | tf_op jit(solution)/shard_map/lt | solution.py:87
  35.7 1.5 %pad_maximum_fusion = bf16[2048,576]{0,1:T(8,128)(2,1)S(1)} fusion(bf16[1024,576]{0,1:T(8,128)(2,1)} %collective-permute-done.1, bf16[512,576]{0,1:T(8,128)(2,1)S(1)} %copy.42, bf16[512,576]{0,1:T(8,128)(2,1)S(1)} %copy-done), kind=kLoop, calls=%fused_computation.7 | loop fusion | flops 7077888 | bytes 4718592 | tf_op jit(solution)/shard_map/concatenate | solution.py:78
  37.2 10.5 %all-to-all-done.1 = bf16[4,8,32,640]{3,2,1,0:T(8,128)(2,1)} async-done(((bf16[4,8,32,640]{3,2,1,0:T(8,128)(2,1)}), bf16[4,8,32,640]{3,2,1,0:T(8,128)(2,1)}, u32[]{:S(2)}, u32[]{:S(2)}) %all-to-all-start.1) | async-done | bytes 1310752 | tf_op jit(solution)/shard_map/all_to_all | solution.py:68
  47.7 0.9 slice.72
  50.0 0.8 fusion.26
  50.9 5.5 %select_reduce_fusion = (f32[32,32]{1,0:T(8,128)S(1)}, f32[32,32,2048]{2,1,0:T(8,128)S(1)}) fusion(pred[32,2048]{1,0:T(8,128)(4,1)S(1)} %broadcast_compare_fusion, bf16[1024,576]{0,1:T(8,128)(2,1)} %collective-permute-done.1, bf16[512,576]{0,1:T(8,128)(2,1)S(1)} %copy.42, bf16[512,576]{0,1:T(8,128)(2,1)S(1)} %copy-done, bf16[32,32,640]{2,1,0:T(8,128)(2,1)} %bitcast.4), kind=kOutput, calls=%fused_computation.2 | convolution fusion | flops 2429287424 | bytes 12128256 | tf_op jit(solution)/shard_map/gqk,tk->gqt/dot_general | solution.py:16
  56.4 2.7 %multiply_reduce_fusion = f32[32,32]{1,0:T(8,128)S(1)} fusion(f32[32,32,2048]{2,1,0:T(8,128)S(1)} %get-tuple-element.25, f32[32,2048]{1,0:T(8,128)S(1)} %pad_maximum_fusion.4, f32[32,32]{1,0:T(8,128)S(1)} %get-tuple-element.24, pred[32,2048]{1,0:T(8,128)(4,1)S(1)} %broadcast_compare_fusion), kind=kLoop, calls=%fused_computation | loop fusion | flops 10484736 | bytes 8724480 | tf_op jit(solution)/shard_map/reduce_sum | solution.py:21
  59.1 3.5 %divide_convert_fusion = bf16[32,32,512]{2,1,0:T(8,128)(2,1)} fusion(f32[32,32]{1,0:T(8,128)S(1)} %multiply_reduce_fusion, bf16[2048,576]{0,1:T(8,128)(2,1)S(1)} %pad_maximum_fusion, f32[32,32,2048]{2,1,0:T(8,128)S(1)} %get-tuple-element.25, f32[32,32]{1,0:T(8,128)S(1)} %get-tuple-element.24, pred[32,2048]{1,0:T(8,128)(4,1)S(1)} %broadcast_compare_fusion, ...), kind=kOutput, calls=%fused_computation.12 | convolution fusion | flops 2159017984 | bytes 11763712 | tf_op jit(solution)/shard_map/gqt,td->gqd/dot_general | solution.py:23
  62.6 1.7 %reshape.384 = bf16[32,128,128]{2,1,0:T(8,128)(2,1)S(1)} reshape(bf16[32,32,512]{2,1,0:T(8,128)(2,1)} %divide_convert_fusion) | data formatting | bytes 2097152 | tf_op jit(solution)/shard_map/reshape | solution.py:97
  64.6 1.1 %pad_maximum_fusion.2 = bf16[32,144,128]{2,1,0:T(8,128)(2,1)} fusion(bf16[32,16,128]{2,1,0:T(8,128)(2,1)S(1)} %bitcast.97, bf16[32,128,128]{2,1,0:T(8,128)(2,1)S(1)} %reshape.384), kind=kLoop, calls=%fused_computation.16 | loop fusion | flops 2359296 | bytes 2359296 | tf_op jit(solution)/shard_map/concatenate | solution.py:101
  65.7 3.9 %all-to-all-start.2 = ((bf16[32,144,128]{2,1,0:T(8,128)(2,1)}), bf16[32,144,128]{2,1,0:T(8,128)(2,1)S(1)}, u32[]{:S(2)}, u32[]{:S(2)}) async-start(bf16[32,144,128]{2,1,0:T(8,128)(2,1)} %pad_maximum_fusion.2), calls=%async_computation.2 | async-start | bytes 2359296 | tf_op jit(solution)/shard_map/all_to_all | solution.py:102
  70.4 28.6 %all-to-all-done.2 = bf16[32,144,128]{2,1,0:T(8,128)(2,1)S(1)} async-done(((bf16[32,144,128]{2,1,0:T(8,128)(2,1)}), bf16[32,144,128]{2,1,0:T(8,128)(2,1)S(1)}, u32[]{:S(2)}, u32[]{:S(2)}) %all-to-all-start.2) | async-done | bytes 1179680 | tf_op jit(solution)/shard_map/all_to_all | solution.py:102
  100.4 0.9 fusion.14
  (58 shorter events, 5.1 us)
Async XLA Ops:
  0.0 13.4 %copy-start = (bf16[512,576]{0,1:T(8,128)(2,1)S(1)}, bf16[512,576]{0,1:T(8,128)(2,1)}, u32[]{:S(2)}) copy-start(bf16[512,576]{0,1:T(8,128)(2,1)} %param.8) | copy-start | bytes 1769476
  5.0 20.4 %all-to-all-start = ((bf16[8,32,640]{2,1,0:T(8,128)(2,1)}), bf16[8,32,640]{2,1,0:T(8,128)(2,1)S(1)}, u32[]{:S(2)}, u32[]{:S(2)}) async-start(bf16[8,32,640]{2,1,0:T(8,128)(2,1)} %broadcast_in_dim.99), calls=%async_computation | async-start | bytes 655360 | tf_op jit(solution)/shard_map/all_to_all | solution.py:65
  13.6 22.1 %collective-permute-start.1 = (bf16[1024,576]{0,1:T(8,128)(2,1)S(1)}, bf16[1024,576]{0,1:T(8,128)(2,1)}, u32[]{:S(2)}, u32[]{:S(2)}) collective-permute-start(bf16[1024,576]{0,1:T(8,128)(2,1)S(1)} %pad_maximum_fusion.1), channel_id=1, source_target_pairs={{0,8},{8,0},{1,9},{9,1},{2,10},{10,2},{3,11},{11,3},{4,12},{12,4},... | collective-permute-start | bytes 3538952 | tf_op jit(solution)/shard_map/ppermute | solution.py:77
  26.6 21.1 %all-to-all-start.1 = ((bf16[4,8,32,640]{3,2,1,0:T(8,128)(2,1)}), bf16[4,8,32,640]{3,2,1,0:T(8,128)(2,1)}, u32[]{:S(2)}, u32[]{:S(2)}) async-start(bf16[4,8,32,640]{3,2,1,0:T(8,128)(2,1)} %broadcast_in_dim.100), calls=%async_computation.1 | async-start | bytes 2621440 | tf_op jit(solution)/shard_map/all_to_all | solution.py:68
  30.9 3.7 %collective-permute-start = (s32[1]{0:T(128)}, s32[1]{0:T(128)}, u32[]{:S(2)}, u32[]{:S(2)}) collective-permute-start(s32[1]{0:T(128)} %param.11), channel_id=1, source_target_pairs={{0,8},{8,0},{1,9},{9,1},{2,10},{10,2},{3,11},{11,3},{4,12},{12,4},... | collective-permute-start | bytes 20 | tf_op jit(solution)/shard_map/ppermute | solution.py:77
  64.5 5.1 %copy-start.3 = (pred[512]{0:T(512)(128)(4,1)S(1)}, pred[512]{0:T(512)(128)(4,1)}, u32[]{:S(2)}) copy-start(pred[512]{0:T(512)(128)(4,1)} %iota_compare_fusion.1) | copy-start | bytes 1540
  64.5 5.1 %copy-start.1 = (bf16[1,8,64,576]{3,2,1,0:T(8,128)(2,1)S(1)}, bf16[1,8,64,576]{3,2,1,0:T(8,128)(2,1)}, u32[]{:S(2)}) copy-start(bf16[1,8,64,576]{3,2,1,0:T(8,128)(2,1)} %param.9) | copy-start | bytes 1769476
  64.6 5.1 %copy-start.2 = (bf16[2,1,16,576]{3,2,1,0:T(8,128)(2,1)S(1)}, bf16[2,1,16,576]{3,2,1,0:T(8,128)(2,1)}, u32[]{:S(2)}) copy-start(bf16[2,1,16,576]{3,2,1,0:T(8,128)(2,1)} %param.7) | copy-start | bytes 110596
  64.6 5.1 %copy-start.4 = (bf16[2,1,576]{2,0,1:T(2,128)(2,1)S(1)}, bf16[2,1,576]{2,0,1:T(2,128)(2,1)}, u32[]{:S(2)}) copy-start(bf16[2,1,576]{2,0,1:T(2,128)(2,1)} %param.10) | copy-start | bytes 6916
  65.7 33.3 %all-to-all-start.2 = ((bf16[32,144,128]{2,1,0:T(8,128)(2,1)}), bf16[32,144,128]{2,1,0:T(8,128)(2,1)S(1)}, u32[]{:S(2)}, u32[]{:S(2)}) async-start(bf16[32,144,128]{2,1,0:T(8,128)(2,1)} %pad_maximum_fusion.2), calls=%async_computation.2 | async-start | bytes 2359296 | tf_op jit(solution)/shard_map/all_to_all | solution.py:102

commit v7 on v3

--- a/solution.py
+++ b/solution.py
@@ -10,6 +10,29 @@
 
 score_scale = 192.0 ** (-0.5)
 neg_large = -1e30
+
+
+def prompt_softmax(rows, keys):
+    scores = jnp.einsum("gqk,tk->gqt", rows, keys, preferred_element_type=jnp.float32) * score_scale
+    top = jnp.max(scores, axis=-1)
+    weights = jnp.exp(scores - top[..., None])
+    total = jnp.sum(weights, axis=-1)
+    summed = jnp.einsum(
+        "gqt,td->gqd", weights.astype(jnp.bfloat16), keys[:, :DL], preferred_element_type=jnp.float32
+    )
+    return top, total, summed
+
+
+def fork_softmax(rows, keys, valid):
+    scores = jnp.einsum("gqk,gtk->gqt", rows, keys, preferred_element_type=jnp.float32) * score_scale
+    v = valid[:, None, :]
+    top = jnp.max(jnp.where(v, scores, neg_large), axis=-1)
+    weights = jnp.where(v, jnp.exp(scores - top[..., None]), 0.0)
+    total = jnp.sum(weights, axis=-1)
+    summed = jnp.einsum(
+        "gqt,gtd->gqd", weights.astype(jnp.bfloat16), keys[..., :DL], preferred_element_type=jnp.float32
+    )
+    return top, total, summed
 
 
 def masked_softmax(rows, keys, mult):
@@ -74,24 +97,26 @@
     own_suffix = suffix_cache.reshape(suffix_n, width)
     local_keys = jnp.concatenate([prompt_cache, own_suffix], axis=0)
     partner_keys, partner_len = lax.ppermute((local_keys, suffix_len), "core", [(0, 1), (1, 0)])
-    keys = jnp.concatenate([local_keys, partner_keys], axis=0)
+    prompt_keys = jnp.concatenate([prompt_cache, partner_keys[:prompt_n]], axis=0)
+    pages = jnp.concatenate(
+        [suffix_cache[0], partner_keys[prompt_n:].reshape(pages_n, page_len, width)], axis=0
+    )
 
-    position = jnp.arange(suffix_n, dtype=jnp.int32)
-    page = position // page_len
+    mine = par == my_beam
+    here = mine | (par == partner_beam)
+    picked = jnp.stack([fp0, fp1], axis=1)
+    fork_keys = pages[jnp.where(mine, 0, pages_n)[:, None] + picked].reshape(chips, -1, width)
+    length = jnp.where(mine, suffix_len[0], partner_len[0])
+    offsets = (picked[:, :, None] * page_len + jnp.arange(page_len, dtype=jnp.int32)[None, None, :]).reshape(chips, -1)
+    fork_ok = here[:, None] & (offsets < length[:, None])
 
-    def fork_count(owner, length):
-        hits = (page[None, :] == fp0[:, None]).astype(jnp.float32) + (page[None, :] == fp1[:, None]).astype(
-            jnp.float32
-        )
-        keep = (par == owner)[:, None] & (position < length)[None, :]
-        return jnp.where(keep, hits, 0.0)
-
-    ones = jnp.ones((chips, prompt_n), jnp.float32)
-    mult = jnp.concatenate(
-        [ones, fork_count(my_beam, suffix_len[0]), ones, fork_count(partner_beam, partner_len[0])], axis=1
-    )
-    top, total, summed = masked_softmax(rows, keys, mult)
-    out = (summed / total[..., None]).astype(jnp.bfloat16)
+    top_p, total_p, summed_p = prompt_softmax(rows, prompt_keys)
+    top_f, total_f, summed_f = fork_softmax(rows, fork_keys, fork_ok)
+    top = jnp.maximum(top_p, top_f)
+    scale_p = jnp.exp(top_p - top)
+    scale_f = jnp.exp(top_f - top)
+    total = scale_p * total_p + scale_f * total_f
+    out = ((scale_p[..., None] * summed_p + scale_f[..., None] * summed_f) / total[..., None]).astype(jnp.bfloat16)
 
     out_rows = out.reshape(chips, -1, LANES)
     parts = jnp.stack(split3(top) + split3(total), axis=1).reshape(chips, -1)
@@ -106,6 +131,7 @@
     top_r = (got[:, 0] + got[:, 1]) + got[:, 2]
     total_r = (got[:, 3] + got[:, 4]) + got[:, 5]
 
+    position = jnp.arange(suffix_n, dtype=jnp.int32)
     own_keys = jnp.concatenate([own_suffix, new_latent[:, 0, :]], axis=0)
     old_valid = jnp.broadcast_to((position < suffix_len[0])[None, :], (steps_n, suffix_n))
     new_valid = jnp.arange(steps_n, dtype=jnp.int32)[None, :] <= jnp.arange(steps_n, dtype=jnp.int32)[:, None]

time: 99 us -> 114 us (1.15)
  blocking collectives: 0 us -> 20.8 us
  starting transfers between devices: 19.2 us -> 12.2 us
  local copies, waits for them, and re-layouts: 9.17 us -> 16.1 us
  waiting for transfers between devices: 47.7 us -> 40.9 us
  matrix products: 9.23 us -> 12.7 us
  other arithmetic: 11.2 us -> 8.16 us
    all_to_all x0 -> x1, blocking collectives: none -> 20.8 us  [on_device(): lax.all_to_all(jnp.broadcast_to(packed[None], (lax.axis_size('cy'),) + pa...]
    all_to_all x1 -> x0, waiting for transfers between devices: 8.84 us -> none  [on_device(): lax.all_to_all(jnp.broadcast_to(packed[None], (lax.axis_size('cy'),) + pa...]
    all_to_all x1 -> x0, starting transfers between devices: 7.1 us -> none  [on_device(): lax.all_to_all(jnp.broadcast_to(packed[None], (lax.axis_size('cy'),) + pa...]
    gather x0 -> x1, local copies, waits for them, and re-layouts: none -> 3.49 us  [on_device(): pages[jnp.where(mine, 0, pages_n)[:, None] + picked]]
    dot_general x2 -> x4, matrix products: 7.93 us -> 11.4 us  [the longest x1 4.56 us: fork_softmax(): jnp.einsum('gqk,gtk->gqt', rows, keys, preferred_element_type=jnp.float32)]
    slice x0 -> x2, local copies, waits for them, and re-layouts: none -> 3.25 us  [the longest x1 2.15 us: on_device(): partner_keys[:prompt_n]]
    concatenate x2 -> x1, other arithmetic: 3.04 us -> 1.27 us  [on_device(): jnp.concatenate([suffix_cache[0], partner_keys[prompt_n:].reshape(pages_n...]
    all_to_all x1, waiting for transfers between devices: 28.6 us -> 30.1 us  [on_device(): arrived = lax.all_to_all(payload, ('cx', 'cy'), 0, 0, tiled=True)]
  transfers between devices with their start and end apart: 5 -> 4, of which waited for: 4 -> 2; matrix products, arithmetic and copies ran while one was open for 8% -> 17% of each run, Pallas kernels for 0% -> 0%
where the time goes in v7:
time: 114 us; the launch traced here: 113 us
  waiting for transfers between devices  40.9 us (36%)
  blocking collectives  20.8 us (18%)
  local copies, waits for them, and re-layouts  16.1 us (14%)
  matrix products  12.7 us (11%)
  starting transfers between devices  12.2 us (11%)
  other arithmetic  8.16 us (7%)
  between operations  1.66 us (1%)
    all_to_all x1, waiting for transfers between devices, on_device(): arrived = lax.all_to_all(payload, ('cx', 'cy'), 0, 0, tiled=True)  30.1 us
    all_to_all x1, blocking collectives, on_device(): lax.all_to_all(jnp.broadcast_to(packed[None], (lax.axis_size('cy'),) + pa...  20.8 us
    all_to_all x1, waiting for transfers between devices, on_device(): lax.all_to_all(jnp.broadcast_to(along_y[None], (lax.axis_size('cx'),) + a...  10.8 us
    dot_general x1, matrix products, fork_softmax(): jnp.einsum('gqk,gtk->gqt', rows, keys, preferred_element_type=jnp.float32)  4.56 us
    all_to_all x1, starting transfers between devices, on_device(): lax.all_to_all(jnp.broadcast_to(along_y[None], (lax.axis_size('cx'),) + a...  4.29 us
    ppermute x2, starting transfers between devices, on_device(): lax.ppermute((local_keys, suffix_len), 'core', [(0, 1), (1, 0)])  3.96 us
    all_to_all x1, starting transfers between devices, on_device(): arrived = lax.all_to_all(payload, ('cx', 'cy'), 0, 0, tiled=True)  3.94 us
    gather x1, local copies, waits for them, and re-layouts, on_device(): pages[jnp.where(mine, 0, pages_n)[:, None] + picked]  3.49 us
  transfers between devices with their start and end apart: 4, of which 2 were waited for; matrix products, arithmetic and copies ran while one was open for 17% of the time, Pallas kernels for 0%

profile of v7, /device:TPU:448, one launch (start us, length us, event | category | flops | bytes accessed | tf_op | source)
XLA Modules:
  0.0 112.6 jit_solution(9778503046503280019)
XLA Ops:
  0.0 1.3 %copy.40 = bf16[512,576]{0,1:T(8,128)(2,1)S(1)} copy(bf16[512,576]{1,0:T(8,128)(2,1)} %bitcast.118) | data formatting | bytes 1179648 | tf_op jit(solution)/shard_map/reshape | solution.py:97
  1.3 1.2 %pad_maximum_fusion = bf16[1024,576]{0,1:T(8,128)(2,1)S(1)} fusion(bf16[512,576]{0,1:T(8,128)(2,1)} %param.8, bf16[512,576]{0,1:T(8,128)(2,1)S(1)} %copy.40), kind=kLoop, calls=%fused_computation.13 | loop fusion | flops 2359296 | bytes 2359296 | tf_op jit(solution)/shard_map/concatenate | solution.py:98
  2.6 1.9 %collective-permute-start = (bf16[1024,576]{0,1:T(8,128)(2,1)S(1)}, bf16[1024,576]{0,1:T(8,128)(2,1)}, u32[]{:S(2)}, u32[]{:S(2)}) collective-permute-start(bf16[1024,576]{0,1:T(8,128)(2,1)S(1)} %pad_maximum_fusion), channel_id=1, source_target_pairs={{0,8},{8,0},{1,9},{9,1},{2,10},{10,2},{3,11},{11,3},{4,12},{12,4},... | collective-permute-start | bytes 3538952 | tf_op jit(solution)/shard_map/ppermute | solution.py:99
  5.9 1.2 %compare_select_fusion.1 = s32[128]{0:T(128)S(1)} fusion(s32[]{:T(128)} %bitcast.2, s32[]{:T(128)} %bitcast.1), kind=kLoop, calls=%fused_computation.99 | loop fusion | flops 256 | bytes 520 | tf_op jit(solution)/shard_map/jit(_where)/select_n | solution.py:84
  7.2 20.8 %all_to_all.15 = bf16[8,160,128]{2,1,0:T(8,128)(2,1)S(1)} all-to-all(bf16[8,160,128]{2,1,0:T(8,128)(2,1)S(1)} %broadcast_in_dim.109), channel_id=1, replica_groups=mesh['cx'=4,'cy'=8,'core'=2,'hd'=8] {'cy'}, dimensions={0} | all-to-all | bytes 655360 | tf_op jit(solution)/shard_map/all_to_all | solution.py:87
  28.1 1.3 %broadcast_in_dim.110 = bf16[4,8,160,128]{3,2,1,0:T(8,128)(2,1)} broadcast(bf16[8,160,128]{2,1,0:T(8,128)(2,1)S(1)} %all_to_all.15), dimensions={1,2,3} | broadcast | bytes 1638400 | tf_op jit(solution)/shard_map/broadcast_in_dim | solution.py:91
  29.3 4.3 %all-to-all-start.1 = ((bf16[4,8,160,128]{3,2,1,0:T(8,128)(2,1)}), bf16[4,8,160,128]{3,2,1,0:T(8,128)(2,1)S(1)}, u32[]{:S(2)}, u32[]{:S(2)}) async-start(bf16[4,8,160,128]{3,2,1,0:T(8,128)(2,1)} %broadcast_in_dim.110), calls=%async_computation.1 | async-start | bytes 2621440 | tf_op jit(solution)/shard_map/all_to_all | solution.py:90
  33.6 2.0 %collective-permute-start.1 = (s32[1]{0:T(128)}, s32[1]{0:T(128)}, u32[]{:S(2)}, u32[]{:S(2)}) collective-permute-start(s32[1]{0:T(128)} %param.11), channel_id=1, source_target_pairs={{0,8},{8,0},{1,9},{9,1},{2,10},{10,2},{3,11},{11,3},{4,12},{12,4},... | collective-permute-start | bytes 20 | tf_op jit(solution)/shard_map/ppermute | solution.py:99
  36.4 2.1 %fusion.65 = (bf16[512,576]{0,1:T(8,128)(2,1)}, bf16[512,576]{0,1:T(8,128)(2,1)S(1)}) fusion(bf16[1024,576]{0,1:T(8,128)(2,1)} %collective-permute-done), kind=kLoop, calls=%fused_computation.120 | loop fusion | bytes 2359296 | tf_op jit(solution)/shard_map/slice | solution.py:100
  38.6 1.1 copy.43
  39.7 1.3 %pad_maximum_fusion.2 = bf16[16,64,576]{2,1,0:T(8,128)(2,1)S(1)} fusion(bf16[8,64,576]{2,1,0:T(8,128)(2,1)} %bitcast.122, bf16[8,64,576]{2,1,0:T(8,128)(2,1)S(1)} %bitcast.119), kind=kLoop, calls=%fused_computation.16 | loop fusion | flops 589824 | bytes 2359296 | tf_op jit(solution)/shard_map/concatenate | solution.py:101
  41.0 10.8 %all-to-all-done.1 = bf16[4,8,160,128]{3,2,1,0:T(8,128)(2,1)S(1)} async-done(((bf16[4,8,160,128]{3,2,1,0:T(8,128)(2,1)}), bf16[4,8,160,128]{3,2,1,0:T(8,128)(2,1)S(1)}, u32[]{:S(2)}, u32[]{:S(2)}) %all-to-all-start.1) | async-done | bytes 1310752 | tf_op jit(solution)/shard_map/all_to_all | solution.py:90
  51.8 1.1 slice.81
  52.9 2.6 %reshape.377 = bf16[32,32,576]{2,1,0:T(8,128)(2,1)S(1)} reshape(bf16[32,144,128]{2,1,0:T(8,128)(2,1)} %slice.81) | data formatting | bytes 2359296 | tf_op jit(solution)/shard_map/reshape | solution.py:93
  55.5 3.1 %multiply_reduce_fusion = (f32[32,32]{1,0:T(8,128)S(1)}, f32[32,32,1024]{2,1,0:T(8,128)S(1)}) fusion(bf16[32,32,576]{2,1,0:T(8,128)(2,1)S(1)} %reshape.377, bf16[512,576]{0,1:T(8,128)(2,1)} %get-tuple-element.16, bf16[512,576]{0,1:T(8,128)(2,1)} %param.8), kind=kOutput, calls=%fused_computation.4 | convolution fusion | flops 1212414976 | bytes 6557696 | tf_op jit(solution)/shard_map/gqk,tk->gqt/dot_general | solution.py:16
  58.6 0.9 fusion.2
  59.9 2.7 %fusion.4 = f32[32,32,512]{2,1,0:T(8,128)} fusion(f32[32,32,1024]{2,1,0:T(8,128)S(1)} %get-tuple-element.32, f32[32,32]{1,0:T(8,128)S(1)} %get-tuple-element.31, bf16[512,576]{0,1:T(8,128)(2,1)S(1)} %copy-done.3, bf16[512,576]{0,1:T(8,128)(2,1)S(1)} %copy-done.2), kind=kOutput, calls=%fused_computation.7 | convolution fusion | flops 1078984704 | bytes 7475200 | tf_op jit(solution)/shard_map/gqt,td->gqd/dot_general | solution.py:20
  63.8 3.5 %gather_fusion = bf16[64,64,576]{2,1,0:T(8,128)(2,1)} fusion(bf16[16,64,576]{2,1,0:T(8,128)(2,1)S(1)} %pad_maximum_fusion.2, s32[1024]{0:T(1024)S(1)} %pad_clamp_fusion), kind=kCustom, calls=%fused_computation | custom fusion | bytes 9437440 | tf_op jit(solution)/shard_map/gather | solution.py:108
  67.4 4.6 %select_reduce_fusion = (f32[32,32]{1,0:T(8,128)S(1)}, f32[32,32,128]{2,1,0:T(8,128)S(1)}) fusion(pred[32,128]{1,0:T(8,128)(4,1)S(1)} %fusion.50, bf16[32,32,576]{2,1,0:T(8,128)(2,1)S(1)} %reshape.377, bf16[32,128,576]{2,1,0:T(8,128)(2,1)} %bitcast.114), kind=kOutput, calls=%fused_computation.39 | convolution fusion | flops 151387136 | bytes 6430720 | tf_op jit(solution)/shard_map/gqk,gtk->gqt/dot_general | solution.py:27
  72.4 1.0 divide_convert_fusion
  74.4 1.1 pad_maximum_fusion.3
  75.5 3.9 %all-to-all-start.2 = ((bf16[32,144,128]{2,1,0:T(8,128)(2,1)}), bf16[32,144,128]{2,1,0:T(8,128)(2,1)S(1)}, u32[]{:S(2)}, u32[]{:S(2)}) async-start(bf16[32,144,128]{2,1,0:T(8,128)(2,1)} %pad_maximum_fusion.3), calls=%async_computation.2 | async-start | bytes 2359296 | tf_op jit(solution)/shard_map/all_to_all | solution.py:126
  80.2 30.1 %all-to-all-done.2 = bf16[32,144,128]{2,1,0:T(8,128)(2,1)S(1)} async-done(((bf16[32,144,128]{2,1,0:T(8,128)(2,1)}), bf16[32,144,128]{2,1,0:T(8,128)(2,1)S(1)}, u32[]{:S(2)}, u32[]{:S(2)}) %all-to-all-start.2) | async-done | bytes 1179680 | tf_op jit(solution)/shard_map/all_to_all | solution.py:126
  111.7 0.9 fusion.18
  (76 shorter events, 5.9 us)
Async XLA Ops:
  0.0 4.5 %copy-start.5 = (s32[1,2]{1,0:T(1,128)S(1)}, s32[1,2]{1,0:T(1,128)}, u32[]{:S(2)}) copy-start(s32[1,2]{1,0:T(1,128)} %param.13) | copy-start | bytes 28
  0.0 5.8 %copy-start.4 = (bf16[2,1,16,576]{3,2,1,0:T(8,128)(2,1)S(1)}, bf16[2,1,16,576]{3,2,1,0:T(8,128)(2,1)}, u32[]{:S(2)}) copy-start(bf16[2,1,16,576]{3,2,1,0:T(8,128)(2,1)} %param.7) | copy-start | bytes 110596
  2.6 33.9 %collective-permute-start = (bf16[1024,576]{0,1:T(8,128)(2,1)S(1)}, bf16[1024,576]{0,1:T(8,128)(2,1)}, u32[]{:S(2)}, u32[]{:S(2)}) collective-permute-start(bf16[1024,576]{0,1:T(8,128)(2,1)S(1)} %pad_maximum_fusion), channel_id=1, source_target_pairs={{0,8},{8,0},{1,9},{9,1},{2,10},{10,2},{3,11},{11,3},{4,12},{12,4},... | collective-permute-start | bytes 3538952 | tf_op jit(solution)/shard_map/ppermute | solution.py:99
  29.3 22.4 %all-to-all-start.1 = ((bf16[4,8,160,128]{3,2,1,0:T(8,128)(2,1)}), bf16[4,8,160,128]{3,2,1,0:T(8,128)(2,1)S(1)}, u32[]{:S(2)}, u32[]{:S(2)}) async-start(bf16[4,8,160,128]{3,2,1,0:T(8,128)(2,1)} %broadcast_in_dim.110), calls=%async_computation.1 | async-start | bytes 2621440 | tf_op jit(solution)/shard_map/all_to_all | solution.py:90
  33.6 6.1 %copy-start.1 = (bf16[1,8,64,576]{3,2,1,0:T(8,128)(2,1)S(1)}, bf16[1,8,64,576]{3,2,1,0:T(8,128)(2,1)}, u32[]{:S(2)}) copy-start(bf16[1,8,64,576]{3,2,1,0:T(8,128)(2,1)} %param.9) | copy-start | bytes 1769476
  33.6 29.0 %collective-permute-start.1 = (s32[1]{0:T(128)}, s32[1]{0:T(128)}, u32[]{:S(2)}, u32[]{:S(2)}) collective-permute-start(s32[1]{0:T(128)} %param.11), channel_id=1, source_target_pairs={{0,8},{8,0},{1,9},{9,1},{2,10},{10,2},{3,11},{11,3},{4,12},{12,4},... | collective-permute-start | bytes 20 | tf_op jit(solution)/shard_map/ppermute | solution.py:99
  58.6 1.1 copy-start.2
  58.6 1.2 %copy-start.3 = (bf16[512,576]{0,1:T(8,128)(2,1)S(1)}, bf16[512,576]{0,1:T(8,128)(2,1)}, u32[]{:S(2)}) copy-start(bf16[512,576]{0,1:T(8,128)(2,1)} %get-tuple-element.16) | copy-start | bytes 1769476
  67.4 5.0 %copy-start = (bf16[64,64,576]{2,1,0:T(8,128)(2,1)S(1)}, bf16[64,64,576]{2,1,0:T(8,128)(2,1)}, u32[]{:S(2)}) copy-start(bf16[64,64,576]{2,1,0:T(8,128)(2,1)} %gather_fusion) | copy-start | bytes 14155780
  67.4 5.0 %copy-start.7 = (f32[32,32,512]{2,1,0:T(8,128)S(1)}, f32[32,32,512]{2,1,0:T(8,128)}, u32[]{:S(2)}) copy-start(f32[32,32,512]{2,1,0:T(8,128)} %fusion.4) | copy-start | bytes 6291460
  74.4 5.1 %copy-start.6 = (bf16[2,1,576]{2,0,1:T(2,128)(2,1)S(1)}, bf16[2,1,576]{2,0,1:T(2,128)(2,1)}, u32[]{:S(2)}) copy-start(bf16[2,1,576]{2,0,1:T(2,128)(2,1)} %param.10) | copy-start | bytes 6916
  75.5 34.8 %all-to-all-start.2 = ((bf16[32,144,128]{2,1,0:T(8,128)(2,1)}), bf16[32,144,128]{2,1,0:T(8,128)(2,1)S(1)}, u32[]{:S(2)}, u32[]{:S(2)}) async-start(bf16[32,144,128]{2,1,0:T(8,128)(2,1)} %pad_maximum_fusion.3), calls=%async_computation.2 | async-start | bytes 2359296 | tf_op jit(solution)/shard_map/all_to_all | solution.py:126

commit v8 on v3

--- a/solution.py
+++ b/solution.py
@@ -61,15 +61,12 @@
     meta = jnp.where(lane == 0, parent[0], jnp.where(lane == 1, fork_pages[0, 0], fork_pages[0, 1]))
     meta = jnp.where(first & (lane < 3), meta, 0).astype(jnp.bfloat16)
     packed = jnp.concatenate([queries.reshape(q_rows, LANES), meta], axis=0)
-    along_y = lax.all_to_all(
-        jnp.broadcast_to(packed[None], (lax.axis_size("cy"),) + packed.shape), "cy", 0, 0, tiled=True
-    )
-    gathered = lax.all_to_all(
-        jnp.broadcast_to(along_y[None], (lax.axis_size("cx"),) + along_y.shape), "cx", 0, 0, tiled=True
-    ).reshape((chips,) + packed.shape)
-    rows = gathered[:, :q_rows].reshape(chips, steps_n * head_dev, width)
-    meta_all = gathered[:, q_rows, :3].astype(jnp.int32)
-    par, fp0, fp1 = meta_all[:, 0], meta_all[:, 1], meta_all[:, 2]
+    x_n, y_n = lax.axis_size("cx"), lax.axis_size("cy")
+    x_me = lax.axis_index("cx")
+    along_y = lax.all_to_all(jnp.broadcast_to(packed[None], (y_n,) + packed.shape), "cy", 0, 0, tiled=True)
+    along_x = lax.all_to_all(jnp.broadcast_to(along_y[None], (x_n,) + along_y.shape), "cx", 0, 0, tiled=True)
+    others = (x_me + 1 + jnp.arange(x_n - 1, dtype=jnp.int32)) % x_n
+    far = jnp.take(along_x, others, axis=0).reshape(((x_n - 1) * y_n,) + packed.shape)
 
     own_suffix = suffix_cache.reshape(suffix_n, width)
     local_keys = jnp.concatenate([prompt_cache, own_suffix], axis=0)
@@ -78,26 +75,41 @@
 
     position = jnp.arange(suffix_n, dtype=jnp.int32)
     page = position // page_len
+    ones = jnp.ones((prompt_n,), jnp.float32)
 
-    def fork_count(owner, length):
-        hits = (page[None, :] == fp0[:, None]).astype(jnp.float32) + (page[None, :] == fp1[:, None]).astype(
-            jnp.float32
+    def partials(block):
+        n = block.shape[0]
+        rows = block[:, :q_rows].reshape(n, steps_n * head_dev, width)
+        meta_all = block[:, q_rows, :3].astype(jnp.int32)
+        par, fp0, fp1 = meta_all[:, 0], meta_all[:, 1], meta_all[:, 2]
+
+        def fork_count(owner, length):
+            hits = (page[None, :] == fp0[:, None]).astype(jnp.float32) + (
+                page[None, :] == fp1[:, None]
+            ).astype(jnp.float32)
+            keep = (par == owner)[:, None] & (position < length)[None, :]
+            return jnp.where(keep, hits, 0.0)
+
+        full = jnp.broadcast_to(ones[None], (n, prompt_n))
+        mult = jnp.concatenate(
+            [full, fork_count(my_beam, suffix_len[0]), full, fork_count(partner_beam, partner_len[0])], axis=1
         )
-        keep = (par == owner)[:, None] & (position < length)[None, :]
-        return jnp.where(keep, hits, 0.0)
+        top, total, summed = masked_softmax(rows, keys, mult)
+        return (summed / total[..., None]).astype(jnp.bfloat16), top, total
 
-    ones = jnp.ones((chips, prompt_n), jnp.float32)
-    mult = jnp.concatenate(
-        [ones, fork_count(my_beam, suffix_len[0]), ones, fork_count(partner_beam, partner_len[0])], axis=1
-    )
-    top, total, summed = masked_softmax(rows, keys, mult)
-    out = (summed / total[..., None]).astype(jnp.bfloat16)
+    near_out, near_top, near_total = partials(along_y)
+    far_out, far_top, far_total = partials(far)
+    out = jnp.concatenate([near_out, far_out], axis=0)
+    top = jnp.concatenate([near_top, far_top], axis=0)
+    total = jnp.concatenate([near_total, far_total], axis=0)
 
     out_rows = out.reshape(chips, -1, LANES)
     parts = jnp.stack(split3(top) + split3(total), axis=1).reshape(chips, -1)
     stat_rows = -(-parts.shape[1] // (META_ROWS * LANES)) * META_ROWS
     parts = jnp.pad(parts, ((0, 0), (0, stat_rows * LANES - parts.shape[1])))
     payload = jnp.concatenate([out_rows, parts.reshape(chips, stat_rows, LANES)], axis=1)
+    unroll = (jnp.arange(x_n, dtype=jnp.int32) - x_me) % x_n
+    payload = jnp.take(payload.reshape((x_n, y_n) + payload.shape[1:]), unroll, axis=0).reshape(payload.shape)
     arrived = lax.all_to_all(payload, ("cx", "cy"), 0, 0, tiled=True)
     n_out = out_rows.shape[1]
     row_n = steps_n * head_dev

time: 99 us -> 120 us (1.21); the launches traced: 98 us -> 118 us
  local copies, waits for them, and re-layouts: 9.17 us -> 24.4 us
  waiting for transfers between devices: 47.7 us -> 42.8 us
  matrix products: 9.23 us -> 14 us
  other arithmetic: 11.2 us -> 13.9 us
  starting transfers between devices: 19.2 us -> 20.9 us
    slice x2 -> x4, local copies, waits for them, and re-layouts: 0.09 us -> 7.62 us  [the longest x3 7.62 us: partials(): rows = block[:, :q_rows].reshape(n, steps_n * head_dev, width)]
    gather x0 -> x3, local copies, waits for them, and re-layouts: none -> 5.68 us  [the longest x2 4.9 us: on_device(): jnp.take(along_x, others, axis=0).reshape(((x_n - 1) * y_n,) + packed.shape)]
    all_to_all x2, waiting for transfers between devices: 18.4 us -> 13 us  [the longest x1 8.26 us: on_device(): lax.all_to_all(jnp.broadcast_to(along_y[None], (x_n,) + along_y.shape), '...]
    select_n x0 -> x4, other arithmetic: none -> 4.22 us  [the longest x2 2.95 us: on_device(): jnp.take(along_x, others, axis=0).reshape(((x_n - 1) * y_n,) + packed.shape)]
    dot_general x1 -> x2, matrix products: 2.48 us -> 6.17 us  [masked_softmax(): jnp.einsum('gqt,td->gqd', rounded, keys[:, :DL], preferred_element_type=j...]
    unnamed x17 -> x22, local copies, waits for them, and re-layouts: 0.21 us -> 2.84 us
    reshape x2, local copies, waits for them, and re-layouts: 2.62 us -> 1.02 us  [partials(): rows = block[:, :q_rows].reshape(n, steps_n * head_dev, width)]
    concatenate x1, other arithmetic: 3.02 us -> 1.59 us  [on_device(): keys = jnp.concatenate([local_keys, partner_keys], axis=0)]
  transfers between devices with their start and end apart: 5 -> 5, of which waited for: 4 -> 3; matrix products, arithmetic and copies ran while one was open for 8% -> 10% of each run, Pallas kernels for 0% -> 0%
where the time goes in v8:
time: 120 us; the launch traced here: 118 us
  waiting for transfers between devices  42.8 us (36%)
  local copies, waits for them, and re-layouts  24.4 us (20%)
  starting transfers between devices  20.9 us (17%)
  matrix products  14 us (12%)
  other arithmetic  13.9 us (12%)
  between operations  1.8 us (2%)
    all_to_all x1, waiting for transfers between devices, on_device(): arrived = lax.all_to_all(payload, ('cx', 'cy'), 0, 0, tiled=True)  29.8 us
    all_to_all x1, waiting for transfers between devices, on_device(): lax.all_to_all(jnp.broadcast_to(along_y[None], (x_n,) + along_y.shape), '...  8.26 us
    slice x3, local copies, waits for them, and re-layouts, partials(): rows = block[:, :q_rows].reshape(n, steps_n * head_dev, width)  7.62 us
    all_to_all x1, starting transfers between devices, on_device(): lax.all_to_all(jnp.broadcast_to(packed[None], (y_n,) + packed.shape), 'cy...  7.1 us
    dot_general x2, matrix products, masked_softmax(): jnp.einsum('gqk,tk->gqt', rows, keys, preferred_element_type=jnp.float32)  6.57 us
    dot_general x2, matrix products, masked_softmax(): jnp.einsum('gqt,td->gqd', rounded, keys[:, :DL], preferred_element_type=j...  6.17 us
    all_to_all x1, starting transfers between devices, on_device(): arrived = lax.all_to_all(payload, ('cx', 'cy'), 0, 0, tiled=True)  5.16 us
    gather x2, local copies, waits for them, and re-layouts, on_device(): jnp.take(along_x, others, axis=0).reshape(((x_n - 1) * y_n,) + packed.shape)  4.9 us
  transfers between devices with their start and end apart: 5, of which 3 were waited for; matrix products, arithmetic and copies ran while one was open for 10% of the time, Pallas kernels for 0%

profile of v8, /device:TPU:448, one launch (start us, length us, event | category | flops | bytes accessed | tf_op | source)
XLA Modules:
  0.0 117.8 jit_solution(12760144789838958765)
XLA Ops:
  0.0 1.3 %fusion.73 = (s32[1,1]{1,0:T(1,128)}, s32[1,1]{1,0:T(1,128)}) fusion(s32[1,2]{1,0:T(1,128)} %param.13), kind=kLoop, calls=%fused_computation.164 | loop fusion | bytes 16 | tf_op jit(solution)/shard_map/slice | solution.py:61
  2.9 1.3 %compare_select_fusion.12 = s32[128]{0:T(128)S(1)} fusion(s32[]{:T(128)} %bitcast.2, s32[]{:T(128)} %bitcast.1), kind=kLoop, calls=%fused_computation.132 | loop fusion | flops 256 | bytes 520 | tf_op jit(solution)/shard_map/jit(_where)/select_n | solution.py:61
  5.0 7.1 %all-to-all-start = ((bf16[8,160,128]{2,1,0:T(8,128)(2,1)}), bf16[8,160,128]{2,1,0:T(8,128)(2,1)S(1)}, u32[]{:S(2)}, u32[]{:S(2)}) async-start(bf16[8,160,128]{2,1,0:T(8,128)(2,1)} %broadcast_in_dim.160), calls=%async_computation | async-start | bytes 655360 | tf_op jit(solution)/shard_map/all_to_all | solution.py:66
  12.1 1.9 %collective-permute-start = (s32[1]{0:T(128)}, s32[1]{0:T(128)}, u32[]{:S(2)}, u32[]{:S(2)}) collective-permute-start(s32[1]{0:T(128)} %param.11), channel_id=1, source_target_pairs={{0,8},{8,0},{1,9},{9,1},{2,10},{10,2},{3,11},{11,3},{4,12},{12,4},... | collective-permute-start | bytes 20 | tf_op jit(solution)/shard_map/ppermute | solution.py:73
  14.0 1.3 %copy.64 = bf16[512,576]{0,1:T(8,128)(2,1)S(1)} copy(bf16[512,576]{1,0:T(8,128)(2,1)} %bitcast.102) | data formatting | bytes 1179648 | tf_op jit(solution)/shard_map/reshape | solution.py:71
  16.6 2.4 %collective-permute-start.1 = (bf16[1024,576]{0,1:T(8,128)(2,1)}, bf16[1024,576]{0,1:T(8,128)(2,1)}, u32[]{:S(2)}, u32[]{:S(2)}) collective-permute-start(bf16[1024,576]{0,1:T(8,128)(2,1)} %pad_maximum_fusion.1), channel_id=1, source_target_pairs={{0,8},{8,0},{1,9},{9,1},{2,10},{10,2},{3,11},{11,3},{4,12},{12,4},... | collective-permute-start | bytes 3538952 | tf_op jit(solution)/shard_map/ppermute | solution.py:73
  20.7 4.7 %all-to-all-done = bf16[8,160,128]{2,1,0:T(8,128)(2,1)S(1)} async-done(((bf16[8,160,128]{2,1,0:T(8,128)(2,1)}), bf16[8,160,128]{2,1,0:T(8,128)(2,1)S(1)}, u32[]{:S(2)}, u32[]{:S(2)}) %all-to-all-start) | async-done | bytes 327712 | tf_op jit(solution)/shard_map/all_to_all | solution.py:66
  25.4 1.3 %broadcast_in_dim.168 = bf16[4,8,160,128]{3,2,1,0:T(8,128)(2,1)} broadcast(bf16[8,160,128]{2,1,0:T(8,128)(2,1)S(1)} %all-to-all-done), dimensions={1,2,3} | broadcast | bytes 1638400 | tf_op jit(solution)/shard_map/broadcast_in_dim | solution.py:67
  26.7 4.3 %all-to-all-start.1 = ((bf16[4,8,160,128]{3,2,1,0:T(8,128)(2,1)}), bf16[4,8,160,128]{3,2,1,0:T(8,128)(2,1)S(1)}, u32[]{:S(2)}, u32[]{:S(2)}) async-start(bf16[4,8,160,128]{3,2,1,0:T(8,128)(2,1)} %broadcast_in_dim.168), calls=%async_computation.1 | async-start | bytes 2621440 | tf_op jit(solution)/shard_map/all_to_all | solution.py:67
  31.5 2.4 %select_reduce_fusion.1 = (f32[8,32]{1,0:T(8,128)S(1)}, f32[8,32,2048]{2,1,0:T(8,128)S(1)}) fusion(pred[8,2048]{1,0:T(8,128)(4,1)S(1)} %broadcast_compare_fusion.1, bf16[8,32,576]{2,1,0:T(8,128)(2,1)S(1)} %reshape.767, bf16[1024,576]{0,1:T(8,128)(2,1)} %collective-permute-done.1, bf16[512,576]{0,1:T(8,128)(2,1)S(1)} %copy.64, bf16[512,576]{0,1:T(8,128)(2,1)S(1)} %copy-done.1), kind=kOutput, calls=%fused_computation.22 | convolution fusion | flops 612630272 | bytes 4768768 | tf_op jit(solution)/shard_map/gqk,tk->gqt/dot_general | solution.py:16
  34.6 1.6 %pad_maximum_fusion = bf16[2048,576]{0,1:T(8,128)(2,1)S(1)} fusion(bf16[1024,576]{0,1:T(8,128)(2,1)} %collective-permute-done.1, bf16[512,576]{0,1:T(8,128)(2,1)S(1)} %copy.64, bf16[512,576]{0,1:T(8,128)(2,1)S(1)} %copy-done.1), kind=kLoop, calls=%fused_computation.14 | loop fusion | flops 7077888 | bytes 4718592 | tf_op jit(solution)/shard_map/concatenate | solution.py:74
  36.2 1.4 %copy-done.2 = bf16[2048,576]{0,1:T(8,128)(2,1)} copy-done((bf16[2048,576]{0,1:T(8,128)(2,1)}, bf16[2048,576]{0,1:T(8,128)(2,1)S(1)}, u32[]{:S(2)}) %copy-start.2) | copy-done | bytes 2359320
  37.6 1.5 %fusion.15 = bf16[8,32,512]{2,1,0:T(8,128)(2,1)} fusion(bf16[2048,576]{0,1:T(8,128)(2,1)S(1)} %pad_maximum_fusion, f32[8,32,2048]{2,1,0:T(8,128)S(1)} %get-tuple-element.33, f32[8,32]{1,0:T(8,128)S(1)} %get-tuple-element.32, pred[8,2048]{1,0:T(8,128)(4,1)S(1)} %broadcast_compare_fusion.1, bf16[8,2048]{1,0:T(8,128)(2,1)S(1)} %fusion.67, ...), kind=kOutput, calls=%fused_computation.31 | convolution fusion | flops 539230208 | bytes 4513792 | tf_op jit(solution)/shard_map/gqt,td->gqd/dot_general | solution.py:23
  39.1 8.3 %all-to-all-done.1 = bf16[4,8,160,128]{3,2,1,0:T(8,128)(2,1)S(1)} async-done(((bf16[4,8,160,128]{3,2,1,0:T(8,128)(2,1)}), bf16[4,8,160,128]{3,2,1,0:T(8,128)(2,1)S(1)}, u32[]{:S(2)}, u32[]{:S(2)}) %all-to-all-start.1) | async-done | bytes 1310752 | tf_op jit(solution)/shard_map/all_to_all | solution.py:67
  48.1 4.2 %copy.66 = bf16[24,160,128]{0,1,2:T(8,128)(2,1)} copy(bf16[24,160,128]{2,1,0:T(8,128)(2,1)S(1)} %bitcast.101) | data formatting | bytes 1966080 | tf_op jit(solution)/shard_map/jit(_take)/gather | solution.py:69
  52.3 2.9 %broadcast_select_fusion = bf16[24,160,128]{0,1,2:T(8,128)(2,1)S(1)} fusion(bf16[24,160,128]{0,1,2:T(8,128)(2,1)} %copy.66, pred[24]{0:T(512)(128)(4,1)S(1)} %broadcast_in_dim.166), kind=kLoop, calls=%fused_computation.5 | loop fusion | flops 491520 | bytes 1966104 | tf_op jit(solution)/shard_map/jit(_take)/select_n | solution.py:69
  55.3 2.4 %slice.101 = bf16[24,144,128]{0,1,2:T(8,128)(2,1)} slice(bf16[24,160,128]{0,1,2:T(8,128)(2,1)S(1)} %broadcast_select_fusion), slice={[0:24], [0:144], [0:128]} | slice | bytes 1769472 | tf_op jit(solution)/shard_map/slice | solution.py:82
  58.5 5.2 %copy.67 = bf16[24,144,128]{2,1,0:T(8,128)(2,1)S(1)} copy(bf16[24,144,128]{0,1,2:T(8,128)(2,1)} %slice.101) | data formatting | bytes 1769472 | tf_op jit(solution)/shard_map/slice | solution.py:82
  64.5 4.2 %select_reduce_fusion = (f32[24,32]{1,0:T(8,128)S(1)}, f32[24,32,2048]{2,1,0:T(8,128)S(1)}) fusion(pred[24,2048]{1,0:T(8,128)(4,1)S(1)} %broadcast_compare_fusion, bf16[24,32,576]{2,1,0:T(8,128)(2,1)S(1)} %reshape.769, bf16[1024,576]{0,1:T(8,128)(2,1)} %collective-permute-done.1, bf16[512,576]{0,1:T(8,128)(2,1)S(1)} %copy.64, bf16[512,576]{0,1:T(8,128)(2,1)S(1)} %copy-done.1), kind=kOutput, calls=%fused_computation.4 | convolution fusion | flops 1823735040 | bytes 9587712 | tf_op jit(solution)/shard_map/gqk,tk->gqt/dot_general | solution.py:16
  68.7 2.0 %multiply_reduce_fusion = f32[24,32]{1,0:T(8,128)S(1)} fusion(f32[24,32,2048]{2,1,0:T(8,128)S(1)} %get-tuple-element.31, f32[24,2048]{1,0:T(8,128)S(1)} %pad_maximum_fusion.5, f32[24,32]{1,0:T(8,128)S(1)} %get-tuple-element.30, pred[24,2048]{1,0:T(8,128)(4,1)S(1)} %broadcast_compare_fusion), kind=kLoop, calls=%fused_computation.2 | loop fusion | flops 7863552 | bytes 6543360 | tf_op jit(solution)/shard_map/reduce_sum | solution.py:21
  72.1 4.7 %divide_convert_fusion = bf16[24,32,512]{2,1,0:T(8,128)(2,1)S(1)} fusion(f32[24,32]{1,0:T(8,128)S(1)} %multiply_reduce_fusion, bf16[2048,576]{0,1:T(8,128)(2,1)S(1)} %copy-done.3, f32[24,32,2048]{2,1,0:T(8,128)} %copy-done, f32[24,32]{1,0:T(8,128)S(1)} %get-tuple-element.30, pred[24,2048]{1,0:T(8,128)(4,1)S(1)} %broadcast_compare_fusion, ...), kind=kOutput, calls=%fused_computation.25 | convolution fusion | flops 1619263488 | bytes 9347072 | tf_op jit(solution)/shard_map/gqt,td->gqd/dot_general | solution.py:23
  78.6 1.3 %bitcast_select_fusion = bf16[32,144,128]{2,1,0:T(8,128)(2,1)} fusion(bf16[4,8,144,128]{3,2,1,0:T(8,128)(2,1)S(1)} %gather_fusion.1, pred[32]{0:T(512)(128)(4,1)S(1)} %broadcast_in_dim.155), kind=kLoop, calls=%fused_computation.29 | loop fusion | flops 589824 | bytes 2359328 | tf_op jit(solution)/shard_map/jit(_take)/select_n | solution.py:112
  79.8 5.2 %all-to-all-start.2 = ((bf16[32,144,128]{2,1,0:T(8,128)(2,1)}), bf16[32,144,128]{2,1,0:T(8,128)(2,1)S(1)}, u32[]{:S(2)}, u32[]{:S(2)}) async-start(bf16[32,144,128]{2,1,0:T(8,128)(2,1)} %bitcast_select_fusion), calls=%async_computation.2 | async-start | bytes 2359296 | tf_op jit(solution)/shard_map/all_to_all | solution.py:113
  85.7 29.8 %all-to-all-done.2 = bf16[32,144,128]{2,1,0:T(8,128)(2,1)S(1)} async-done(((bf16[32,144,128]{2,1,0:T(8,128)(2,1)}), bf16[32,144,128]{2,1,0:T(8,128)(2,1)S(1)}, u32[]{:S(2)}, u32[]{:S(2)}) %all-to-all-start.2) | async-done | bytes 1179680 | tf_op jit(solution)/shard_map/all_to_all | solution.py:113
  (100 shorter events, 13.5 us)
Async XLA Ops:
  0.0 15.3 %copy-start.1 = (bf16[512,576]{0,1:T(8,128)(2,1)S(1)}, bf16[512,576]{0,1:T(8,128)(2,1)}, u32[]{:S(2)}) copy-start(bf16[512,576]{0,1:T(8,128)(2,1)} %param.8) | copy-start | bytes 1769476
  5.0 20.4 %all-to-all-start = ((bf16[8,160,128]{2,1,0:T(8,128)(2,1)}), bf16[8,160,128]{2,1,0:T(8,128)(2,1)S(1)}, u32[]{:S(2)}, u32[]{:S(2)}) async-start(bf16[8,160,128]{2,1,0:T(8,128)(2,1)} %broadcast_in_dim.160), calls=%async_computation | async-start | bytes 655360 | tf_op jit(solution)/shard_map/all_to_all | solution.py:66
  12.1 7.9 %collective-permute-start = (s32[1]{0:T(128)}, s32[1]{0:T(128)}, u32[]{:S(2)}, u32[]{:S(2)}) collective-permute-start(s32[1]{0:T(128)} %param.11), channel_id=1, source_target_pairs={{0,8},{8,0},{1,9},{9,1},{2,10},{10,2},{3,11},{11,3},{4,12},{12,4},... | collective-permute-start | bytes 20 | tf_op jit(solution)/shard_map/ppermute | solution.py:73
  16.6 15.0 %collective-permute-start.1 = (bf16[1024,576]{0,1:T(8,128)(2,1)}, bf16[1024,576]{0,1:T(8,128)(2,1)}, u32[]{:S(2)}, u32[]{:S(2)}) collective-permute-start(bf16[1024,576]{0,1:T(8,128)(2,1)} %pad_maximum_fusion.1), channel_id=1, source_target_pairs={{0,8},{8,0},{1,9},{9,1},{2,10},{10,2},{3,11},{11,3},{4,12},{12,4},... | collective-permute-start | bytes 3538952 | tf_op jit(solution)/shard_map/ppermute | solution.py:73
  26.7 20.7 %all-to-all-start.1 = ((bf16[4,8,160,128]{3,2,1,0:T(8,128)(2,1)}), bf16[4,8,160,128]{3,2,1,0:T(8,128)(2,1)S(1)}, u32[]{:S(2)}, u32[]{:S(2)}) async-start(bf16[4,8,160,128]{3,2,1,0:T(8,128)(2,1)} %broadcast_in_dim.168), calls=%async_computation.1 | async-start | bytes 2621440 | tf_op jit(solution)/shard_map/all_to_all | solution.py:67
  36.2 1.4 %copy-start.2 = (bf16[2048,576]{0,1:T(8,128)(2,1)}, bf16[2048,576]{0,1:T(8,128)(2,1)S(1)}, u32[]{:S(2)}) copy-start(bf16[2048,576]{0,1:T(8,128)(2,1)S(1)} %pad_maximum_fusion) | copy-start | bytes 7077892
  68.6 3.0 %copy-start = (f32[24,32,2048]{2,1,0:T(8,128)}, f32[24,32,2048]{2,1,0:T(8,128)S(1)}, u32[]{:S(2)}) copy-start(f32[24,32,2048]{2,1,0:T(8,128)S(1)} %get-tuple-element.31) | copy-start | bytes 18874372
  68.7 3.4 %copy-start.3 = (bf16[2048,576]{0,1:T(8,128)(2,1)S(1)}, bf16[2048,576]{0,1:T(8,128)(2,1)}, u32[]{:S(2)}) copy-start(bf16[2048,576]{0,1:T(8,128)(2,1)} %copy-done.2) | copy-start | bytes 7077892
  68.7 3.4 %copy-start.6 = (bf16[24,2048]{1,0:T(8,128)(2,1)S(1)}, bf16[24,2048]{1,0:T(8,128)(2,1)}, u32[]{:S(2)}) copy-start(bf16[24,2048]{1,0:T(8,128)(2,1)} %fusion.68) | copy-start | bytes 294916
  72.1 4.7 %copy-start.5 = (bf16[8,32,512]{2,1,0:T(8,128)(2,1)S(1)}, bf16[8,32,512]{2,1,0:T(8,128)(2,1)}, u32[]{:S(2)}) copy-start(bf16[8,32,512]{2,1,0:T(8,128)(2,1)} %fusion.15) | copy-start | bytes 786436
  78.5 6.5 %copy-start.4 = (bf16[1,8,64,576]{3,2,1,0:T(8,128)(2,1)S(1)}, bf16[1,8,64,576]{3,2,1,0:T(8,128)(2,1)}, u32[]{:S(2)}) copy-start(bf16[1,8,64,576]{3,2,1,0:T(8,128)(2,1)} %param.9) | copy-start | bytes 1769476
  78.5 6.5 %copy-start.7 = (bf16[2,1,16,576]{3,2,1,0:T(8,128)(2,1)S(1)}, bf16[2,1,16,576]{3,2,1,0:T(8,128)(2,1)}, u32[]{:S(2)}) copy-start(bf16[2,1,16,576]{3,2,1,0:T(8,128)(2,1)} %param.7) | copy-start | bytes 110596
  78.5 6.5 %copy-start.8 = (bf16[2,1,576]{2,0,1:T(2,128)(2,1)S(1)}, bf16[2,1,576]{2,0,1:T(2,128)(2,1)}, u32[]{:S(2)}) copy-start(bf16[2,1,576]{2,0,1:T(2,128)(2,1)} %param.10) | copy-start | bytes 6916
  79.8 35.8 %all-to-all-start.2 = ((bf16[32,144,128]{2,1,0:T(8,128)(2,1)}), bf16[32,144,128]{2,1,0:T(8,128)(2,1)S(1)}, u32[]{:S(2)}, u32[]{:S(2)}) async-start(bf16[32,144,128]{2,1,0:T(8,128)(2,1)} %bitcast_select_fusion), calls=%async_computation.2 | async-start | bytes 2359296 | tf_op jit(solution)/shard_map/all_to_all | solution.py:113

commit v9 on v3

--- a/solution.py
+++ b/solution.py
@@ -56,10 +56,8 @@
     partner_beam = chip * 2 + (1 - core)
 
     q_rows = steps_n * head_dev * width // LANES
-    lane = lax.broadcasted_iota(jnp.int32, (META_ROWS, LANES), 1)
-    first = lax.broadcasted_iota(jnp.int32, (META_ROWS, LANES), 0) == 0
-    meta = jnp.where(lane == 0, parent[0], jnp.where(lane == 1, fork_pages[0, 0], fork_pages[0, 1]))
-    meta = jnp.where(first & (lane < 3), meta, 0).astype(jnp.bfloat16)
+    meta = jnp.concatenate([parent, fork_pages.reshape(-1)]).astype(jnp.bfloat16)
+    meta = jnp.pad(meta, (0, META_ROWS * LANES - meta.shape[0])).reshape(META_ROWS, LANES)
     packed = jnp.concatenate([queries.reshape(q_rows, LANES), meta], axis=0)
     along_y = lax.all_to_all(
         jnp.broadcast_to(packed[None], (lax.axis_size("cy"),) + packed.shape), "cy", 0, 0, tiled=True

time: 99 us -> 97 us (0.980)
  local copies, waits for them, and re-layouts: 9.17 us -> 7.86 us
    slice x1 -> x0, local copies, waits for them, and re-layouts: 1.34 us -> none  [on_device(): fork_pages[0, 0]]
    select_n x1 -> x0, other arithmetic: 1.26 us -> none  [on_device(): jnp.where(lane == 1, fork_pages[0, 0], fork_pages[0, 1])]
where the time goes in v9:
time: 97 us; the launch traced here: 96.1 us
  waiting for transfers between devices  47.6 us (49%)
  starting transfers between devices  19.2 us (20%)
  other arithmetic  10.6 us (11%)
  matrix products  9.22 us (10%)
  local copies, waits for them, and re-layouts  7.86 us (8%)
  between operations  1.65 us (2%)
    all_to_all x1, waiting for transfers between devices, on_device(): arrived = lax.all_to_all(payload, ('cx', 'cy'), 0, 0, tiled=True)  28.6 us
    all_to_all x1, waiting for transfers between devices, on_device(): lax.all_to_all(jnp.broadcast_to(along_y[None], (lax.axis_size('cx'),) + a...  9.63 us
    all_to_all x1, waiting for transfers between devices, on_device(): lax.all_to_all(jnp.broadcast_to(packed[None], (lax.axis_size('cy'),) + pa...  8.85 us
    all_to_all x1, starting transfers between devices, on_device(): lax.all_to_all(jnp.broadcast_to(packed[None], (lax.axis_size('cy'),) + pa...  7.1 us
    dot_general x1, matrix products, masked_softmax(): jnp.einsum('gqk,tk->gqt', rows, keys, preferred_element_type=jnp.float32)  5.44 us
    all_to_all x1, starting transfers between devices, on_device(): lax.all_to_all(jnp.broadcast_to(along_y[None], (lax.axis_size('cx'),) + a...  4.29 us
    all_to_all x1, starting transfers between devices, on_device(): arrived = lax.all_to_all(payload, ('cx', 'cy'), 0, 0, tiled=True)  3.94 us
    ppermute x2, starting transfers between devices, on_device(): lax.ppermute((local_keys, suffix_len), 'core', [(0, 1), (1, 0)])  3.82 us
  transfers between devices with their start and end apart: 5, of which 4 were waited for; matrix products, arithmetic and copies ran while one was open for 8% of the time, Pallas kernels for 0%

profile of v9, /device:TPU:448, one launch (start us, length us, event | category | flops | bytes accessed | tf_op | source)
XLA Modules:
  0.0 96.1 jit_solution(14278003790999004291)
XLA Ops:
  0.0 1.0 reshape.391
  1.6 0.7 convert_bitcast_fusion
  2.4 0.8 broadcast_in_dim.82
  3.1 7.1 %all-to-all-start = ((bf16[8,160,128]{2,1,0:T(8,128)(2,1)}), bf16[8,160,128]{2,1,0:T(8,128)(2,1)S(1)}, u32[]{:S(2)}, u32[]{:S(2)}) async-start(bf16[8,160,128]{2,1,0:T(8,128)(2,1)} %broadcast_in_dim.82), calls=%async_computation | async-start | bytes 655360 | tf_op jit(solution)/shard_map/all_to_all | solution.py:62
  10.2 1.3 %copy.30 = bf16[512,576]{0,1:T(8,128)(2,1)S(1)} copy(bf16[512,576]{1,0:T(8,128)(2,1)} %bitcast.98) | data formatting | bytes 1179648 | tf_op jit(solution)/shard_map/reshape | solution.py:72
  11.6 1.2 %pad_maximum_fusion.1 = bf16[1024,576]{0,1:T(8,128)(2,1)} fusion(bf16[512,576]{0,1:T(8,128)(2,1)S(1)} %copy.30, bf16[512,576]{0,1:T(8,128)(2,1)S(1)} %copy-done), kind=kLoop, calls=%fused_computation.14 | loop fusion | flops 2359296 | bytes 2359296 | tf_op jit(solution)/shard_map/concatenate | solution.py:73
  12.8 1.9 %collective-permute-start.1 = (bf16[1024,576]{0,1:T(8,128)(2,1)}, bf16[1024,576]{0,1:T(8,128)(2,1)}, u32[]{:S(2)}, u32[]{:S(2)}) collective-permute-start(bf16[1024,576]{0,1:T(8,128)(2,1)} %pad_maximum_fusion.1), channel_id=1, source_target_pairs={{0,8},{8,0},{1,9},{9,1},{2,10},{10,2},{3,11},{11,3},{4,12},{12,4},... | collective-permute-start | bytes 3538952 | tf_op jit(solution)/shard_map/ppermute | solution.py:74
  14.7 8.9 %all-to-all-done = bf16[8,160,128]{2,1,0:T(8,128)(2,1)S(1)} async-done(((bf16[8,160,128]{2,1,0:T(8,128)(2,1)}), bf16[8,160,128]{2,1,0:T(8,128)(2,1)S(1)}, u32[]{:S(2)}, u32[]{:S(2)}) %all-to-all-start) | async-done | bytes 327712 | tf_op jit(solution)/shard_map/all_to_all | solution.py:62
  23.5 1.3 %broadcast_in_dim.83 = bf16[4,8,160,128]{3,2,1,0:T(8,128)(2,1)} broadcast(bf16[8,160,128]{2,1,0:T(8,128)(2,1)S(1)} %all-to-all-done), dimensions={1,2,3} | broadcast | bytes 1638400 | tf_op jit(solution)/shard_map/broadcast_in_dim | solution.py:66
  24.8 4.3 %all-to-all-start.1 = ((bf16[4,8,160,128]{3,2,1,0:T(8,128)(2,1)}), bf16[4,8,160,128]{3,2,1,0:T(8,128)(2,1)S(1)}, u32[]{:S(2)}, u32[]{:S(2)}) async-start(bf16[4,8,160,128]{3,2,1,0:T(8,128)(2,1)} %broadcast_in_dim.83), calls=%async_computation.1 | async-start | bytes 2621440 | tf_op jit(solution)/shard_map/all_to_all | solution.py:65
  29.1 1.9 %collective-permute-start = (s32[1]{0:T(128)}, s32[1]{0:T(128)}, u32[]{:S(2)}, u32[]{:S(2)}) collective-permute-start(s32[1]{0:T(128)} %param.11), channel_id=1, source_target_pairs={{0,8},{8,0},{1,9},{9,1},{2,10},{10,2},{3,11},{11,3},{4,12},{12,4},... | collective-permute-start | bytes 20 | tf_op jit(solution)/shard_map/ppermute | solution.py:74
  32.2 0.6 iota_compare_fusion.1
  32.9 3.0 %pad_maximum_fusion = bf16[2048,576]{0,1:T(8,128)(2,1)} fusion(bf16[1024,576]{0,1:T(8,128)(2,1)} %collective-permute-done.1, bf16[512,576]{0,1:T(8,128)(2,1)S(1)} %copy.30, bf16[512,576]{0,1:T(8,128)(2,1)S(1)} %copy-done), kind=kLoop, calls=%fused_computation.7 | loop fusion | flops 7077888 | bytes 4718592 | tf_op jit(solution)/shard_map/concatenate | solution.py:75
  35.9 9.6 %all-to-all-done.1 = bf16[4,8,160,128]{3,2,1,0:T(8,128)(2,1)S(1)} async-done(((bf16[4,8,160,128]{3,2,1,0:T(8,128)(2,1)}), bf16[4,8,160,128]{3,2,1,0:T(8,128)(2,1)S(1)}, u32[]{:S(2)}, u32[]{:S(2)}) %all-to-all-start.1) | async-done | bytes 1310752 | tf_op jit(solution)/shard_map/all_to_all | solution.py:65
  46.0 1.9 %reshape.395 = bf16[32,32,576]{2,1,0:T(8,128)(2,1)} reshape(bf16[32,144,128]{2,1,0:T(8,128)(2,1)S(1)} %slice.65) | data formatting | bytes 2359296 | tf_op jit(solution)/shard_map/reshape | solution.py:68
  47.9 5.4 %select_reduce_fusion = (f32[32,32]{1,0:T(8,128)S(1)}, f32[32,32,2048]{2,1,0:T(8,128)S(1)}) fusion(pred[32,2048]{1,0:T(8,128)(4,1)S(1)} %broadcast_compare_fusion, bf16[32,32,576]{2,1,0:T(8,128)(2,1)} %reshape.395, bf16[1024,576]{0,1:T(8,128)(2,1)} %collective-permute-done.1, bf16[512,576]{0,1:T(8,128)(2,1)S(1)} %copy.30, bf16[512,576]{0,1:T(8,128)(2,1)S(1)} %copy-done.1), kind=kOutput, calls=%fused_computation.2 | convolution fusion | flops 2429287424 | bytes 11997184 | tf_op jit(solution)/shard_map/gqk,tk->gqt/dot_general | solution.py:16
  53.4 2.7 %multiply_reduce_fusion = f32[32,32]{1,0:T(8,128)S(1)} fusion(f32[32,32,2048]{2,1,0:T(8,128)S(1)} %get-tuple-element.23, f32[32,2048]{1,0:T(8,128)S(1)} %pad_maximum_fusion.4, f32[32,32]{1,0:T(8,128)S(1)} %get-tuple-element.22, pred[32,2048]{1,0:T(8,128)(4,1)S(1)} %broadcast_compare_fusion), kind=kLoop, calls=%fused_computation | loop fusion | flops 10484736 | bytes 8724480 | tf_op jit(solution)/shard_map/reduce_sum | solution.py:21
  56.0 2.5 %divide_convert_fusion = bf16[32,32,512]{2,1,0:T(8,128)(2,1)S(1)} fusion(f32[32,32]{1,0:T(8,128)S(1)} %multiply_reduce_fusion, bf16[2048,576]{0,1:T(8,128)(2,1)S(1)} %copy-done.2, f32[32,32,2048]{2,1,0:T(8,128)S(1)} %get-tuple-element.23, f32[32,32]{1,0:T(8,128)S(1)} %get-tuple-element.22, pred[32,2048]{1,0:T(8,128)(4,1)S(1)} %broadcast_compare_fusion, ...), kind=kOutput, calls=%fused_computation.12 | convolution fusion | flops 2159017984 | bytes 11763712 | tf_op jit(solution)/shard_map/gqt,td->gqd/dot_general | solution.py:23
  58.5 0.7 reshape.397
  59.5 1.1 %pad_maximum_fusion.2 = bf16[32,144,128]{2,1,0:T(8,128)(2,1)} fusion(bf16[32,16,128]{2,1,0:T(8,128)(2,1)S(1)} %bitcast.101, bf16[32,128,128]{2,1,0:T(8,128)(2,1)S(1)} %reshape.397), kind=kLoop, calls=%fused_computation.15 | loop fusion | flops 2359296 | bytes 2359296 | tf_op jit(solution)/shard_map/concatenate | solution.py:98
  60.6 3.9 %all-to-all-start.2 = ((bf16[32,144,128]{2,1,0:T(8,128)(2,1)}), bf16[32,144,128]{2,1,0:T(8,128)(2,1)S(1)}, u32[]{:S(2)}, u32[]{:S(2)}) async-start(bf16[32,144,128]{2,1,0:T(8,128)(2,1)} %pad_maximum_fusion.2), calls=%async_computation.2 | async-start | bytes 2359296 | tf_op jit(solution)/shard_map/all_to_all | solution.py:99
  65.3 28.6 %all-to-all-done.2 = bf16[32,144,128]{2,1,0:T(8,128)(2,1)S(1)} async-done(((bf16[32,144,128]{2,1,0:T(8,128)(2,1)}), bf16[32,144,128]{2,1,0:T(8,128)(2,1)S(1)}, u32[]{:S(2)}, u32[]{:S(2)}) %all-to-all-start.2) | async-done | bytes 1179680 | tf_op jit(solution)/shard_map/all_to_all | solution.py:99
  94.5 0.7 multiply_reduce_fusion.1
  95.2 0.9 fusion.13
  (60 shorter events, 2.6 us)
Async XLA Ops:
  0.0 11.6 %copy-start = (bf16[512,576]{0,1:T(8,128)(2,1)S(1)}, bf16[512,576]{0,1:T(8,128)(2,1)}, u32[]{:S(2)}) copy-start(bf16[512,576]{0,1:T(8,128)(2,1)} %param.8) | copy-start | bytes 1769476
  3.1 20.4 %all-to-all-start = ((bf16[8,160,128]{2,1,0:T(8,128)(2,1)}), bf16[8,160,128]{2,1,0:T(8,128)(2,1)S(1)}, u32[]{:S(2)}, u32[]{:S(2)}) async-start(bf16[8,160,128]{2,1,0:T(8,128)(2,1)} %broadcast_in_dim.82), calls=%async_computation | async-start | bytes 655360 | tf_op jit(solution)/shard_map/all_to_all | solution.py:62
  12.8 20.1 %collective-permute-start.1 = (bf16[1024,576]{0,1:T(8,128)(2,1)}, bf16[1024,576]{0,1:T(8,128)(2,1)}, u32[]{:S(2)}, u32[]{:S(2)}) collective-permute-start(bf16[1024,576]{0,1:T(8,128)(2,1)} %pad_maximum_fusion.1), channel_id=1, source_target_pairs={{0,8},{8,0},{1,9},{9,1},{2,10},{10,2},{3,11},{11,3},{4,12},{12,4},... | collective-permute-start | bytes 3538952 | tf_op jit(solution)/shard_map/ppermute | solution.py:74
  24.8 20.7 %all-to-all-start.1 = ((bf16[4,8,160,128]{3,2,1,0:T(8,128)(2,1)}), bf16[4,8,160,128]{3,2,1,0:T(8,128)(2,1)S(1)}, u32[]{:S(2)}, u32[]{:S(2)}) async-start(bf16[4,8,160,128]{3,2,1,0:T(8,128)(2,1)} %broadcast_in_dim.83), calls=%async_computation.1 | async-start | bytes 2621440 | tf_op jit(solution)/shard_map/all_to_all | solution.py:65
  29.1 3.2 %collective-permute-start = (s32[1]{0:T(128)}, s32[1]{0:T(128)}, u32[]{:S(2)}, u32[]{:S(2)}) collective-permute-start(s32[1]{0:T(128)} %param.11), channel_id=1, source_target_pairs={{0,8},{8,0},{1,9},{9,1},{2,10},{10,2},{3,11},{11,3},{4,12},{12,4},... | collective-permute-start | bytes 20 | tf_op jit(solution)/shard_map/ppermute | solution.py:74
  45.6 2.3 %copy-start.1 = (bf16[512,576]{0,1:T(8,128)(2,1)S(1)}, bf16[512,576]{0,1:T(8,128)(2,1)}, u32[]{:S(2)}) copy-start(bf16[512,576]{0,1:T(8,128)(2,1)} %param.8) | copy-start | bytes 1769476
  53.4 2.7 %copy-start.2 = (bf16[2048,576]{0,1:T(8,128)(2,1)S(1)}, bf16[2048,576]{0,1:T(8,128)(2,1)}, u32[]{:S(2)}) copy-start(bf16[2048,576]{0,1:T(8,128)(2,1)} %pad_maximum_fusion) | copy-start | bytes 7077892
  59.5 5.1 %copy-start.3 = (bf16[1,8,64,576]{3,2,1,0:T(8,128)(2,1)S(1)}, bf16[1,8,64,576]{3,2,1,0:T(8,128)(2,1)}, u32[]{:S(2)}) copy-start(bf16[1,8,64,576]{3,2,1,0:T(8,128)(2,1)} %param.9) | copy-start | bytes 1769476
  59.5 5.1 %copy-start.4 = (bf16[2,1,16,576]{3,2,1,0:T(8,128)(2,1)S(1)}, bf16[2,1,16,576]{3,2,1,0:T(8,128)(2,1)}, u32[]{:S(2)}) copy-start(bf16[2,1,16,576]{3,2,1,0:T(8,128)(2,1)} %param.7) | copy-start | bytes 110596
  59.5 5.1 %copy-start.5 = (bf16[2,1,576]{2,0,1:T(2,128)(2,1)S(1)}, bf16[2,1,576]{2,0,1:T(2,128)(2,1)}, u32[]{:S(2)}) copy-start(bf16[2,1,576]{2,0,1:T(2,128)(2,1)} %param.10) | copy-start | bytes 6916
  60.6 33.3 %all-to-all-start.2 = ((bf16[32,144,128]{2,1,0:T(8,128)(2,1)}), bf16[32,144,128]{2,1,0:T(8,128)(2,1)S(1)}, u32[]{:S(2)}, u32[]{:S(2)}) async-start(bf16[32,144,128]{2,1,0:T(8,128)(2,1)} %pad_maximum_fusion.2), calls=%async_computation.2 | async-start | bytes 2359296 | tf_op jit(solution)/shard_map/all_to_all | solution.py:99

commit v10 on v9

--- a/solution.py
+++ b/solution.py
@@ -89,7 +89,7 @@
         [ones, fork_count(my_beam, suffix_len[0]), ones, fork_count(partner_beam, partner_len[0])], axis=1
     )
     top, total, summed = masked_softmax(rows, keys, mult)
-    out = (summed / total[..., None]).astype(jnp.bfloat16)
+    out = summed.astype(jnp.bfloat16)
 
     out_rows = out.reshape(chips, -1, LANES)
     parts = jnp.stack(split3(top) + split3(total), axis=1).reshape(chips, -1)
@@ -114,9 +114,9 @@
     total_l = total_l.reshape(row_n)
     summed_l = summed_l.reshape(row_n, DL)
     peak = jnp.maximum(jnp.max(top_r, axis=0), top_l)
-    weight_r = total_r * jnp.exp(top_r - peak[None])
+    weight_r = jnp.exp(top_r - peak[None])
     weight_l = jnp.exp(top_l - peak)
-    denom = jnp.sum(weight_r, axis=0) + total_l * weight_l
+    denom = jnp.sum(total_r * weight_r, axis=0) + total_l * weight_l
     numer = jnp.sum(weight_r[..., None] * out_r.astype(jnp.float32), axis=0) + weight_l[:, None] * summed_l
     result = (numer / denom[:, None]).astype(jnp.bfloat16)
     return result.reshape(steps_n, 1, head_dev, DL)

time: 97 us -> 102 us (1.052)
  local copies, waits for them, and re-layouts: 7.86 us -> 11.1 us
  other arithmetic: 10.6 us -> 12.8 us
    unnamed x17 -> x19, local copies, waits for them, and re-layouts: 0.21 us -> 3.42 us
    reduce_sum x1, other arithmetic: 2.66 us -> 4.74 us  [masked_softmax(): total = jnp.sum(weights * m, axis=-1)]
where the time goes in v10:
time: 102 us
  waiting for transfers between devices  47.5 us (47%)
  starting transfers between devices  19.2 us (19%)
  other arithmetic  12.8 us (13%)
  local copies, waits for them, and re-layouts  11.1 us (11%)
  matrix products  9.35 us (9%)
  between operations  1.67 us (2%)
    all_to_all x1, waiting for transfers between devices, on_device(): arrived = lax.all_to_all(payload, ('cx', 'cy'), 0, 0, tiled=True)  28.6 us
    all_to_all x1, waiting for transfers between devices, on_device(): lax.all_to_all(jnp.broadcast_to(along_y[None], (lax.axis_size('cx'),) + a...  9.41 us
    all_to_all x1, waiting for transfers between devices, on_device(): lax.all_to_all(jnp.broadcast_to(packed[None], (lax.axis_size('cy'),) + pa...  8.82 us
    all_to_all x1, starting transfers between devices, on_device(): lax.all_to_all(jnp.broadcast_to(packed[None], (lax.axis_size('cy'),) + pa...  7.1 us
    dot_general x1, matrix products, masked_softmax(): jnp.einsum('gqk,tk->gqt', rows, keys, preferred_element_type=jnp.float32)  5.6 us
    reduce_sum x1, other arithmetic, masked_softmax(): total = jnp.sum(weights * m, axis=-1)  4.74 us
    all_to_all x1, starting transfers between devices, on_device(): lax.all_to_all(jnp.broadcast_to(along_y[None], (lax.axis_size('cx'),) + a...  4.29 us
    all_to_all x1, starting transfers between devices, on_device(): arrived = lax.all_to_all(payload, ('cx', 'cy'), 0, 0, tiled=True)  3.94 us
  transfers between devices with their start and end apart: 5, of which 4 were waited for; matrix products, arithmetic and copies ran while one was open for 8% of the time, Pallas kernels for 0%

profile of v10, /device:TPU:448, one launch (start us, length us, event | category | flops | bytes accessed | tf_op | source)
XLA Modules:
  0.0 101.5 jit_solution(14611703942470308256)
XLA Ops:
  0.0 1.0 reshape.375
  2.4 0.8 broadcast_in_dim.81
  3.1 7.1 %all-to-all-start = ((bf16[8,160,128]{2,1,0:T(8,128)(2,1)}), bf16[8,160,128]{2,1,0:T(8,128)(2,1)S(1)}, u32[]{:S(2)}, u32[]{:S(2)}) async-start(bf16[8,160,128]{2,1,0:T(8,128)(2,1)} %broadcast_in_dim.81), calls=%async_computation | async-start | bytes 655360 | tf_op jit(solution)/shard_map/all_to_all | solution.py:62
  10.2 1.3 %copy.30 = bf16[512,576]{0,1:T(8,128)(2,1)S(1)} copy(bf16[512,576]{1,0:T(8,128)(2,1)} %bitcast.100) | data formatting | bytes 1179648 | tf_op jit(solution)/shard_map/reshape | solution.py:72
  11.6 1.2 %pad_maximum_fusion.1 = bf16[1024,576]{0,1:T(8,128)(2,1)} fusion(bf16[512,576]{0,1:T(8,128)(2,1)S(1)} %copy.30, bf16[512,576]{0,1:T(8,128)(2,1)S(1)} %copy-done.1), kind=kLoop, calls=%fused_computation.14 | loop fusion | flops 2359296 | bytes 2359296 | tf_op jit(solution)/shard_map/concatenate | solution.py:73
  12.8 1.9 %collective-permute-start.1 = (bf16[1024,576]{0,1:T(8,128)(2,1)}, bf16[1024,576]{0,1:T(8,128)(2,1)}, u32[]{:S(2)}, u32[]{:S(2)}) collective-permute-start(bf16[1024,576]{0,1:T(8,128)(2,1)} %pad_maximum_fusion.1), channel_id=1, source_target_pairs={{0,8},{8,0},{1,9},{9,1},{2,10},{10,2},{3,11},{11,3},{4,12},{12,4},... | collective-permute-start | bytes 3538952 | tf_op jit(solution)/shard_map/ppermute | solution.py:74
  14.7 8.8 %all-to-all-done = bf16[8,160,128]{2,1,0:T(8,128)(2,1)S(1)} async-done(((bf16[8,160,128]{2,1,0:T(8,128)(2,1)}), bf16[8,160,128]{2,1,0:T(8,128)(2,1)S(1)}, u32[]{:S(2)}, u32[]{:S(2)}) %all-to-all-start) | async-done | bytes 327712 | tf_op jit(solution)/shard_map/all_to_all | solution.py:62
  23.5 1.3 %broadcast_in_dim.82 = bf16[4,8,160,128]{3,2,1,0:T(8,128)(2,1)} broadcast(bf16[8,160,128]{2,1,0:T(8,128)(2,1)S(1)} %all-to-all-done), dimensions={1,2,3} | broadcast | bytes 1638400 | tf_op jit(solution)/shard_map/broadcast_in_dim | solution.py:66
  24.8 4.3 %all-to-all-start.1 = ((bf16[4,8,160,128]{3,2,1,0:T(8,128)(2,1)}), bf16[4,8,160,128]{3,2,1,0:T(8,128)(2,1)S(1)}, u32[]{:S(2)}, u32[]{:S(2)}) async-start(bf16[4,8,160,128]{3,2,1,0:T(8,128)(2,1)} %broadcast_in_dim.82), calls=%async_computation.1 | async-start | bytes 2621440 | tf_op jit(solution)/shard_map/all_to_all | solution.py:65
  29.1 1.9 %collective-permute-start = (s32[1]{0:T(128)}, s32[1]{0:T(128)}, u32[]{:S(2)}, u32[]{:S(2)}) collective-permute-start(s32[1]{0:T(128)} %param.11), channel_id=1, source_target_pairs={{0,8},{8,0},{1,9},{9,1},{2,10},{10,2},{3,11},{11,3},{4,12},{12,4},... | collective-permute-start | bytes 20 | tf_op jit(solution)/shard_map/ppermute | solution.py:74
  31.7 0.7 collective-permute-done
  33.0 3.1 %pad_maximum_fusion = bf16[2048,576]{0,1:T(8,128)(2,1)} fusion(bf16[1024,576]{0,1:T(8,128)(2,1)} %collective-permute-done.1, bf16[512,576]{0,1:T(8,128)(2,1)S(1)} %copy.30, bf16[512,576]{0,1:T(8,128)(2,1)S(1)} %copy-done.1), kind=kLoop, calls=%fused_computation.7 | loop fusion | flops 7077888 | bytes 4718592 | tf_op jit(solution)/shard_map/concatenate | solution.py:75
  36.1 9.4 %all-to-all-done.1 = bf16[4,8,160,128]{3,2,1,0:T(8,128)(2,1)S(1)} async-done(((bf16[4,8,160,128]{3,2,1,0:T(8,128)(2,1)}), bf16[4,8,160,128]{3,2,1,0:T(8,128)(2,1)S(1)}, u32[]{:S(2)}, u32[]{:S(2)}) %all-to-all-start.1) | async-done | bytes 1310752 | tf_op jit(solution)/shard_map/all_to_all | solution.py:65
  45.9 2.0 %reshape.379 = bf16[32,32,576]{2,1,0:T(8,128)(2,1)} reshape(bf16[32,144,128]{2,1,0:T(8,128)(2,1)S(1)} %slice.65) | data formatting | bytes 2359296 | tf_op jit(solution)/shard_map/reshape | solution.py:68
  47.9 5.6 %select_reduce_fusion = (f32[32,32]{1,0:T(8,128)S(1)}, f32[32,32,2048]{2,1,0:T(8,128)S(1)}) fusion(pred[32,2048]{1,0:T(8,128)(4,1)S(1)} %broadcast_compare_fusion, bf16[32,32,576]{2,1,0:T(8,128)(2,1)} %reshape.379, bf16[1024,576]{0,1:T(8,128)(2,1)} %collective-permute-done.1, bf16[512,576]{0,1:T(8,128)(2,1)S(1)} %copy.30, bf16[512,576]{0,1:T(8,128)(2,1)S(1)} %copy-done.2), kind=kOutput, calls=%fused_computation.2 | convolution fusion | flops 2429287424 | bytes 11997184 | tf_op jit(solution)/shard_map/gqk,tk->gqt/dot_general | solution.py:16
  53.5 3.2 %copy-done = f32[32,32,2048]{2,1,0:T(8,128)} copy-done((f32[32,32,2048]{2,1,0:T(8,128)}, f32[32,32,2048]{2,1,0:T(8,128)S(1)}, u32[]{:S(2)}) %copy-start) | copy-done | bytes 8388632
  56.7 2.5 %fusion.8 = bf16[32,32,512]{2,1,0:T(8,128)(2,1)S(1)} fusion(bf16[2048,576]{0,1:T(8,128)(2,1)S(1)} %copy-done.3, f32[32,32,2048]{2,1,0:T(8,128)S(1)} %get-tuple-element.20, f32[32,32]{1,0:T(8,128)S(1)} %get-tuple-element.19, pred[32,2048]{1,0:T(8,128)(4,1)S(1)} %broadcast_compare_fusion, bf16[32,2048]{1,0:T(8,128)(2,1)S(1)} %fusion.51), kind=kOutput, calls=%fused_computation.13 | convolution fusion | flops 2158493696 | bytes 11747328 | tf_op jit(solution)/shard_map/gqt,td->gqd/dot_general | solution.py:23
  59.2 0.7 reshape.381
  59.9 4.7 %multiply_reduce_fusion = f32[32,32]{1,0:T(8,128)S(1)} fusion(f32[32,32,2048]{2,1,0:T(8,128)} %copy-done, f32[32,2048]{1,0:T(8,128)S(1)} %pad_maximum_fusion.4, f32[32,32]{1,0:T(8,128)S(1)} %get-tuple-element.19, pred[32,2048]{1,0:T(8,128)(4,1)S(1)} %broadcast_compare_fusion), kind=kLoop, calls=%fused_computation | loop fusion | flops 10484736 | bytes 8724480 | tf_op jit(solution)/shard_map/reduce_sum | solution.py:21
  64.9 1.1 %pad_maximum_fusion.2 = bf16[32,144,128]{2,1,0:T(8,128)(2,1)} fusion(bf16[32,16,128]{2,1,0:T(8,128)(2,1)S(1)} %bitcast.103, bf16[32,128,128]{2,1,0:T(8,128)(2,1)S(1)} %reshape.381), kind=kLoop, calls=%fused_computation.15 | loop fusion | flops 2359296 | bytes 2359296 | tf_op jit(solution)/shard_map/concatenate | solution.py:98
  66.0 3.9 %all-to-all-start.2 = ((bf16[32,144,128]{2,1,0:T(8,128)(2,1)}), bf16[32,144,128]{2,1,0:T(8,128)(2,1)S(1)}, u32[]{:S(2)}, u32[]{:S(2)}) async-start(bf16[32,144,128]{2,1,0:T(8,128)(2,1)} %pad_maximum_fusion.2), calls=%async_computation.2 | async-start | bytes 2359296 | tf_op jit(solution)/shard_map/all_to_all | solution.py:99
  70.7 28.6 %all-to-all-done.2 = bf16[32,144,128]{2,1,0:T(8,128)(2,1)S(1)} async-done(((bf16[32,144,128]{2,1,0:T(8,128)(2,1)}), bf16[32,144,128]{2,1,0:T(8,128)(2,1)S(1)}, u32[]{:S(2)}, u32[]{:S(2)}) %all-to-all-start.2) | async-done | bytes 1179680 | tf_op jit(solution)/shard_map/all_to_all | solution.py:99
  99.9 0.7 multiply_reduce_fusion.1
  100.7 0.9 fusion.16
  (63 shorter events, 3.3 us)
Async XLA Ops:
  0.0 11.5 %copy-start.1 = (bf16[512,576]{0,1:T(8,128)(2,1)S(1)}, bf16[512,576]{0,1:T(8,128)(2,1)}, u32[]{:S(2)}) copy-start(bf16[512,576]{0,1:T(8,128)(2,1)} %param.8) | copy-start | bytes 1769476
  3.1 20.4 %all-to-all-start = ((bf16[8,160,128]{2,1,0:T(8,128)(2,1)}), bf16[8,160,128]{2,1,0:T(8,128)(2,1)S(1)}, u32[]{:S(2)}, u32[]{:S(2)}) async-start(bf16[8,160,128]{2,1,0:T(8,128)(2,1)} %broadcast_in_dim.81), calls=%async_computation | async-start | bytes 655360 | tf_op jit(solution)/shard_map/all_to_all | solution.py:62
  12.8 20.2 %collective-permute-start.1 = (bf16[1024,576]{0,1:T(8,128)(2,1)}, bf16[1024,576]{0,1:T(8,128)(2,1)}, u32[]{:S(2)}, u32[]{:S(2)}) collective-permute-start(bf16[1024,576]{0,1:T(8,128)(2,1)} %pad_maximum_fusion.1), channel_id=1, source_target_pairs={{0,8},{8,0},{1,9},{9,1},{2,10},{10,2},{3,11},{11,3},{4,12},{12,4},... | collective-permute-start | bytes 3538952 | tf_op jit(solution)/shard_map/ppermute | solution.py:74
  24.8 20.7 %all-to-all-start.1 = ((bf16[4,8,160,128]{3,2,1,0:T(8,128)(2,1)}), bf16[4,8,160,128]{3,2,1,0:T(8,128)(2,1)S(1)}, u32[]{:S(2)}, u32[]{:S(2)}) async-start(bf16[4,8,160,128]{3,2,1,0:T(8,128)(2,1)} %broadcast_in_dim.82), calls=%async_computation.1 | async-start | bytes 2621440 | tf_op jit(solution)/shard_map/all_to_all | solution.py:65
  29.1 3.3 %collective-permute-start = (s32[1]{0:T(128)}, s32[1]{0:T(128)}, u32[]{:S(2)}, u32[]{:S(2)}) collective-permute-start(s32[1]{0:T(128)} %param.11), channel_id=1, source_target_pairs={{0,8},{8,0},{1,9},{9,1},{2,10},{10,2},{3,11},{11,3},{4,12},{12,4},... | collective-permute-start | bytes 20 | tf_op jit(solution)/shard_map/ppermute | solution.py:74
  45.6 2.3 %copy-start.2 = (bf16[512,576]{0,1:T(8,128)(2,1)S(1)}, bf16[512,576]{0,1:T(8,128)(2,1)}, u32[]{:S(2)}) copy-start(bf16[512,576]{0,1:T(8,128)(2,1)} %param.8) | copy-start | bytes 1769476
  47.9 8.8 %copy-start.3 = (bf16[2048,576]{0,1:T(8,128)(2,1)S(1)}, bf16[2048,576]{0,1:T(8,128)(2,1)}, u32[]{:S(2)}) copy-start(bf16[2048,576]{0,1:T(8,128)(2,1)} %pad_maximum_fusion) | copy-start | bytes 7077892
  53.5 3.2 %copy-start = (f32[32,32,2048]{2,1,0:T(8,128)}, f32[32,32,2048]{2,1,0:T(8,128)S(1)}, u32[]{:S(2)}) copy-start(f32[32,32,2048]{2,1,0:T(8,128)S(1)} %get-tuple-element.20) | copy-start | bytes 25165828
  64.9 5.1 %copy-start.4 = (bf16[1,8,64,576]{3,2,1,0:T(8,128)(2,1)S(1)}, bf16[1,8,64,576]{3,2,1,0:T(8,128)(2,1)}, u32[]{:S(2)}) copy-start(bf16[1,8,64,576]{3,2,1,0:T(8,128)(2,1)} %param.9) | copy-start | bytes 1769476
  64.9 5.1 %copy-start.5 = (bf16[2,1,16,576]{3,2,1,0:T(8,128)(2,1)S(1)}, bf16[2,1,16,576]{3,2,1,0:T(8,128)(2,1)}, u32[]{:S(2)}) copy-start(bf16[2,1,16,576]{3,2,1,0:T(8,128)(2,1)} %param.7) | copy-start | bytes 110596
  64.9 5.1 %copy-start.6 = (bf16[2,1,576]{2,0,1:T(2,128)(2,1)S(1)}, bf16[2,1,576]{2,0,1:T(2,128)(2,1)}, u32[]{:S(2)}) copy-start(bf16[2,1,576]{2,0,1:T(2,128)(2,1)} %param.10) | copy-start | bytes 6916
  66.0 33.3 %all-to-all-start.2 = ((bf16[32,144,128]{2,1,0:T(8,128)(2,1)}), bf16[32,144,128]{2,1,0:T(8,128)(2,1)S(1)}, u32[]{:S(2)}, u32[]{:S(2)}) async-start(bf16[32,144,128]{2,1,0:T(8,128)(2,1)} %pad_maximum_fusion.2), calls=%async_computation.2 | async-start | bytes 2359296 | tf_op jit(solution)/shard_map/all_to_all | solution.py:99

commit v11 on v9

--- a/solution.py
+++ b/solution.py
@@ -58,10 +58,14 @@
     q_rows = steps_n * head_dev * width // LANES
     meta = jnp.concatenate([parent, fork_pages.reshape(-1)]).astype(jnp.bfloat16)
     meta = jnp.pad(meta, (0, META_ROWS * LANES - meta.shape[0])).reshape(META_ROWS, LANES)
-    packed = jnp.concatenate([queries.reshape(q_rows, LANES), meta], axis=0)
-    along_y = lax.all_to_all(
-        jnp.broadcast_to(packed[None], (lax.axis_size("cy"),) + packed.shape), "cy", 0, 0, tiled=True
+    y_n = lax.axis_size("cy")
+    q_flat = queries.reshape(q_rows, LANES)
+    send = jnp.concatenate(
+        [jnp.broadcast_to(q_flat[None], (y_n,) + q_flat.shape), jnp.broadcast_to(meta[None], (y_n,) + meta.shape)],
+        axis=1,
     )
+    packed = send[0]
+    along_y = lax.all_to_all(send, "cy", 0, 0, tiled=True)
     gathered = lax.all_to_all(
         jnp.broadcast_to(along_y[None], (lax.axis_size("cx"),) + along_y.shape), "cx", 0, 0, tiled=True
     ).reshape((chips,) + packed.shape)

time: 97 us -> 97 us (level)
  no operation moved by 1% of the time
where the time goes in v11:
time: 97 us; the launch traced here: 96.1 us
  waiting for transfers between devices  47.6 us (49%)
  starting transfers between devices  19.2 us (20%)
  other arithmetic  11.4 us (12%)
  matrix products  9.23 us (10%)
  local copies, waits for them, and re-layouts  7.12 us (7%)
  between operations  1.66 us (2%)
    all_to_all x1, waiting for transfers between devices, on_device(): arrived = lax.all_to_all(payload, ('cx', 'cy'), 0, 0, tiled=True)  28.6 us
    all_to_all x1, waiting for transfers between devices, on_device(): lax.all_to_all(jnp.broadcast_to(along_y[None], (lax.axis_size('cx'),) + a...  9.63 us
    all_to_all x1, waiting for transfers between devices, on_device(): along_y = lax.all_to_all(send, 'cy', 0, 0, tiled=True)  8.85 us
    all_to_all x1, starting transfers between devices, on_device(): along_y = lax.all_to_all(send, 'cy', 0, 0, tiled=True)  7.1 us
    dot_general x1, matrix products, masked_softmax(): jnp.einsum('gqk,tk->gqt', rows, keys, preferred_element_type=jnp.float32)  5.44 us
    all_to_all x1, starting transfers between devices, on_device(): lax.all_to_all(jnp.broadcast_to(along_y[None], (lax.axis_size('cx'),) + a...  4.29 us
    all_to_all x1, starting transfers between devices, on_device(): arrived = lax.all_to_all(payload, ('cx', 'cy'), 0, 0, tiled=True)  3.94 us
    ppermute x2, starting transfers between devices, on_device(): lax.ppermute((local_keys, suffix_len), 'core', [(0, 1), (1, 0)])  3.82 us
  transfers between devices with their start and end apart: 5, of which 4 were waited for; matrix products, arithmetic and copies ran while one was open for 8% of the time, Pallas kernels for 0%

profile of v11, /device:TPU:448, one launch (start us, length us, event | category | flops | bytes accessed | tf_op | source)
XLA Modules:
  0.0 96.1 jit_solution(296212252342009068)
XLA Ops:
  0.0 1.0 broadcast_in_dim.90
  1.6 0.7 convert_bitcast_fusion
  2.4 0.8 pad_maximum_fusion.4
  3.2 7.1 %all-to-all-start = ((bf16[8,160,128]{2,1,0:T(8,128)(2,1)}), bf16[8,160,128]{2,1,0:T(8,128)(2,1)S(1)}, u32[]{:S(2)}, u32[]{:S(2)}) async-start(bf16[8,160,128]{2,1,0:T(8,128)(2,1)} %pad_maximum_fusion.4), calls=%async_computation | async-start | bytes 655360 | tf_op jit(solution)/shard_map/all_to_all | solution.py:68
  10.3 1.3 %copy.30 = bf16[512,576]{0,1:T(8,128)(2,1)S(1)} copy(bf16[512,576]{1,0:T(8,128)(2,1)} %bitcast.98) | data formatting | bytes 1179648 | tf_op jit(solution)/shard_map/reshape | solution.py:76
  11.6 1.2 %pad_maximum_fusion.1 = bf16[1024,576]{0,1:T(8,128)(2,1)} fusion(bf16[512,576]{0,1:T(8,128)(2,1)S(1)} %copy.30, bf16[512,576]{0,1:T(8,128)(2,1)S(1)} %copy-done), kind=kLoop, calls=%fused_computation.14 | loop fusion | flops 2359296 | bytes 2359296 | tf_op jit(solution)/shard_map/concatenate | solution.py:77
  12.8 1.9 %collective-permute-start.1 = (bf16[1024,576]{0,1:T(8,128)(2,1)}, bf16[1024,576]{0,1:T(8,128)(2,1)}, u32[]{:S(2)}, u32[]{:S(2)}) collective-permute-start(bf16[1024,576]{0,1:T(8,128)(2,1)} %pad_maximum_fusion.1), channel_id=1, source_target_pairs={{0,8},{8,0},{1,9},{9,1},{2,10},{10,2},{3,11},{11,3},{4,12},{12,4},... | collective-permute-start | bytes 3538952 | tf_op jit(solution)/shard_map/ppermute | solution.py:78
  14.7 8.9 %all-to-all-done = bf16[8,160,128]{2,1,0:T(8,128)(2,1)S(1)} async-done(((bf16[8,160,128]{2,1,0:T(8,128)(2,1)}), bf16[8,160,128]{2,1,0:T(8,128)(2,1)S(1)}, u32[]{:S(2)}, u32[]{:S(2)}) %all-to-all-start) | async-done | bytes 327712 | tf_op jit(solution)/shard_map/all_to_all | solution.py:68
  23.6 1.3 %broadcast_in_dim.94 = bf16[4,8,160,128]{3,2,1,0:T(8,128)(2,1)} broadcast(bf16[8,160,128]{2,1,0:T(8,128)(2,1)S(1)} %all-to-all-done), dimensions={1,2,3} | broadcast | bytes 1638400 | tf_op jit(solution)/shard_map/broadcast_in_dim | solution.py:70
  24.8 4.3 %all-to-all-start.1 = ((bf16[4,8,160,128]{3,2,1,0:T(8,128)(2,1)}), bf16[4,8,160,128]{3,2,1,0:T(8,128)(2,1)S(1)}, u32[]{:S(2)}, u32[]{:S(2)}) async-start(bf16[4,8,160,128]{3,2,1,0:T(8,128)(2,1)} %broadcast_in_dim.94), calls=%async_computation.1 | async-start | bytes 2621440 | tf_op jit(solution)/shard_map/all_to_all | solution.py:69
  29.1 1.9 %collective-permute-start = (s32[1]{0:T(128)}, s32[1]{0:T(128)}, u32[]{:S(2)}, u32[]{:S(2)}) collective-permute-start(s32[1]{0:T(128)} %param.11), channel_id=1, source_target_pairs={{0,8},{8,0},{1,9},{9,1},{2,10},{10,2},{3,11},{11,3},{4,12},{12,4},... | collective-permute-start | bytes 20 | tf_op jit(solution)/shard_map/ppermute | solution.py:78
  32.3 0.6 iota_compare_fusion.1
  32.9 3.0 %pad_maximum_fusion = bf16[2048,576]{0,1:T(8,128)(2,1)} fusion(bf16[1024,576]{0,1:T(8,128)(2,1)} %collective-permute-done.1, bf16[512,576]{0,1:T(8,128)(2,1)S(1)} %copy.30, bf16[512,576]{0,1:T(8,128)(2,1)S(1)} %copy-done), kind=kLoop, calls=%fused_computation.7 | loop fusion | flops 7077888 | bytes 4718592 | tf_op jit(solution)/shard_map/concatenate | solution.py:79
  35.9 9.6 %all-to-all-done.1 = bf16[4,8,160,128]{3,2,1,0:T(8,128)(2,1)S(1)} async-done(((bf16[4,8,160,128]{3,2,1,0:T(8,128)(2,1)}), bf16[4,8,160,128]{3,2,1,0:T(8,128)(2,1)S(1)}, u32[]{:S(2)}, u32[]{:S(2)}) %all-to-all-start.1) | async-done | bytes 1310752 | tf_op jit(solution)/shard_map/all_to_all | solution.py:69
  46.0 1.9 %reshape.388 = bf16[32,32,576]{2,1,0:T(8,128)(2,1)} reshape(bf16[32,144,128]{2,1,0:T(8,128)(2,1)S(1)} %slice.65) | data formatting | bytes 2359296 | tf_op jit(solution)/shard_map/reshape | solution.py:72
  48.0 5.4 %select_reduce_fusion = (f32[32,32]{1,0:T(8,128)S(1)}, f32[32,32,2048]{2,1,0:T(8,128)S(1)}) fusion(pred[32,2048]{1,0:T(8,128)(4,1)S(1)} %broadcast_compare_fusion, bf16[32,32,576]{2,1,0:T(8,128)(2,1)} %reshape.388, bf16[1024,576]{0,1:T(8,128)(2,1)} %collective-permute-done.1, bf16[512,576]{0,1:T(8,128)(2,1)S(1)} %copy.30, bf16[512,576]{0,1:T(8,128)(2,1)S(1)} %copy-done.1), kind=kOutput, calls=%fused_computation.2 | convolution fusion | flops 2429287424 | bytes 11997184 | tf_op jit(solution)/shard_map/gqk,tk->gqt/dot_general | solution.py:16
  53.4 2.7 %multiply_reduce_fusion = f32[32,32]{1,0:T(8,128)S(1)} fusion(f32[32,32,2048]{2,1,0:T(8,128)S(1)} %get-tuple-element.23, f32[32,2048]{1,0:T(8,128)S(1)} %pad_maximum_fusion.5, f32[32,32]{1,0:T(8,128)S(1)} %get-tuple-element.22, pred[32,2048]{1,0:T(8,128)(4,1)S(1)} %broadcast_compare_fusion), kind=kLoop, calls=%fused_computation | loop fusion | flops 10484736 | bytes 8724480 | tf_op jit(solution)/shard_map/reduce_sum | solution.py:21
  56.1 2.5 %divide_convert_fusion = bf16[32,32,512]{2,1,0:T(8,128)(2,1)S(1)} fusion(f32[32,32]{1,0:T(8,128)S(1)} %multiply_reduce_fusion, bf16[2048,576]{0,1:T(8,128)(2,1)S(1)} %copy-done.2, f32[32,32,2048]{2,1,0:T(8,128)S(1)} %get-tuple-element.23, f32[32,32]{1,0:T(8,128)S(1)} %get-tuple-element.22, pred[32,2048]{1,0:T(8,128)(4,1)S(1)} %broadcast_compare_fusion, ...), kind=kOutput, calls=%fused_computation.12 | convolution fusion | flops 2159017984 | bytes 11763712 | tf_op jit(solution)/shard_map/gqt,td->gqd/dot_general | solution.py:23
  58.6 0.7 reshape.390
  59.6 1.1 %pad_maximum_fusion.2 = bf16[32,144,128]{2,1,0:T(8,128)(2,1)} fusion(bf16[32,16,128]{2,1,0:T(8,128)(2,1)S(1)} %bitcast.101, bf16[32,128,128]{2,1,0:T(8,128)(2,1)S(1)} %reshape.390), kind=kLoop, calls=%fused_computation.15 | loop fusion | flops 2359296 | bytes 2359296 | tf_op jit(solution)/shard_map/concatenate | solution.py:102
  60.6 3.9 %all-to-all-start.2 = ((bf16[32,144,128]{2,1,0:T(8,128)(2,1)}), bf16[32,144,128]{2,1,0:T(8,128)(2,1)S(1)}, u32[]{:S(2)}, u32[]{:S(2)}) async-start(bf16[32,144,128]{2,1,0:T(8,128)(2,1)} %pad_maximum_fusion.2), calls=%async_computation.2 | async-start | bytes 2359296 | tf_op jit(solution)/shard_map/all_to_all | solution.py:103
  65.3 28.6 %all-to-all-done.2 = bf16[32,144,128]{2,1,0:T(8,128)(2,1)S(1)} async-done(((bf16[32,144,128]{2,1,0:T(8,128)(2,1)}), bf16[32,144,128]{2,1,0:T(8,128)(2,1)S(1)}, u32[]{:S(2)}, u32[]{:S(2)}) %all-to-all-start.2) | async-done | bytes 1179680 | tf_op jit(solution)/shard_map/all_to_all | solution.py:103
  94.5 0.7 multiply_reduce_fusion.1
  95.3 0.9 fusion.13
  (61 shorter events, 2.6 us)
Async XLA Ops:
  0.0 11.6 %copy-start = (bf16[512,576]{0,1:T(8,128)(2,1)S(1)}, bf16[512,576]{0,1:T(8,128)(2,1)}, u32[]{:S(2)}) copy-start(bf16[512,576]{0,1:T(8,128)(2,1)} %param.8) | copy-start | bytes 1769476
  3.2 20.4 %all-to-all-start = ((bf16[8,160,128]{2,1,0:T(8,128)(2,1)}), bf16[8,160,128]{2,1,0:T(8,128)(2,1)S(1)}, u32[]{:S(2)}, u32[]{:S(2)}) async-start(bf16[8,160,128]{2,1,0:T(8,128)(2,1)} %pad_maximum_fusion.4), calls=%async_computation | async-start | bytes 655360 | tf_op jit(solution)/shard_map/all_to_all | solution.py:68
  12.8 20.1 %collective-permute-start.1 = (bf16[1024,576]{0,1:T(8,128)(2,1)}, bf16[1024,576]{0,1:T(8,128)(2,1)}, u32[]{:S(2)}, u32[]{:S(2)}) collective-permute-start(bf16[1024,576]{0,1:T(8,128)(2,1)} %pad_maximum_fusion.1), channel_id=1, source_target_pairs={{0,8},{8,0},{1,9},{9,1},{2,10},{10,2},{3,11},{11,3},{4,12},{12,4},... | collective-permute-start | bytes 3538952 | tf_op jit(solution)/shard_map/ppermute | solution.py:78
  24.8 20.7 %all-to-all-start.1 = ((bf16[4,8,160,128]{3,2,1,0:T(8,128)(2,1)}), bf16[4,8,160,128]{3,2,1,0:T(8,128)(2,1)S(1)}, u32[]{:S(2)}, u32[]{:S(2)}) async-start(bf16[4,8,160,128]{3,2,1,0:T(8,128)(2,1)} %broadcast_in_dim.94), calls=%async_computation.1 | async-start | bytes 2621440 | tf_op jit(solution)/shard_map/all_to_all | solution.py:69
  29.1 3.2 %collective-permute-start = (s32[1]{0:T(128)}, s32[1]{0:T(128)}, u32[]{:S(2)}, u32[]{:S(2)}) collective-permute-start(s32[1]{0:T(128)} %param.11), channel_id=1, source_target_pairs={{0,8},{8,0},{1,9},{9,1},{2,10},{10,2},{3,11},{11,3},{4,12},{12,4},... | collective-permute-start | bytes 20 | tf_op jit(solution)/shard_map/ppermute | solution.py:78
  45.6 2.3 %copy-start.1 = (bf16[512,576]{0,1:T(8,128)(2,1)S(1)}, bf16[512,576]{0,1:T(8,128)(2,1)}, u32[]{:S(2)}) copy-start(bf16[512,576]{0,1:T(8,128)(2,1)} %param.8) | copy-start | bytes 1769476
  53.4 2.7 %copy-start.2 = (bf16[2048,576]{0,1:T(8,128)(2,1)S(1)}, bf16[2048,576]{0,1:T(8,128)(2,1)}, u32[]{:S(2)}) copy-start(bf16[2048,576]{0,1:T(8,128)(2,1)} %pad_maximum_fusion) | copy-start | bytes 7077892
  59.5 5.1 %copy-start.3 = (bf16[1,8,64,576]{3,2,1,0:T(8,128)(2,1)S(1)}, bf16[1,8,64,576]{3,2,1,0:T(8,128)(2,1)}, u32[]{:S(2)}) copy-start(bf16[1,8,64,576]{3,2,1,0:T(8,128)(2,1)} %param.9) | copy-start | bytes 1769476
  59.5 5.1 %copy-start.4 = (bf16[2,1,16,576]{3,2,1,0:T(8,128)(2,1)S(1)}, bf16[2,1,16,576]{3,2,1,0:T(8,128)(2,1)}, u32[]{:S(2)}) copy-start(bf16[2,1,16,576]{3,2,1,0:T(8,128)(2,1)} %param.7) | copy-start | bytes 110596
  59.5 5.1 %copy-start.5 = (bf16[2,1,576]{2,0,1:T(2,128)(2,1)S(1)}, bf16[2,1,576]{2,0,1:T(2,128)(2,1)}, u32[]{:S(2)}) copy-start(bf16[2,1,576]{2,0,1:T(2,128)(2,1)} %param.10) | copy-start | bytes 6916
  60.6 33.3 %all-to-all-start.2 = ((bf16[32,144,128]{2,1,0:T(8,128)(2,1)}), bf16[32,144,128]{2,1,0:T(8,128)(2,1)S(1)}, u32[]{:S(2)}, u32[]{:S(2)}) async-start(bf16[32,144,128]{2,1,0:T(8,128)(2,1)} %pad_maximum_fusion.2), calls=%async_computation.2 | async-start | bytes 2359296 | tf_op jit(solution)/shard_map/all_to_all | solution.py:103
